TPU v7x, 1024 devices: a whole 4x8x16 slice. The times are simulated.
1024 devices in a mesh: section: 32 (over x, y), ctx: 32 (over z, core).
Axes of the slice: x: 4, y: 8, z: 16, core: 2. Of those that a mesh axis runs over, the one named last changes fastest.
Arguments:
- queries: bfloat16 [32, 8192, 1024], P('section', 'ctx'), may hold values from -2.5 to 2.5
- attn_keys: bfloat16 [32, 8192, 128], P('section', 'ctx'), may hold values from -2.5 to 2.5
- attn_values: bfloat16 [32, 8192, 128], P('section', 'ctx'), may hold values from -4 to 4
- attn_outputs: bfloat16 [32, 8192, 1024], P('section', 'ctx'), may hold values from -4 to 4
- head_grad: bfloat16 [32, 8192, 1024], P('section', 'ctx'), may hold values from -4 to 4
- next_grad: bfloat16 [32, 8192, 1024], P('section', 'ctx'), may hold values from -4 to 4
- lse_saved: float32 [32, 8, 8192], P('section', None, 'ctx'), may hold values from 4 to 7
- block_keys: int32 [64, 7], P('ctx'), may hold values from -1 to 63, as said below
Outputs:
- query_grads: bfloat16 [32, 8192, 1024], P('section', 'ctx')
- key_grads: bfloat16 [32, 8192, 128], P('section', 'ctx')
- value_grads: bfloat16 [32, 8192, 128], P('section', 'ctx')
Inputs may be any that keep to these rules, and one draw needn't show every extreme that they name: `block_keys`: row i lists distinct blocks, none after block i: first its window i, i - 1, ..., i - w + 1 for some w of 1 to 4, then, falling, every block j before the window with j % 16 == 15; the remaining slots hold -1. The last row's window has 4 blocks.
All inputs are finite; a program needn't handle non-finite values.
Results may differ from a plain program's by a relative error of at most 0.018.
Values may be sent and summed in bfloat16 or wider, within the bound.
No kernel may reach another device: no remote copies, remote signals or barrier semaphores. Data moves between devices by JAX's collectives and lax.ppermute only.
A program may use at most 64 MiB of HBM per device.

v0:
```python
import jax
import jax.numpy as jnp
from jax import lax
from jax.sharding import PartitionSpec as P

SUMMARY = 4


def from_behind(block, axis, distance):
    devices = range(lax.axis_size(axis))
    route = [(i - distance, i) for i in devices if i - distance in devices]
    return lax.ppermute(block, axis, route)


def on_device(
    queries, attn_keys, attn_values, attn_outputs, head_grad, next_grad, lse_saved, block_keys
):
    tokens = queries.shape[1]
    features = queries.shape[2]
    head_size = attn_keys.shape[2]
    group_heads = features // head_size
    local_blocks = block_keys.shape[0]
    block_rows = tokens // local_blocks
    score_scale = head_size ** (-0.5)
    ctx_count = lax.axis_size("ctx")
    sequence = tokens * ctx_count
    blocks = sequence // block_rows
    stride = blocks // SUMMARY
    incoming = from_behind(next_grad, "section", -1)
    upstream = (head_grad[0].astype(jnp.float32) + incoming[0].astype(jnp.float32)).astype(
        jnp.bfloat16
    )
    products = upstream.astype(jnp.float32) * attn_outputs[0].astype(jnp.float32)
    deltas = jnp.sum(products.reshape(tokens, group_heads, head_size), axis=2).T
    lse_rows = lse_saved[0]
    device = lax.axis_index("ctx")
    first_block = device * local_blocks
    paired = jnp.concatenate([attn_keys[0], attn_values[0]], axis=1)
    key_source = lax.all_gather(paired, "ctx", axis=0, tiled=True)
    lowest_block = jnp.int32(0)
    positions = jnp.arange(block_rows, dtype=jnp.int32)
    causal = positions[None, :] <= positions[:, None]
    query_heads = queries[0].reshape(tokens, group_heads, head_size)
    upstream_heads = upstream.reshape(tokens, group_heads, head_size)

    def one_block(partial_value, local_index):
        row_start = local_index * block_rows
        block_index = first_block + local_index
        query_block = lax.dynamic_slice_in_dim(query_heads, row_start, block_rows, 0)
        upstream_block = lax.dynamic_slice_in_dim(upstream_heads, row_start, block_rows, 0)
        lse_block = lax.dynamic_slice_in_dim(lse_rows, row_start, block_rows, 1)
        delta_block = lax.dynamic_slice_in_dim(deltas, row_start, block_rows, 1)
        row_keys = lax.dynamic_index_in_dim(block_keys, local_index, 0, keepdims=False)

        def one_slot(slot_state, target):

            def compute(inner_state):
                grad_q, partial_value = inner_state
                key_start = target * block_rows
                tile_start = jnp.where(
                    target >= lowest_block,
                    target * block_rows,
                    sequence + target // stride * block_rows,
                )
                both_tiles = lax.dynamic_slice_in_dim(key_source, tile_start, block_rows, 0)
                key_tile = both_tiles[:, :head_size]
                value_tile = both_tiles[:, head_size:]
                scores = (
                    jnp.einsum(
                        "tgh,uh->gtu", query_block, key_tile, preferred_element_type=jnp.float32
                    )
                    * score_scale
                )
                allowed = (target < block_index) | causal
                weights = jnp.where(allowed[None], jnp.exp(scores - lse_block[:, :, None]), 0.0)
                dweights = jnp.einsum(
                    "tgh,uh->gtu", upstream_block, value_tile, preferred_element_type=jnp.float32
                )
                dscores = weights * (dweights - delta_block[:, :, None])
                weights_low = weights.astype(jnp.bfloat16)
                dscores_low = dscores.astype(jnp.bfloat16)
                grad_q = grad_q + jnp.einsum(
                    "gtu,uh->tgh", dscores_low, key_tile, preferred_element_type=jnp.float32
                )
                key_part = (
                    jnp.einsum(
                        "gtu,tgh->uh", dscores_low, query_block, preferred_element_type=jnp.float32
                    )
                    * score_scale
                )
                value_part = jnp.einsum(
                    "gtu,tgh->uh", weights_low, upstream_block, preferred_element_type=jnp.float32
                )
                previous = lax.dynamic_slice_in_dim(partial_value, key_start, block_rows, 0)
                update = previous + jnp.concatenate([key_part, value_part], axis=1)
                partial_value = lax.dynamic_update_slice_in_dim(partial_value, update, key_start, 0)
                return (grad_q, partial_value)

            def unchanged(inner_state):
                return inner_state

            return (lax.cond(target >= 0, compute, unchanged, slot_state), None)

        start_state = (jnp.zeros((block_rows, group_heads, head_size), jnp.float32), partial_value)
        (grad_q, partial_value), unused = lax.scan(one_slot, start_state, row_keys)
        block_grads = (grad_q * score_scale).reshape(block_rows, features).astype(jnp.bfloat16)
        return (partial_value, block_grads)

    partial_value, block_grads = lax.scan(
        one_block,
        jnp.zeros((sequence, 2 * head_size), jnp.float32),
        jnp.arange(local_blocks, dtype=jnp.int32),
    )
    query_grads = block_grads.reshape(tokens, features)
    totals = lax.psum_scatter(
        partial_value.astype(jnp.bfloat16), "ctx", scatter_dimension=0, tiled=True
    ).astype(jnp.float32)
    key_grads = totals[:, :head_size].astype(jnp.bfloat16)
    value_grads = totals[:, head_size:].astype(jnp.bfloat16)
    return (query_grads[None], key_grads[None], value_grads[None])


def solution(mesh):
    placed = (
        P("section", "ctx", None),
        P("section", "ctx", None),
        P("section", "ctx", None),
        P("section", "ctx", None),
        P("section", "ctx", None),
        P("section", "ctx", None),
        P("section", None, "ctx"),
        P("ctx", None),
    )
    return jax.shard_map(
        on_device,
        mesh=mesh,
        in_specs=placed,
        out_specs=(P("section", "ctx", None), P("section", "ctx", None), P("section", "ctx", None)),
        check_vma=False,
    )
```

profile of v0, /device:TPU:6, one launch (start us, length us, event | category | flops | bytes accessed | tf_op | source)
XLA Modules:
  0.0 387.5 jit_solution(14971608854868270037)
XLA Ops:
  7.2 1.5 pad_maximum_fusion
  8.8 5.6 %collective-permute-start = (bf16[1,256,1024]{2,1,0:T(8,128)(2,1)}, bf16[1,256,1024]{2,1,0:T(8,128)(2,1)S(1)}, u32[]{:S(2)}, u32[]{:S(2)}) collective-permute-start(bf16[1,256,1024]{2,1,0:T(8,128)(2,1)} %param.19), channel_id=1, source_target_pairs={{32,0},{64,32},{96,64},{128,96},{160,128},{192,160},{224,192},{256... | collective-permute-start | bytes 1572872 | tf_op jit(solution)/shard_map/ppermute | solution.py:12
  14.5 1.2 copy.19
  15.7 1.2 copy.17
  17.0 9.0 %collective-permute-done = bf16[1,256,1024]{2,1,0:T(8,128)(2,1)S(1)} collective-permute-done((bf16[1,256,1024]{2,1,0:T(8,128)(2,1)}, bf16[1,256,1024]{2,1,0:T(8,128)(2,1)S(1)}, u32[]{:S(2)}, u32[]{:S(2)}) %collective-permute-start) | collective-permute-done | bytes 524320 | tf_op jit(solution)/shard_map/ppermute | solution.py:12
  26.0 1.2 add_convert_fusion
  27.6 68.3 %all-gather.2.cloned.1.call-done = bf16[8192,256]{1,0:T(8,128)(2,1)} async-done(((bf16[256,256]{1,0:T(8,128)(2,1)}), bf16[8192,256]{1,0:T(8,128)(2,1)}) %all-gather.2.cloned.1.call-update) | async-done | bytes 4194320 | tf_op jit(solution)/shard_map/all_gather | solution.py:39
  95.9 4.2 %broadcast_in_dim.31 = f32[8192,256]{0,1:T(8,128)} broadcast(f32[]{:T(128)} %constant.62.clone.1), dimensions={} | broadcast | bytes 8388612 | tf_op jit(solution)/shard_map/broadcast_in_dim | solution.py:111
  100.1 46.3 %while.27 = (s32[]{:T(128)}, f32[8192,256]{0,1:T(8,128)}, bf16[2,128,1024]{2,1,0:T(8,128)(2,1)}, s32[2]{0:T(128)S(1)}, s32[2,7]{1,0:T(2,128)S(1)}, /*index=5*/bf...) while((s32[]{:T(128)}, f32[8192,256]{0,1:T(8,128)}, ...), condition=%wide.region_6.7_spmd.clone, body=%wide.region_1.6_spmd.clone.sunk | while | flops 169197616 | bytes 8578586 | solution.py:109
  104.0 18.3 %while.28 = (s32[]{:T(128)}, f32[128,8,128]{0,2,1:T(8,128)S(1)}, f32[8192,256]{0,1:T(8,128)}, s32[7]{0:T(128)S(1)}, bf16[8192,256]{1,0:T(8,128)(2,1)}, /*index=5...) while((s32[]{:T(128)}, f32[128,8,128]{0,2,1:T(8,128)S(1)}, ...), condition=%wide.region_5.5_spmd, body=%wide.region_2.4_spmd.sunk | while | flops 168919072 | bytes 5136973 | solution.py:105
  105.3 9.5 %conditional.2 = ((f32[128,8,128]{0,2,1:T(8,128)S(1)}, f32[8192,256]{0,1:T(8,128)})) conditional(s32[]{:T(128)} %convert_element_type.101, (f32[128,8,128]{0,2,1:T(8,128)S(1)}, f32[8192,256]{0,1:T(8,128)}) %tuple.58, (s32[]{:T(128)}, bf16[8192,256]{1,0:T(8,128)(2,1)}, s32[]{:T(128)}, pred[128,128]{0,1:T(8,128)(4,1)S(1)}, ...), branch_computations={%region_3.2_spmd, %region_4.3_spmd} | conditional | flops 168919072 | bytes 5136726 | solution.py:102
  109.6 1.0 fusion.7
  110.6 1.0 fusion.9
  112.1 1.6 fusion.12
  113.7 1.0 fusion.2
  127.2 18.3 %while.28 = (s32[]{:T(128)}, f32[128,8,128]{0,2,1:T(8,128)S(1)}, f32[8192,256]{0,1:T(8,128)}, s32[7]{0:T(128)S(1)}, bf16[8192,256]{1,0:T(8,128)(2,1)}, /*index=5...) while((s32[]{:T(128)}, f32[128,8,128]{0,2,1:T(8,128)S(1)}, ...), condition=%wide.region_5.5_spmd, body=%wide.region_2.4_spmd.sunk | while | flops 168919072 | bytes 5136973 | solution.py:105
  128.4 9.5 %conditional.2 = ((f32[128,8,128]{0,2,1:T(8,128)S(1)}, f32[8192,256]{0,1:T(8,128)})) conditional(s32[]{:T(128)} %convert_element_type.101, (f32[128,8,128]{0,2,1:T(8,128)S(1)}, f32[8192,256]{0,1:T(8,128)}) %tuple.58, (s32[]{:T(128)}, bf16[8192,256]{1,0:T(8,128)(2,1)}, s32[]{:T(128)}, pred[128,128]{0,1:T(8,128)(4,1)S(1)}, ...), branch_computations={%region_3.2_spmd, %region_4.3_spmd} | conditional | flops 168919072 | bytes 5136726 | solution.py:102
  132.8 1.0 fusion.7
  133.8 1.0 fusion.9
  135.3 1.6 fusion.12
  136.9 1.0 fusion.2
  146.4 7.2 %copy.21 = bf16[8192,256]{1,0:T(8,128)(2,1)} copy(f32[8192,256]{0,1:T(8,128)} %get-tuple-element.161) | data formatting | bytes 12582912 | tf_op jit(solution)/shard_map/while | solution.py:109
  153.6 225.5 %reduce-scatter.2.cloned.1.call-done = bf16[256,256]{1,0:T(8,128)(2,1)} async-done(((bf16[8192,256]{1,0:T(8,128)(2,1)}), bf16[256,256]{1,0:T(8,128)(2,1)}) %reduce-scatter.2.cloned.1.call-update) | async-done | bytes 131088 | tf_op jit(solution)/shard_map/reduce_scatter | solution.py:115
  379.1 1.5 slice_bitcast_fusion
  (62 shorter events, 13.3 us)
Async XLA Ops:
  7.2 93.0 %copy-start = (f32[1,8,256]{2,1,0:T(8,128)S(1)}, f32[1,8,256]{2,1,0:T(8,128)}, u32[]{:S(2)}) copy-start(f32[1,8,256]{2,1,0:T(8,128)} %param.20) | copy-start | bytes 24580
  7.2 93.0 %copy-start.1 = (s32[2,7]{1,0:T(2,128)S(1)}, s32[2,7]{1,0:T(2,128)}, u32[]{:S(2)}) copy-start(s32[2,7]{1,0:T(2,128)} %param.21) | copy-start | bytes 172
  7.2 88.7 %all-gather.2.cloned.1.call-start = ((), (), s32[]{:S(2)}) async-start(), calls=%async_computation.1 | async-start | bytes 4325376 | tf_op jit(solution)/shard_map/all_gather | solution.py:39
  8.8 370.4 %reduce-scatter.2.cloned.1.call-start = ((), (), s32[]{:S(2)}) async-start(), calls=%async_computation.2 | async-start | bytes 4325376 | tf_op jit(solution)/shard_map/reduce_scatter | solution.py:115
  8.8 17.1 %collective-permute-start = (bf16[1,256,1024]{2,1,0:T(8,128)(2,1)}, bf16[1,256,1024]{2,1,0:T(8,128)(2,1)S(1)}, u32[]{:S(2)}, u32[]{:S(2)}) collective-permute-start(bf16[1,256,1024]{2,1,0:T(8,128)(2,1)} %param.19), channel_id=1, source_target_pairs={{32,0},{64,32},{96,64},{128,96},{160,128},{192,160},{224,192},{256... | collective-permute-start | bytes 1572872 | tf_op jit(solution)/shard_map/ppermute | solution.py:12
Sparse Core Ops, SparseCore 0:
  10.7 85.1 all-gather.1
  153.8 225.3 reduce-scatter.1
where the time goes:
time: 392 us; the launch traced here: 388 us
  waiting for transfers between devices  303 us (77%)
  local copies, waits for them, and re-layouts  27.2 us (7%)
  loops' own time  24.4 us (6%)
  between operations  14.1 us (4%)
  matrix products  6.93 us (2%)
  other arithmetic  6.35 us (2%)
  starting transfers between devices  5.72 us (1%)
    reduce_scatter x1, waiting for transfers between devices, on_device(): lax.psum_scatter(partial_value.astype(jnp.bfloat16), 'ctx', scatter_dimen...  225 us
    all_gather x1, waiting for transfers between devices, on_device(): key_source = lax.all_gather(paired, 'ctx', axis=0, tiled=True)  68.3 us
    another operation x2, loops' own time, one_block(): (grad_q, partial_value), unused = lax.scan(one_slot, start_state, row_keys)  9.08 us
    another operation x14, loops' own time, one_slot(): return (lax.cond(target >= 0, compute, unchanged, slot_state), None)  8.97 us
    ppermute x1, waiting for transfers between devices, from_behind(): return lax.ppermute(block, axis, route)  8.96 us
    dynamic_slice x14, local copies, waits for them, and re-layouts, one_block(): (grad_q, partial_value), unused = lax.scan(one_slot, start_state, row_keys)  8.32 us
  transfers between devices with their start and end apart: 3, of which 3 were waited for; matrix products, arithmetic and copies ran while one was open for 1% of the time, Pallas kernels for 0%

commit v1 on v0

v1 whole, which is shorter than its diff:
```python
import jax
import jax.numpy as jnp
from jax import lax
from jax.sharding import PartitionSpec as P

SUMMARY = 4
WINDOW = 4


def from_behind(block, axis, distance):
    devices = range(lax.axis_size(axis))
    route = [(i - distance, i) for i in devices if i - distance in devices]
    return lax.ppermute(block, axis, route)


def on_device(
    queries, attn_keys, attn_values, attn_outputs, head_grad, next_grad, lse_saved, block_keys
):
    tokens = queries.shape[1]
    features = queries.shape[2]
    head_size = attn_keys.shape[2]
    group_heads = features // head_size
    local_blocks = block_keys.shape[0]
    block_rows = tokens // local_blocks
    score_scale = head_size ** (-0.5)
    ctx_count = lax.axis_size("ctx")
    blocks = local_blocks * ctx_count
    stride = blocks // SUMMARY
    reach = WINDOW - 1
    behind = -(-reach // local_blocks)
    counts = [min(local_blocks, reach - (k - 1) * local_blocks) for k in range(1, behind + 1)]
    span = reach + local_blocks
    n_summary = blocks // stride - 1
    device = lax.axis_index("ctx")
    first_block = device * local_blocks
    low_block = first_block - reach

    incoming = from_behind(next_grad, "section", -1)
    upstream = (head_grad[0].astype(jnp.float32) + incoming[0].astype(jnp.float32)).astype(
        jnp.bfloat16
    )
    products = upstream.astype(jnp.float32) * attn_outputs[0].astype(jnp.float32)
    deltas = jnp.sum(products.reshape(local_blocks, block_rows, group_heads, head_size), axis=3)
    deltas = jnp.swapaxes(deltas, 1, 2)
    lse_rows = jnp.swapaxes(lse_saved[0].reshape(group_heads, local_blocks, block_rows), 0, 1)

    paired = jnp.concatenate([attn_keys[0], attn_values[0]], axis=1)
    pieces = []
    for k in range(behind, 0, -1):
        piece = paired[(local_blocks - counts[k - 1]) * block_rows :]
        pieces.append(from_behind(piece, "ctx", k))
    pieces.append(paired)
    own_blocks = paired.reshape(local_blocks, block_rows, 2 * head_size)
    summary_parts = []
    for k in range(n_summary):
        summary_block = k * stride + stride - 1
        owner = summary_block // local_blocks
        summary_parts.append(
            jnp.where(device == owner, own_blocks[summary_block % local_blocks], 0).astype(
                jnp.bfloat16
            )
        )
    summary_kv = lax.psum(jnp.stack(summary_parts), "ctx")
    table = jnp.concatenate(pieces + [summary_kv.reshape(n_summary * block_rows, -1)], axis=0)
    key_table = table[:, :head_size]
    value_table = table[:, head_size:]
    slots = span + n_summary

    targets = block_keys
    slot_of = jnp.where(targets >= low_block, targets - low_block, span + targets // stride)
    slot_of = jnp.where(targets >= 0, slot_of, -1)
    chosen = jnp.any(slot_of[:, :, None] == jnp.arange(slots)[None, None, :], axis=1)
    table_ids = jnp.concatenate(
        [
            low_block + jnp.arange(span, dtype=jnp.int32),
            jnp.arange(n_summary, dtype=jnp.int32) * stride + stride - 1,
        ]
    )
    query_ids = first_block + jnp.arange(local_blocks, dtype=jnp.int32)
    positions = jnp.arange(block_rows, dtype=jnp.int32)
    causal = positions[None, :] <= positions[:, None]
    earlier = table_ids[None, :] < query_ids[:, None]
    allowed = chosen[:, None, :, None] & (earlier[:, None, :, None] | causal[None, :, None, :])
    allowed = allowed.reshape(local_blocks, block_rows, slots * block_rows)

    query_heads = queries[0].reshape(local_blocks, block_rows, group_heads, head_size)
    upstream_heads = upstream.reshape(local_blocks, block_rows, group_heads, head_size)
    scores = (
        jnp.einsum("rtgh,uh->rgtu", query_heads, key_table, preferred_element_type=jnp.float32)
        * score_scale
    )
    weights = jnp.where(allowed[:, None], jnp.exp(scores - lse_rows[:, :, :, None]), 0.0)
    dweights = jnp.einsum(
        "rtgh,uh->rgtu", upstream_heads, value_table, preferred_element_type=jnp.float32
    )
    dscores = weights * (dweights - deltas[:, :, :, None])
    weights_low = weights.astype(jnp.bfloat16)
    dscores_low = dscores.astype(jnp.bfloat16)
    grad_q = jnp.einsum("rgtu,uh->rtgh", dscores_low, key_table, preferred_element_type=jnp.float32)
    query_grads = (grad_q * score_scale).reshape(tokens, features).astype(jnp.bfloat16)
    key_part = (
        jnp.einsum("rgtu,rtgh->uh", dscores_low, query_heads, preferred_element_type=jnp.float32)
        * score_scale
    )
    value_part = jnp.einsum(
        "rgtu,rtgh->uh", weights_low, upstream_heads, preferred_element_type=jnp.float32
    )
    partial = jnp.concatenate([key_part, value_part], axis=1).astype(jnp.bfloat16)

    totals = partial[(span - local_blocks) * block_rows : span * block_rows].astype(jnp.float32)
    offset = 0
    for k in range(behind, 0, -1):
        size = counts[k - 1] * block_rows
        returned = from_behind(partial[offset : offset + size], "ctx", -k).astype(jnp.float32)
        totals = totals.at[tokens - size :].add(returned)
        offset += size
    summary_grads = lax.psum(
        partial[span * block_rows :].astype(jnp.float32).reshape(n_summary, block_rows, -1), "ctx"
    )
    for k in range(n_summary):
        summary_block = k * stride + stride - 1
        owner = summary_block // local_blocks
        start = (summary_block % local_blocks) * block_rows
        mine = jnp.where(device == owner, summary_grads[k], 0.0)
        totals = totals.at[start : start + block_rows].add(mine)
    key_grads = totals[:, :head_size].astype(jnp.bfloat16)
    value_grads = totals[:, head_size:].astype(jnp.bfloat16)
    return (query_grads[None], key_grads[None], value_grads[None])


def solution(mesh):
    placed = (
        P("section", "ctx", None),
        P("section", "ctx", None),
        P("section", "ctx", None),
        P("section", "ctx", None),
        P("section", "ctx", None),
        P("section", "ctx", None),
        P("section", None, "ctx"),
        P("ctx", None),
    )
    return jax.shard_map(
        on_device,
        mesh=mesh,
        in_specs=placed,
        out_specs=(P("section", "ctx", None), P("section", "ctx", None), P("section", "ctx", None)),
        check_vma=False,
    )
```

time: 392 us -> 473 us (1.21)
  the two profiles are of different devices: /device:TPU:6 before, /device:TPU:2 now
where the time goes in v1:
time: 473 us; the launch traced here: 472 us
  waiting for transfers between devices  413 us (87%)
  matrix products  15.1 us (3%)
  starting transfers between devices  14.4 us (3%)
  between operations  14.4 us (3%)
  other arithmetic  9.95 us (2%)
  local copies, waits for them, and re-layouts  5.6 us (1%)
    psum x1, waiting for transfers between devices, on_device(): lax.psum(partial[span * block_rows:].astype(jnp.float32).reshape(n_summar...  206 us
    psum x1, waiting for transfers between devices, on_device(): summary_kv = lax.psum(jnp.stack(summary_parts), 'ctx')  204 us
    ppermute x5, starting transfers between devices, from_behind(): return lax.ppermute(block, axis, route)  14.3 us
  transfers between devices with their start and end apart: 7, of which 3 were waited for; matrix products, arithmetic and copies ran while one was open for 3% of the time, Pallas kernels for 0%

profile of v1, /device:TPU:2, one launch (start us, length us, event | category | flops | bytes accessed | tf_op | source)
XLA Modules:
  0.0 472.0 jit_solution(12829094983073470555)
XLA Ops:
  7.2 0.8 select_bitcast_fusion.2
  8.0 4.3 collective-permute-start
  13.1 0.9 pad_maximum_fusion.3
  14.0 2.1 collective-permute-start.1
  16.1 5.3 %collective-permute-start.2 = (bf16[1,256,1024]{2,1,0:T(8,128)(2,1)}, bf16[1,256,1024]{2,1,0:T(8,128)(2,1)S(1)}, u32[]{:S(2)}, u32[]{:S(2)}) collective-permute-start(bf16[1,256,1024]{2,1,0:T(8,128)(2,1)} %param.25), channel_id=1, source_target_pairs={{32,0},{64,32},{96,64},{128,96},{160,128},{192,160},{224,192},{256... | collective-permute-start | bytes 1572872 | tf_op jit(solution)/shard_map/ppermute | solution.py:13
  22.6 1.1 convert_bitcast_fusion
  23.8 0.8 or_and_fusion
  24.6 1.1 copy.76
  26.0 204.1 %all-reduce.3.cloned.1.call-done = bf16[384,256]{1,0:T(8,128)(2,1)} async-done(((bf16[384,256]{1,0:T(8,128)(2,1)}), bf16[384,256]{1,0:T(8,128)(2,1)}) %all-reduce.3.cloned.1.call-update) | async-done | bytes 196624 | tf_op jit(solution)/shard_map/psum | solution.py:63
  230.1 1.1 pad_maximum_fusion
  231.2 6.4 %fusion.4 = (bf16[2,8,128,1024]{2,3,1,0:T(8,128)(2,1)}, f32[1024,2,128,8]{2,0,3,1:T(8,128)}) fusion(f32[2,8,128]{2,1,0:T(8,128)} %bitcast.131, pred[2,128,1024]{1,2,0:T(8,128)(4,1)S(1)} %or_and_fusion, bf16[2,128,8,128]{3,2,1,0:T(8,128)(2,1)S(1)} %bitcast.115, bf16[1024,256]{1,0:T(8,128)(2,1)S(1)} %pad_maximum_fusion), kind=kOutput, calls=%fused_computation.6 | convolution fusion | flops 545259520 | bytes 13639680 | tf_op jit(solution)/shard_map/rtgh,uh->rgtu/dot_general | solution.py:89
  238.4 4.9 %fusion.1 = bf16[2,8,128,1024]{2,3,1,0:T(8,128)(2,1)S(1)} fusion(f32[1024,2,128,8]{2,0,3,1:T(8,128)} %get-tuple-element.92, f32[2,8,128]{2,1,0:T(8,128)S(1)} %copy.51, f32[2,8,128]{2,1,0:T(8,128)S(1)} %bitcast.132, pred[2,128,1024]{1,2,0:T(8,128)(4,1)S(1)} %or_and_fusion, bf16[2,128,8,128]{3,2,1,0:T(8,128)(2,1)S(1)} %bitcast.118, ...), kind=kOutput, calls=%fused_computation.2 | convolution fusion | flops 549453824 | bytes 13647872 | tf_op jit(solution)/shard_map/rtgh,uh->rgtu/dot_general | solution.py:93
  243.3 1.5 fusion.20
  244.8 0.8 fusion.10
  245.6 1.5 fusion.23
  247.5 1.0 convert_element_type.100
  248.5 1.3 collective-permute-start.3
  250.0 0.9 copy.60
  250.9 1.3 collective-permute-start.4
  252.2 2.4 collective-permute-done.3
  254.7 206.0 %all-reduce.5.cloned.1.call-done = f32[3,128,256]{1,2,0:T(8,128)} async-done(((f32[3,128,256]{1,2,0:T(8,128)}), f32[3,128,256]{1,2,0:T(8,128)}) %all-reduce.5.cloned.1.call-update) | async-done | bytes 393232 | tf_op jit(solution)/shard_map/psum | solution.py:117
  460.8 0.9 fusion.43
  461.7 0.9 fusion.47
  462.6 1.0 fusion.39
  (45 shorter events, 5.0 us)
Async XLA Ops:
  7.2 222.9 %all-reduce.3.cloned.1.call-start = ((), (), s32[]{:S(2)}) async-start(), calls=%async_computation | async-start | bytes 393216 | tf_op jit(solution)/shard_map/psum | solution.py:63
  8.0 18.0 %collective-permute-start = (bf16[128,256]{1,0:T(8,128)(2,1)S(1)}, bf16[128,256]{1,0:T(8,128)(2,1)S(1)}, u32[]{:S(2)}, u32[]{:S(2)}) collective-permute-start(bf16[128,256]{1,0:T(8,128)(2,1)S(1)} %get-tuple-element.84), channel_id=1, source_target_pairs={{0,2},{1,3},{2,4},{3,5},{4,6},{5,7},{6,8},{7,9},{8,10},{9,11},{10,... | collective-permute-start | bytes 196616 | tf_op jit(solution)/shard_map/ppermute | solution.py:13
  13.1 447.7 %all-reduce.5.cloned.1.call-start = ((), (), s32[]{:S(2)}) async-start(), calls=%async_computation.1 | async-start | bytes 786432 | tf_op jit(solution)/shard_map/psum | solution.py:117
  14.0 216.1 %collective-permute-start.1 = (bf16[256,256]{1,0:T(8,128)(2,1)S(1)}, bf16[256,256]{1,0:T(8,128)(2,1)}, u32[]{:S(2)}, u32[]{:S(2)}) collective-permute-start(bf16[256,256]{1,0:T(8,128)(2,1)S(1)} %pad_maximum_fusion.3), channel_id=1, source_target_pairs={{0,1},{1,2},{2,3},{3,4},{4,5},{5,6},{6,7},{7,8},{8,9},{9,10},{10,1... | collective-permute-start | bytes 393224 | tf_op jit(solution)/shard_map/ppermute | solution.py:13
  16.1 221.5 %collective-permute-start.2 = (bf16[1,256,1024]{2,1,0:T(8,128)(2,1)}, bf16[1,256,1024]{2,1,0:T(8,128)(2,1)S(1)}, u32[]{:S(2)}, u32[]{:S(2)}) collective-permute-start(bf16[1,256,1024]{2,1,0:T(8,128)(2,1)} %param.25), channel_id=1, source_target_pairs={{32,0},{64,32},{96,64},{128,96},{160,128},{192,160},{224,192},{256... | collective-permute-start | bytes 1572872 | tf_op jit(solution)/shard_map/ppermute | solution.py:13
  25.8 211.9 %copy-start.1 = (bf16[1,256,1024]{2,1,0:T(8,128)(2,1)S(1)}, bf16[1,256,1024]{2,1,0:T(8,128)(2,1)}, u32[]{:S(2)}) copy-start(bf16[1,256,1024]{2,1,0:T(8,128)(2,1)} %param.24) | copy-start | bytes 1572868
  231.2 7.1 %copy-start.2 = (f32[1,8,256]{2,1,0:T(8,128)S(1)}, f32[1,8,256]{2,1,0:T(8,128)}, u32[]{:S(2)}) copy-start(f32[1,8,256]{2,1,0:T(8,128)} %param.26) | copy-start | bytes 24580
  243.3 2.3 copy-start
  248.5 6.1 %collective-permute-start.3 = (bf16[128,256]{0,1:T(8,128)(2,1)S(1)}, bf16[128,256]{0,1:T(8,128)(2,1)S(1)}, u32[]{:S(2)}, u32[]{:S(2)}) collective-permute-start(bf16[128,256]{0,1:T(8,128)(2,1)S(1)} %fusion.45), channel_id=1, source_target_pairs={{2,0},{3,1},{4,2},{5,3},{6,4},{7,5},{8,6},{9,7},{10,8},{11,9},{12,... | collective-permute-start | bytes 196616 | tf_op jit(solution)/shard_map/ppermute | solution.py:13
  250.9 3.7 collective-permute-start.4
Sparse Core Ops, SparseCore 0:
  13.2 216.8 all-reduce.2
  251.0 209.6 all-reduce.4

commit v2 on v1

--- a/solution.py
+++ b/solution.py
@@ -51,16 +51,31 @@
         pieces.append(from_behind(piece, "ctx", k))
     pieces.append(paired)
     own_blocks = paired.reshape(local_blocks, block_rows, 2 * head_size)
-    summary_parts = []
-    for k in range(n_summary):
-        summary_block = k * stride + stride - 1
-        owner = summary_block // local_blocks
-        summary_parts.append(
-            jnp.where(device == owner, own_blocks[summary_block % local_blocks], 0).astype(
-                jnp.bfloat16
-            )
-        )
-    summary_kv = lax.psum(jnp.stack(summary_parts), "ctx")
+    owners = [(k * stride + stride - 1) // local_blocks for k in range(n_summary)]
+    owned = own_blocks[(stride - 1) % local_blocks]
+    radix = 1
+    while radix * radix < ctx_count:
+        radix += 1
+    relay_of = [-1] * ctx_count
+    for k, owner in enumerate(owners):
+        for x in range(owner, min(owner + radix, ctx_count)):
+            relay_of[x] = k
+    relay_table = jnp.array(relay_of, dtype=jnp.int32)
+    is_owner = jnp.array([x in owners for x in range(ctx_count)])[device]
+    held = jnp.where(is_owner, owned, 0).astype(jnp.bfloat16)
+    for shift in range(1, radix):
+        route = [(o, o + shift) for o in owners if o + shift < ctx_count]
+        held = held + lax.ppermute(owned, "ctx", route)
+    summary_parts = [jnp.where(relay_table[device] == k, held, 0) for k in range(n_summary)]
+    for hop in range(1, radix):
+        shift = hop * radix
+        route = [(x, x + shift) for x in range(ctx_count - shift) if relay_of[x] >= 0]
+        arrived = lax.ppermute(held, "ctx", route)
+        for k in range(n_summary):
+            came = [x + shift < ctx_count and relay_of[x] == k for x in range(ctx_count)]
+            came = jnp.array([False] * shift + came[: ctx_count - shift])
+            summary_parts[k] = summary_parts[k] + jnp.where(came[device], arrived, 0)
+    summary_kv = jnp.stack(summary_parts).astype(jnp.bfloat16)
     table = jnp.concatenate(pieces + [summary_kv.reshape(n_summary * block_rows, -1)], axis=0)
     key_table = table[:, :head_size]
     value_table = table[:, head_size:]
@@ -114,15 +129,25 @@
         returned = from_behind(partial[offset : offset + size], "ctx", -k).astype(jnp.float32)
         totals = totals.at[tokens - size :].add(returned)
         offset += size
-    summary_grads = lax.psum(
-        partial[span * block_rows :].astype(jnp.float32).reshape(n_summary, block_rows, -1), "ctx"
+    summary_low = partial[span * block_rows :].reshape(n_summary, block_rows, -1)
+    tree_slot = jnp.maximum(relay_table[device], 0)
+    gathered = lax.dynamic_index_in_dim(summary_low, tree_slot, 0, keepdims=False).astype(
+        jnp.float32
     )
-    for k in range(n_summary):
-        summary_block = k * stride + stride - 1
-        owner = summary_block // local_blocks
-        start = (summary_block % local_blocks) * block_rows
-        mine = jnp.where(device == owner, summary_grads[k], 0.0)
-        totals = totals.at[start : start + block_rows].add(mine)
+    for hop in range(1, radix):
+        shift = hop * radix
+        route = [(x + shift, x) for x in range(ctx_count - shift) if relay_of[x] >= 0]
+        sent_slot = [max(relay_of[y - shift], 0) if y >= shift else 0 for y in range(ctx_count)]
+        slot_here = jnp.array(sent_slot, dtype=jnp.int32)[device]
+        outgoing = lax.dynamic_index_in_dim(summary_low, slot_here, 0, keepdims=False)
+        gathered = gathered + lax.ppermute(outgoing, "ctx", route).astype(jnp.float32)
+    owner_total = gathered
+    for shift in range(1, radix):
+        route = [(o + shift, o) for o in owners if o + shift < ctx_count]
+        owner_total = owner_total + lax.ppermute(gathered, "ctx", route)
+    start = ((stride - 1) % local_blocks) * block_rows
+    mine = jnp.where(is_owner, owner_total, 0.0)
+    totals = totals.at[start : start + block_rows].add(mine)
     key_grads = totals[:, :head_size].astype(jnp.bfloat16)
     value_grads = totals[:, head_size:].astype(jnp.bfloat16)
     return (query_grads[None], key_grads[None], value_grads[None])

time: 473 us -> 125 us (0.26)
  the two profiles are of different devices: /device:TPU:2 before, /device:TPU:199 now
where the time goes in v2:
time: 125 us; the launch traced here: 123 us
  starting transfers between devices  54.9 us (44%)
  local copies, waits for them, and re-layouts  17.8 us (14%)
  waiting for transfers between devices  15.6 us (12%)
  matrix products  14.6 us (12%)
  other arithmetic  13 us (10%)
  between operations  7.47 us (6%)
    ppermute x5, starting transfers between devices, on_device(): held = held + lax.ppermute(owned, 'ctx', route)  17 us
    ppermute x5, starting transfers between devices, from_behind(): return lax.ppermute(block, axis, route)  14.4 us
    ppermute x4, starting transfers between devices, on_device(): arrived = lax.ppermute(held, 'ctx', route)  11.1 us
    dynamic_slice x7, local copies, waits for them, and re-layouts, on_device(): summary_parts[k] = summary_parts[k] + jnp.where(came[device], arrived, 0)  8.85 us
    ppermute x5, waiting for transfers between devices, on_device(): owner_total = owner_total + lax.ppermute(gathered, 'ctx', route)  7.63 us
    ppermute x5, waiting for transfers between devices, on_device(): lax.ppermute(outgoing, 'ctx', route).astype(jnp.float32)  6.74 us
    ppermute x5, starting transfers between devices, on_device(): owner_total = owner_total + lax.ppermute(gathered, 'ctx', route)  6.45 us
    dot_general x1, matrix products, on_device(): jnp.einsum('rtgh,uh->rgtu', query_heads, key_table, preferred_element_typ...  6.4 us
  transfers between devices with their start and end apart: 24, of which 8 were waited for; matrix products, arithmetic and copies ran while one was open for 28% of the time, Pallas kernels for 0%

profile of v2, /device:TPU:199, one launch (start us, length us, event | category | flops | bytes accessed | tf_op | source)
XLA Modules:
  0.0 123.2 jit_solution(12649378245768206284)
XLA Ops:
  1.4 9.4 %collective-permute-start.6 = (bf16[128,256]{1,0:T(8,128)(2,1)S(1)}, bf16[128,256]{1,0:T(8,128)(2,1)S(1)}, u32[]{:S(2)}, u32[]{:S(2)}) collective-permute-start(bf16[128,256]{1,0:T(8,128)(2,1)S(1)} %fusion.44), channel_id=1, source_target_pairs={{7,12},{15,20},{23,28},{39,44},{47,52},{55,60},{71,76},{79,84},{87... | collective-permute-start | bytes 196616 | tf_op jit(solution)/shard_map/ppermute | solution.py:68
  10.8 1.9 %collective-permute-start.5 = (bf16[128,256]{1,0:T(8,128)(2,1)S(1)}, bf16[128,256]{1,0:T(8,128)(2,1)}, u32[]{:S(2)}, u32[]{:S(2)}) collective-permute-start(bf16[128,256]{1,0:T(8,128)(2,1)S(1)} %fusion.44), channel_id=1, source_target_pairs={{7,11},{15,19},{23,27},{39,43},{47,51},{55,59},{71,75},{79,83},{87... | collective-permute-start | bytes 196616 | tf_op jit(solution)/shard_map/ppermute | solution.py:68
  12.7 1.9 %collective-permute-start.4 = (bf16[128,256]{1,0:T(8,128)(2,1)S(1)}, bf16[128,256]{1,0:T(8,128)(2,1)}, u32[]{:S(2)}, u32[]{:S(2)}) collective-permute-start(bf16[128,256]{1,0:T(8,128)(2,1)S(1)} %fusion.44), channel_id=1, source_target_pairs={{7,10},{15,18},{23,26},{39,42},{47,50},{55,58},{71,74},{79,82},{87... | collective-permute-start | bytes 196616 | tf_op jit(solution)/shard_map/ppermute | solution.py:68
  14.6 1.9 %collective-permute-start.3 = (bf16[128,256]{1,0:T(8,128)(2,1)S(1)}, bf16[128,256]{1,0:T(8,128)(2,1)}, u32[]{:S(2)}, u32[]{:S(2)}) collective-permute-start(bf16[128,256]{1,0:T(8,128)(2,1)S(1)} %fusion.44), channel_id=1, source_target_pairs={{7,9},{15,17},{23,25},{39,41},{47,49},{55,57},{71,73},{79,81},{87,... | collective-permute-start | bytes 196616 | tf_op jit(solution)/shard_map/ppermute | solution.py:68
  16.6 1.9 %collective-permute-start.2 = (bf16[128,256]{1,0:T(8,128)(2,1)S(1)}, bf16[128,256]{1,0:T(8,128)(2,1)}, u32[]{:S(2)}, u32[]{:S(2)}) collective-permute-start(bf16[128,256]{1,0:T(8,128)(2,1)S(1)} %fusion.44), channel_id=1, source_target_pairs={{7,8},{15,16},{23,24},{39,40},{47,48},{55,56},{71,72},{79,80},{87,... | collective-permute-start | bytes 196616 | tf_op jit(solution)/shard_map/ppermute | solution.py:68
  26.5 1.3 %dynamic_slice.88 = s32[1]{0:T(128)} dynamic-slice(s32[32]{0:T(128)} %constant.182.clone, s32[]{:T(128)S(6)} %select_n.182), dynamic_slice_sizes={1} | dynamic-slice | bytes 12 | tf_op jit(solution)/shard_map/dynamic_slice | solution.py:69
  31.7 1.3 %dynamic_slice.96 = pred[1]{0:T(512)(128)(4,1)} dynamic-slice(pred[32]{0:T(512)(128)(4,1)} %constant.188.clone, s32[]{:T(128)S(6)} %select_n.182), dynamic_slice_sizes={1} | dynamic-slice | bytes 6 | tf_op jit(solution)/shard_map/dynamic_slice | solution.py:77
  43.3 1.9 %collective-permute-start = (bf16[128,256]{1,0:T(8,128)(2,1)S(1)}, bf16[128,256]{1,0:T(8,128)(2,1)S(1)}, u32[]{:S(2)}, u32[]{:S(2)}) collective-permute-start(bf16[128,256]{1,0:T(8,128)(2,1)S(1)} %fusion.44), channel_id=1, source_target_pairs={{0,2},{1,3},{2,4},{3,5},{4,6},{5,7},{6,8},{7,9},{8,10},{9,11},{10,... | collective-permute-start | bytes 196616 | tf_op jit(solution)/shard_map/ppermute | solution.py:13
  45.2 1.6 %add_add_fusion = bf16[128,256]{1,0:T(8,128)(2,1)S(1)} fusion(bf16[128,256]{1,0:T(8,128)(2,1)S(1)} %collective-permute-done.6, bf16[128,256]{1,0:T(8,128)(2,1)} %collective-permute-done.5, bf16[128,256]{1,0:T(8,128)(2,1)} %collective-permute-done.4, bf16[128,256]{1,0:T(8,128)(2,1)} %collective-permute-done.3, bf16[128,256]{1,0:T(8,128)(2,1)} %collective-permute-done.2, ...), kind=kLoop, calls=%fused_computation.70 | loop fusion | flops 196608 | bytes 458753 | tf_op jit(solution)/shard_map/add | solution.py:68
  46.8 3.3 %collective-permute-start.10 = (bf16[128,256]{1,0:T(8,128)(2,1)S(1)}, bf16[128,256]{1,0:T(8,128)(2,1)S(1)}, u32[]{:S(2)}, u32[]{:S(2)}) collective-permute-start(bf16[128,256]{1,0:T(8,128)(2,1)S(1)} %add_add_fusion), channel_id=1, source_target_pairs={{7,31},{39,63},{71,95},{103,127},{135,159},{167,191},{199,223},{23... | collective-permute-start | bytes 196616 | tf_op jit(solution)/shard_map/ppermute | solution.py:73
  50.2 2.5 %collective-permute-start.9 = (bf16[128,256]{1,0:T(8,128)(2,1)S(1)}, bf16[128,256]{1,0:T(8,128)(2,1)S(1)}, u32[]{:S(2)}, u32[]{:S(2)}) collective-permute-start(bf16[128,256]{1,0:T(8,128)(2,1)S(1)} %add_add_fusion), channel_id=1, source_target_pairs={{7,25},{8,26},{9,27},{10,28},{11,29},{12,30},{39,57},{40,58},{41,5... | collective-permute-start | bytes 196616 | tf_op jit(solution)/shard_map/ppermute | solution.py:73
  54.0 4.0 %collective-permute-start.7 = (bf16[128,256]{1,0:T(8,128)(2,1)S(1)}, bf16[128,256]{1,0:T(8,128)(2,1)S(1)}, u32[]{:S(2)}, u32[]{:S(2)}) collective-permute-start(bf16[128,256]{1,0:T(8,128)(2,1)S(1)} %add_add_fusion), channel_id=1, source_target_pairs={{7,13},{8,14},{9,15},{10,16},{11,17},{12,18},{15,21},{16,22},{17,2... | collective-permute-start | bytes 196616 | tf_op jit(solution)/shard_map/ppermute | solution.py:73
  58.9 3.3 %collective-permute-start.1 = (bf16[256,256]{1,0:T(8,128)(2,1)S(1)}, bf16[256,256]{1,0:T(8,128)(2,1)S(1)}, u32[]{:S(2)}, u32[]{:S(2)}) collective-permute-start(bf16[256,256]{1,0:T(8,128)(2,1)S(1)} %pad_maximum_fusion.2), channel_id=1, source_target_pairs={{0,1},{1,2},{2,3},{3,4},{4,5},{5,6},{6,7},{7,8},{8,9},{9,10},{10,1... | collective-permute-start | bytes 393224 | tf_op jit(solution)/shard_map/ppermute | solution.py:13
  62.2 5.4 %collective-permute-start.11 = (bf16[1,256,1024]{2,1,0:T(8,128)(2,1)}, bf16[1,256,1024]{2,1,0:T(8,128)(2,1)S(1)}, u32[]{:S(2)}, u32[]{:S(2)}) collective-permute-start(bf16[1,256,1024]{2,1,0:T(8,128)(2,1)} %param.43), channel_id=1, source_target_pairs={{32,0},{64,32},{96,64},{128,96},{160,128},{192,160},{224,192},{256... | collective-permute-start | bytes 1572872 | tf_op jit(solution)/shard_map/ppermute | solution.py:13
  67.6 4.4 %add_bitcast_fusion.2 = (bf16[1,128,256]{2,1,0:T(8,128)(2,1)S(1)}, bf16[1,128,256]{2,1,0:T(8,128)(2,1)S(1)}, bf16[1,128,256]{2,1,0:T(8,128)(2,1)S(1)}) fusion(bf16[128,256]{1,0:T(8,128)(2,1)S(1)} %collective-permute-done.10, bf16[128,256]{1,0:T(8,128)(2,1)S(1)} %collective-permute-done.9, bf16[128,256]{1,0:T(8,128)(2,1)S(1)} %collective-permute-done.8, ...), kind=kLoop, calls=%fused_computation.69 | loop fusion | flops 557056 | bytes 524298 | tf_op jit(solution)/shard_map/stack | solution.py:78
  73.0 6.4 %fusion.4 = (bf16[2,8,128,1024]{2,3,1,0:T(8,128)(2,1)}, f32[1024,2,128,8]{2,0,3,1:T(8,128)}) fusion(f32[2,8,128]{2,1,0:T(8,128)} %bitcast.131, pred[2,128,1024]{1,2,0:T(8,128)(4,1)S(1)} %or_and_fusion, bf16[2,128,8,128]{3,2,1,0:T(8,128)(2,1)S(1)} %bitcast.114, bf16[1024,256]{1,0:T(8,128)(2,1)S(1)} %pad_maximum_fusion), kind=kOutput, calls=%fused_computation.6 | convolution fusion | flops 545259520 | bytes 13639680 | tf_op jit(solution)/shard_map/rtgh,uh->rgtu/dot_general | solution.py:104
  80.2 4.9 %fusion.1 = bf16[2,8,128,1024]{2,3,1,0:T(8,128)(2,1)S(1)} fusion(f32[1024,2,128,8]{2,0,3,1:T(8,128)} %get-tuple-element.59, f32[2,8,128]{2,1,0:T(8,128)S(1)} %copy.68, f32[2,8,128]{2,1,0:T(8,128)S(1)} %bitcast.132, pred[2,128,1024]{1,2,0:T(8,128)(4,1)S(1)} %or_and_fusion, bf16[2,128,8,128]{3,2,1,0:T(8,128)(2,1)S(1)} %bitcast.117, ...), kind=kOutput, calls=%fused_computation.2 | convolution fusion | flops 549453824 | bytes 13647872 | tf_op jit(solution)/shard_map/rtgh,uh->rgtu/dot_general | solution.py:108
  95.8 4.4 %collective-permute-done.16 = bf16[128,256]{1,0:T(8,128)(2,1)S(1)} collective-permute-done((bf16[128,256]{1,0:T(8,128)(2,1)S(1)}, bf16[128,256]{1,0:T(8,128)(2,1)S(1)}, u32[]{:S(2)}, u32[]{:S(2)}) %collective-permute-start.16) | collective-permute-done | bytes 65568 | tf_op jit(solution)/shard_map/ppermute | solution.py:143
  100.2 1.9 %collective-permute-start.12 = (bf16[128,256]{1,0:T(8,128)(2,1)S(1)}, bf16[128,256]{1,0:T(8,128)(2,1)S(1)}, u32[]{:S(2)}, u32[]{:S(2)}) collective-permute-start(bf16[128,256]{1,0:T(8,128)(2,1)S(1)} %get-tuple-element.48), channel_id=1, source_target_pairs={{2,0},{3,1},{4,2},{5,3},{6,4},{7,5},{8,6},{9,7},{10,8},{11,9},{12,... | collective-permute-start | bytes 196616 | tf_op jit(solution)/shard_map/ppermute | solution.py:13
  102.2 1.9 %collective-permute-start.13 = (bf16[256,256]{1,0:T(8,128)(2,1)S(1)}, bf16[256,256]{1,0:T(8,128)(2,1)S(1)}, u32[]{:S(2)}, u32[]{:S(2)}) collective-permute-start(bf16[256,256]{1,0:T(8,128)(2,1)S(1)} %get-tuple-element.49), channel_id=1, source_target_pairs={{1,0},{2,1},{3,2},{4,3},{5,4},{6,5},{7,6},{8,7},{9,8},{10,9},{11,1... | collective-permute-start | bytes 393224 | tf_op jit(solution)/shard_map/ppermute | solution.py:13
  104.1 2.3 %collective-permute-done.15 = bf16[128,256]{1,0:T(8,128)(2,1)S(1)} collective-permute-done((bf16[128,256]{1,0:T(8,128)(2,1)S(1)}, bf16[128,256]{1,0:T(8,128)(2,1)S(1)}, u32[]{:S(2)}, u32[]{:S(2)}) %collective-permute-start.15) | collective-permute-done | bytes 65568 | tf_op jit(solution)/shard_map/ppermute | solution.py:143
  114.2 2.7 %collective-permute-done.23 = f32[128,256]{1,0:T(8,128)S(1)} collective-permute-done((f32[128,256]{1,0:T(8,128)S(1)}, f32[128,256]{1,0:T(8,128)S(1)}, u32[]{:S(2)}, u32[]{:S(2)}) %collective-permute-start.23) | collective-permute-done | bytes 131104 | tf_op jit(solution)/shard_map/ppermute | solution.py:147
  116.9 1.6 %collective-permute-done.22 = f32[128,256]{1,0:T(8,128)S(1)} collective-permute-done((f32[128,256]{1,0:T(8,128)S(1)}, f32[128,256]{1,0:T(8,128)S(1)}, u32[]{:S(2)}, u32[]{:S(2)}) %collective-permute-start.22) | collective-permute-done | bytes 131104 | tf_op jit(solution)/shard_map/ppermute | solution.py:147
  119.1 2.6 %collective-permute-done.20 = f32[128,256]{1,0:T(8,128)S(1)} collective-permute-done((f32[128,256]{1,0:T(8,128)S(1)}, f32[128,256]{1,0:T(8,128)S(1)}, u32[]{:S(2)}, u32[]{:S(2)}) %collective-permute-start.20) | collective-permute-done | bytes 131104 | tf_op jit(solution)/shard_map/ppermute | solution.py:147
  (84 shorter events, 40.9 us)
Async XLA Ops:
  1.4 41.8 %collective-permute-start.6 = (bf16[128,256]{1,0:T(8,128)(2,1)S(1)}, bf16[128,256]{1,0:T(8,128)(2,1)S(1)}, u32[]{:S(2)}, u32[]{:S(2)}) collective-permute-start(bf16[128,256]{1,0:T(8,128)(2,1)S(1)} %fusion.44), channel_id=1, source_target_pairs={{7,12},{15,20},{23,28},{39,44},{47,52},{55,60},{71,76},{79,84},{87... | collective-permute-start | bytes 196616 | tf_op jit(solution)/shard_map/ppermute | solution.py:68
  10.8 34.4 %collective-permute-start.5 = (bf16[128,256]{1,0:T(8,128)(2,1)S(1)}, bf16[128,256]{1,0:T(8,128)(2,1)}, u32[]{:S(2)}, u32[]{:S(2)}) collective-permute-start(bf16[128,256]{1,0:T(8,128)(2,1)S(1)} %fusion.44), channel_id=1, source_target_pairs={{7,11},{15,19},{23,27},{39,43},{47,51},{55,59},{71,75},{79,83},{87... | collective-permute-start | bytes 196616 | tf_op jit(solution)/shard_map/ppermute | solution.py:68
  12.7 32.5 %collective-permute-start.4 = (bf16[128,256]{1,0:T(8,128)(2,1)S(1)}, bf16[128,256]{1,0:T(8,128)(2,1)}, u32[]{:S(2)}, u32[]{:S(2)}) collective-permute-start(bf16[128,256]{1,0:T(8,128)(2,1)S(1)} %fusion.44), channel_id=1, source_target_pairs={{7,10},{15,18},{23,26},{39,42},{47,50},{55,58},{71,74},{79,82},{87... | collective-permute-start | bytes 196616 | tf_op jit(solution)/shard_map/ppermute | solution.py:68
  14.6 30.6 %collective-permute-start.3 = (bf16[128,256]{1,0:T(8,128)(2,1)S(1)}, bf16[128,256]{1,0:T(8,128)(2,1)}, u32[]{:S(2)}, u32[]{:S(2)}) collective-permute-start(bf16[128,256]{1,0:T(8,128)(2,1)S(1)} %fusion.44), channel_id=1, source_target_pairs={{7,9},{15,17},{23,25},{39,41},{47,49},{55,57},{71,73},{79,81},{87,... | collective-permute-start | bytes 196616 | tf_op jit(solution)/shard_map/ppermute | solution.py:68
  16.6 28.7 %collective-permute-start.2 = (bf16[128,256]{1,0:T(8,128)(2,1)S(1)}, bf16[128,256]{1,0:T(8,128)(2,1)}, u32[]{:S(2)}, u32[]{:S(2)}) collective-permute-start(bf16[128,256]{1,0:T(8,128)(2,1)S(1)} %fusion.44), channel_id=1, source_target_pairs={{7,8},{15,16},{23,24},{39,40},{47,48},{55,56},{71,72},{79,80},{87,... | collective-permute-start | bytes 196616 | tf_op jit(solution)/shard_map/ppermute | solution.py:68
  43.3 28.8 %collective-permute-start = (bf16[128,256]{1,0:T(8,128)(2,1)S(1)}, bf16[128,256]{1,0:T(8,128)(2,1)S(1)}, u32[]{:S(2)}, u32[]{:S(2)}) collective-permute-start(bf16[128,256]{1,0:T(8,128)(2,1)S(1)} %fusion.44), channel_id=1, source_target_pairs={{0,2},{1,3},{2,4},{3,5},{4,6},{5,7},{6,8},{7,9},{8,10},{9,11},{10,... | collective-permute-start | bytes 196616 | tf_op jit(solution)/shard_map/ppermute | solution.py:13
  46.8 12.0 %collective-permute-start.10 = (bf16[128,256]{1,0:T(8,128)(2,1)S(1)}, bf16[128,256]{1,0:T(8,128)(2,1)S(1)}, u32[]{:S(2)}, u32[]{:S(2)}) collective-permute-start(bf16[128,256]{1,0:T(8,128)(2,1)S(1)} %add_add_fusion), channel_id=1, source_target_pairs={{7,31},{39,63},{71,95},{103,127},{135,159},{167,191},{199,223},{23... | collective-permute-start | bytes 196616 | tf_op jit(solution)/shard_map/ppermute | solution.py:73
  50.2 12.0 %collective-permute-start.9 = (bf16[128,256]{1,0:T(8,128)(2,1)S(1)}, bf16[128,256]{1,0:T(8,128)(2,1)S(1)}, u32[]{:S(2)}, u32[]{:S(2)}) collective-permute-start(bf16[128,256]{1,0:T(8,128)(2,1)S(1)} %add_add_fusion), channel_id=1, source_target_pairs={{7,25},{8,26},{9,27},{10,28},{11,29},{12,30},{39,57},{40,58},{41,5... | collective-permute-start | bytes 196616 | tf_op jit(solution)/shard_map/ppermute | solution.py:73
  52.7 14.9 %collective-permute-start.8 = (bf16[128,256]{1,0:T(8,128)(2,1)S(1)}, bf16[128,256]{1,0:T(8,128)(2,1)S(1)}, u32[]{:S(2)}, u32[]{:S(2)}) collective-permute-start(bf16[128,256]{1,0:T(8,128)(2,1)S(1)} %add_add_fusion), channel_id=1, source_target_pairs={{7,19},{8,20},{9,21},{10,22},{11,23},{12,24},{15,27},{16,28},{17,2... | collective-permute-start | bytes 196616 | tf_op jit(solution)/shard_map/ppermute | solution.py:73
  54.0 13.6 %collective-permute-start.7 = (bf16[128,256]{1,0:T(8,128)(2,1)S(1)}, bf16[128,256]{1,0:T(8,128)(2,1)S(1)}, u32[]{:S(2)}, u32[]{:S(2)}) collective-permute-start(bf16[128,256]{1,0:T(8,128)(2,1)S(1)} %add_add_fusion), channel_id=1, source_target_pairs={{7,13},{8,14},{9,15},{10,16},{11,17},{12,18},{15,21},{16,22},{17,2... | collective-permute-start | bytes 196616 | tf_op jit(solution)/shard_map/ppermute | solution.py:73
  58.9 13.2 %collective-permute-start.1 = (bf16[256,256]{1,0:T(8,128)(2,1)S(1)}, bf16[256,256]{1,0:T(8,128)(2,1)S(1)}, u32[]{:S(2)}, u32[]{:S(2)}) collective-permute-start(bf16[256,256]{1,0:T(8,128)(2,1)S(1)} %pad_maximum_fusion.2), channel_id=1, source_target_pairs={{0,1},{1,2},{2,3},{3,4},{4,5},{5,6},{6,7},{7,8},{8,9},{9,10},{10,1... | collective-permute-start | bytes 393224 | tf_op jit(solution)/shard_map/ppermute | solution.py:13
  62.2 17.2 %collective-permute-start.11 = (bf16[1,256,1024]{2,1,0:T(8,128)(2,1)}, bf16[1,256,1024]{2,1,0:T(8,128)(2,1)S(1)}, u32[]{:S(2)}, u32[]{:S(2)}) collective-permute-start(bf16[1,256,1024]{2,1,0:T(8,128)(2,1)} %param.43), channel_id=1, source_target_pairs={{32,0},{64,32},{96,64},{128,96},{160,128},{192,160},{224,192},{256... | collective-permute-start | bytes 1572872 | tf_op jit(solution)/shard_map/ppermute | solution.py:13
  88.5 11.7 %collective-permute-start.16 = (bf16[128,256]{1,0:T(8,128)(2,1)S(1)}, bf16[128,256]{1,0:T(8,128)(2,1)S(1)}, u32[]{:S(2)}, u32[]{:S(2)}) collective-permute-start(bf16[128,256]{1,0:T(8,128)(2,1)S(1)} %get-tuple-element.47), channel_id=1, source_target_pairs={{25,7},{26,8},{27,9},{28,10},{29,11},{30,12},{57,39},{58,40},{59,4... | collective-permute-start | bytes 196616 | tf_op jit(solution)/shard_map/ppermute | solution.py:143
  89.8 12.3 %collective-permute-start.18 = (bf16[128,256]{1,0:T(8,128)(2,1)S(1)}, bf16[128,256]{1,0:T(8,128)(2,1)S(1)}, u32[]{:S(2)}, u32[]{:S(2)}) collective-permute-start(bf16[128,256]{1,0:T(8,128)(2,1)S(1)} %get-tuple-element.47), channel_id=1, source_target_pairs={} | collective-permute-start | bytes 196616 | tf_op jit(solution)/shard_map/ppermute | solution.py:143
  90.5 13.6 %collective-permute-start.17 = (bf16[128,256]{1,0:T(8,128)(2,1)S(1)}, bf16[128,256]{1,0:T(8,128)(2,1)S(1)}, u32[]{:S(2)}, u32[]{:S(2)}) collective-permute-start(bf16[128,256]{1,0:T(8,128)(2,1)S(1)} %get-tuple-element.47), channel_id=1, source_target_pairs={{31,7},{63,39},{95,71},{127,103},{159,135},{191,167},{223,199},{25... | collective-permute-start | bytes 196616 | tf_op jit(solution)/shard_map/ppermute | solution.py:143
  93.2 10.9 %collective-permute-start.14 = (bf16[128,256]{1,0:T(8,128)(2,1)S(1)}, bf16[128,256]{1,0:T(8,128)(2,1)S(1)}, u32[]{:S(2)}, u32[]{:S(2)}) collective-permute-start(bf16[128,256]{1,0:T(8,128)(2,1)S(1)} %get-tuple-element.51), channel_id=1, source_target_pairs={{13,7},{14,8},{15,9},{16,10},{17,11},{18,12},{21,15},{22,16},{23,1... | collective-permute-start | bytes 196616 | tf_op jit(solution)/shard_map/ppermute | solution.py:143
  94.5 12.0 %collective-permute-start.15 = (bf16[128,256]{1,0:T(8,128)(2,1)S(1)}, bf16[128,256]{1,0:T(8,128)(2,1)S(1)}, u32[]{:S(2)}, u32[]{:S(2)}) collective-permute-start(bf16[128,256]{1,0:T(8,128)(2,1)S(1)} %get-tuple-element.52), channel_id=1, source_target_pairs={{19,7},{20,8},{21,9},{22,10},{23,11},{24,12},{27,15},{28,16},{29,1... | collective-permute-start | bytes 196616 | tf_op jit(solution)/shard_map/ppermute | solution.py:143
  100.2 10.1 %collective-permute-start.12 = (bf16[128,256]{1,0:T(8,128)(2,1)S(1)}, bf16[128,256]{1,0:T(8,128)(2,1)S(1)}, u32[]{:S(2)}, u32[]{:S(2)}) collective-permute-start(bf16[128,256]{1,0:T(8,128)(2,1)S(1)} %get-tuple-element.48), channel_id=1, source_target_pairs={{2,0},{3,1},{4,2},{5,3},{6,4},{7,5},{8,6},{9,7},{10,8},{11,9},{12,... | collective-permute-start | bytes 196616 | tf_op jit(solution)/shard_map/ppermute | solution.py:13
  102.2 10.7 %collective-permute-start.13 = (bf16[256,256]{1,0:T(8,128)(2,1)S(1)}, bf16[256,256]{1,0:T(8,128)(2,1)S(1)}, u32[]{:S(2)}, u32[]{:S(2)}) collective-permute-start(bf16[256,256]{1,0:T(8,128)(2,1)S(1)} %get-tuple-element.49), channel_id=1, source_target_pairs={{1,0},{2,1},{3,2},{4,3},{5,4},{6,5},{7,6},{8,7},{9,8},{10,9},{11,1... | collective-permute-start | bytes 393224 | tf_op jit(solution)/shard_map/ppermute | solution.py:13
  106.5 10.4 %collective-permute-start.23 = (f32[128,256]{1,0:T(8,128)S(1)}, f32[128,256]{1,0:T(8,128)S(1)}, u32[]{:S(2)}, u32[]{:S(2)}) collective-permute-start(f32[128,256]{1,0:T(8,128)S(1)} %fusion.42), channel_id=1, source_target_pairs={{12,7},{20,15},{28,23},{44,39},{52,47},{60,55},{76,71},{84,79},{92... | collective-permute-start | bytes 393224 | tf_op jit(solution)/shard_map/ppermute | solution.py:147
  107.8 10.7 %collective-permute-start.22 = (f32[128,256]{1,0:T(8,128)S(1)}, f32[128,256]{1,0:T(8,128)S(1)}, u32[]{:S(2)}, u32[]{:S(2)}) collective-permute-start(f32[128,256]{1,0:T(8,128)S(1)} %fusion.42), channel_id=1, source_target_pairs={{11,7},{19,15},{27,23},{43,39},{51,47},{59,55},{75,71},{83,79},{91... | collective-permute-start | bytes 393224 | tf_op jit(solution)/shard_map/ppermute | solution.py:147
  109.1 10.0 %collective-permute-start.21 = (f32[128,256]{1,0:T(8,128)S(1)}, f32[128,256]{1,0:T(8,128)S(1)}, u32[]{:S(2)}, u32[]{:S(2)}) collective-permute-start(f32[128,256]{1,0:T(8,128)S(1)} %fusion.42), channel_id=1, source_target_pairs={{10,7},{18,15},{26,23},{42,39},{50,47},{58,55},{74,71},{82,79},{90... | collective-permute-start | bytes 393224 | tf_op jit(solution)/shard_map/ppermute | solution.py:147
  110.4 11.3 %collective-permute-start.20 = (f32[128,256]{1,0:T(8,128)S(1)}, f32[128,256]{1,0:T(8,128)S(1)}, u32[]{:S(2)}, u32[]{:S(2)}) collective-permute-start(f32[128,256]{1,0:T(8,128)S(1)} %fusion.42), channel_id=1, source_target_pairs={{9,7},{17,15},{25,23},{41,39},{49,47},{57,55},{73,71},{81,79},{89,... | collective-permute-start | bytes 393224 | tf_op jit(solution)/shard_map/ppermute | solution.py:147
  112.9 9.0 %collective-permute-start.19 = (f32[128,256]{1,0:T(8,128)S(1)}, f32[128,256]{1,0:T(8,128)S(1)}, u32[]{:S(2)}, u32[]{:S(2)}) collective-permute-start(f32[128,256]{1,0:T(8,128)S(1)} %fusion.42), channel_id=1, source_target_pairs={{8,7},{16,15},{24,23},{40,39},{48,47},{56,55},{72,71},{80,79},{88,... | collective-permute-start | bytes 393224 | tf_op jit(solution)/shard_map/ppermute | solution.py:147
  (3 other events, 46.8 us)

commit v3 on v2

--- a/solution.py
+++ b/solution.py
@@ -1,3 +1,5 @@
+import functools
+
 import jax
 import jax.numpy as jnp
 from jax import lax
@@ -45,36 +47,40 @@
     lse_rows = jnp.swapaxes(lse_saved[0].reshape(group_heads, local_blocks, block_rows), 0, 1)
 
     paired = jnp.concatenate([attn_keys[0], attn_values[0]], axis=1)
+    own_blocks = paired.reshape(local_blocks, block_rows, 2 * head_size)
+    owners = [(k * stride + stride - 1) // local_blocks for k in range(n_summary)]
+    radix = 1
+    while radix * radix < ctx_count - owners[0]:
+        radix += 1
+
+    def member(position, k):
+        return (position >= owners[k]) & (position < owners[k] + radix)
+
+    relays = [x for x in range(ctx_count) if any(o <= x < o + radix for o in owners)]
+    is_owner = functools.reduce(jnp.logical_or, [device == o for o in owners])
+    owned = jnp.where(is_owner, own_blocks[(stride - 1) % local_blocks], 0).astype(jnp.bfloat16)
+    held = owned
     pieces = []
     for k in range(behind, 0, -1):
-        piece = paired[(local_blocks - counts[k - 1]) * block_rows :]
-        pieces.append(from_behind(piece, "ctx", k))
+        size = counts[k - 1] * block_rows
+        piece = paired[tokens - size :]
+        if k < radix:
+            arrived = from_behind(jnp.concatenate([piece, owned], axis=0), "ctx", k)
+            pieces.append(arrived[:size])
+            held = held + arrived[size:]
+        else:
+            pieces.append(from_behind(piece, "ctx", k))
     pieces.append(paired)
-    own_blocks = paired.reshape(local_blocks, block_rows, 2 * head_size)
-    owners = [(k * stride + stride - 1) // local_blocks for k in range(n_summary)]
-    owned = own_blocks[(stride - 1) % local_blocks]
-    radix = 1
-    while radix * radix < ctx_count:
-        radix += 1
-    relay_of = [-1] * ctx_count
-    for k, owner in enumerate(owners):
-        for x in range(owner, min(owner + radix, ctx_count)):
-            relay_of[x] = k
-    relay_table = jnp.array(relay_of, dtype=jnp.int32)
-    is_owner = jnp.array([x in owners for x in range(ctx_count)])[device]
-    held = jnp.where(is_owner, owned, 0).astype(jnp.bfloat16)
-    for shift in range(1, radix):
+    for shift in range(behind + 1, radix):
         route = [(o, o + shift) for o in owners if o + shift < ctx_count]
         held = held + lax.ppermute(owned, "ctx", route)
-    summary_parts = [jnp.where(relay_table[device] == k, held, 0) for k in range(n_summary)]
+    summary_parts = [jnp.where(member(device, k), held, 0) for k in range(n_summary)]
     for hop in range(1, radix):
         shift = hop * radix
-        route = [(x, x + shift) for x in range(ctx_count - shift) if relay_of[x] >= 0]
+        route = [(x, x + shift) for x in relays if x + shift < ctx_count]
         arrived = lax.ppermute(held, "ctx", route)
         for k in range(n_summary):
-            came = [x + shift < ctx_count and relay_of[x] == k for x in range(ctx_count)]
-            came = jnp.array([False] * shift + came[: ctx_count - shift])
-            summary_parts[k] = summary_parts[k] + jnp.where(came[device], arrived, 0)
+            summary_parts[k] = summary_parts[k] + jnp.where(member(device - shift, k), arrived, 0)
     summary_kv = jnp.stack(summary_parts).astype(jnp.bfloat16)
     table = jnp.concatenate(pieces + [summary_kv.reshape(n_summary * block_rows, -1)], axis=0)
     key_table = table[:, :head_size]
@@ -130,16 +136,16 @@
         totals = totals.at[tokens - size :].add(returned)
         offset += size
     summary_low = partial[span * block_rows :].reshape(n_summary, block_rows, -1)
-    tree_slot = jnp.maximum(relay_table[device], 0)
-    gathered = lax.dynamic_index_in_dim(summary_low, tree_slot, 0, keepdims=False).astype(
-        jnp.float32
-    )
+
+    def slot_at(position):
+        return sum(jnp.where(member(position, k), k, 0) for k in range(n_summary))
+
+    gathered = lax.dynamic_index_in_dim(summary_low, slot_at(device), 0, keepdims=False)
+    gathered = gathered.astype(jnp.float32)
     for hop in range(1, radix):
         shift = hop * radix
-        route = [(x + shift, x) for x in range(ctx_count - shift) if relay_of[x] >= 0]
-        sent_slot = [max(relay_of[y - shift], 0) if y >= shift else 0 for y in range(ctx_count)]
-        slot_here = jnp.array(sent_slot, dtype=jnp.int32)[device]
-        outgoing = lax.dynamic_index_in_dim(summary_low, slot_here, 0, keepdims=False)
+        route = [(x + shift, x) for x in relays if x + shift < ctx_count]
+        outgoing = lax.dynamic_index_in_dim(summary_low, slot_at(device - shift), 0, keepdims=False)
         gathered = gathered + lax.ppermute(outgoing, "ctx", route).astype(jnp.float32)
     owner_total = gathered
     for shift in range(1, radix):

time: 125 us -> 98.5 us (0.79)
  local copies, waits for them, and re-layouts: 17.8 us -> 5.43 us
  other arithmetic: 13 us -> 6.81 us
  between operations: 7.47 us -> 1.29 us
  starting transfers between devices: 54.9 us -> 49.5 us
  waiting for transfers between devices: 15.6 us -> 20.9 us
    dynamic_slice x11 -> x0, local copies, waits for them, and re-layouts: 13.9 us -> none  [the longest x7 8.85 us: on_device(): summary_parts[k] = summary_parts[k] + jnp.where(came[device], arrived, 0)]
    ppermute x5 -> x2, starting transfers between devices: 17 us -> 8.87 us  [on_device(): held = held + lax.ppermute(owned, 'ctx', route)]
    ppermute x4, starting transfers between devices: 11.1 us -> 17.3 us  [on_device(): arrived = lax.ppermute(held, 'ctx', route)]
    another operation x2 -> x3, other arithmetic: 4.45 us -> 0.12 us  [on_device(): summary_kv = jnp.stack(summary_parts).astype(jnp.bfloat16)]
    ppermute x5 -> x4, waiting for transfers between devices: 6.74 us -> 11.1 us  [on_device(): lax.ppermute(outgoing, 'ctx', route).astype(jnp.float32)]
    ppermute x5 -> x4, waiting for transfers between devices: 7.63 us -> 9.78 us  [on_device(): owner_total = owner_total + lax.ppermute(gathered, 'ctx', route)]
    add x1 -> x0, other arithmetic: 1.61 us -> none  [on_device(): held = held + lax.ppermute(owned, 'ctx', route)]
    ppermute x5, starting transfers between devices: 14.4 us -> 13 us  [from_behind(): return lax.ppermute(block, axis, route)]
  transfers between devices with their start and end apart: 24 -> 19, of which waited for: 8 -> 7; matrix products, arithmetic and copies ran while one was open for 28% -> 13% of each run, Pallas kernels for 0% -> 0%
where the time goes in v3:
time: 98.5 us; the launch traced here: 97.8 us
  starting transfers between devices  49.5 us (50%)
  waiting for transfers between devices  20.9 us (21%)
  matrix products  13.8 us (14%)
  other arithmetic  6.81 us (7%)
  local copies, waits for them, and re-layouts  5.43 us (6%)
  between operations  1.29 us (1%)
    ppermute x4, starting transfers between devices, on_device(): arrived = lax.ppermute(held, 'ctx', route)  17.3 us
    ppermute x5, starting transfers between devices, from_behind(): return lax.ppermute(block, axis, route)  13 us
    ppermute x4, waiting for transfers between devices, on_device(): lax.ppermute(outgoing, 'ctx', route).astype(jnp.float32)  11.1 us
    ppermute x4, waiting for transfers between devices, on_device(): owner_total = owner_total + lax.ppermute(gathered, 'ctx', route)  9.78 us
    ppermute x2, starting transfers between devices, on_device(): held = held + lax.ppermute(owned, 'ctx', route)  8.87 us
    dot_general x1, matrix products, on_device(): jnp.einsum('rtgh,uh->rgtu', query_heads, key_table, preferred_element_typ...  5.69 us
    ppermute x4, starting transfers between devices, on_device(): owner_total = owner_total + lax.ppermute(gathered, 'ctx', route)  5.17 us
    ppermute x4, starting transfers between devices, on_device(): lax.ppermute(outgoing, 'ctx', route).astype(jnp.float32)  5.17 us
  transfers between devices with their start and end apart: 19, of which 7 were waited for; matrix products, arithmetic and copies ran while one was open for 13% of the time, Pallas kernels for 0%

profile of v3, /device:TPU:199, one launch (start us, length us, event | category | flops | bytes accessed | tf_op | source)
XLA Modules:
  0.0 97.8 jit_solution(4643677848294084428)
XLA Ops:
  1.5 7.6 %collective-permute-start.2 = (bf16[128,256]{1,0:T(8,128)(2,1)S(1)}, bf16[128,256]{1,0:T(8,128)(2,1)S(1)}, u32[]{:S(2)}, u32[]{:S(2)}) collective-permute-start(bf16[128,256]{1,0:T(8,128)(2,1)S(1)} %get-tuple-element.47), channel_id=1, source_target_pairs={{7,10},{15,18},{23,26},{39,42},{47,50},{55,58},{71,74},{79,82},{87... | collective-permute-start | bytes 196616 | tf_op jit(solution)/shard_map/ppermute | solution.py:76
  9.1 1.3 %collective-permute-start.3 = (bf16[128,256]{1,0:T(8,128)(2,1)S(1)}, bf16[128,256]{1,0:T(8,128)(2,1)S(1)}, u32[]{:S(2)}, u32[]{:S(2)}) collective-permute-start(bf16[128,256]{1,0:T(8,128)(2,1)S(1)} %get-tuple-element.47), channel_id=1, source_target_pairs={{7,11},{15,19},{23,27},{39,43},{47,51},{55,59},{71,75},{79,83},{87... | collective-permute-start | bytes 196616 | tf_op jit(solution)/shard_map/ppermute | solution.py:76
  10.4 1.9 %collective-permute-start = (bf16[256,256]{1,0:T(8,128)(2,1)S(1)}, bf16[256,256]{1,0:T(8,128)(2,1)S(1)}, u32[]{:S(2)}, u32[]{:S(2)}) collective-permute-start(bf16[256,256]{1,0:T(8,128)(2,1)S(1)} %pad_maximum_fusion.4), channel_id=1, source_target_pairs={{0,2},{1,3},{2,4},{3,5},{4,6},{5,7},{6,8},{7,9},{8,10},{9,11},{10,... | collective-permute-start | bytes 393224 | tf_op jit(solution)/shard_map/ppermute | solution.py:15
  13.2 1.9 %collective-permute-start.1 = (bf16[384,256]{1,0:T(8,128)(2,1)S(1)}, bf16[384,256]{1,0:T(8,128)(2,1)S(1)}, u32[]{:S(2)}, u32[]{:S(2)}) collective-permute-start(bf16[384,256]{1,0:T(8,128)(2,1)S(1)} %pad_maximum_fusion.2), channel_id=1, source_target_pairs={{0,1},{1,2},{2,3},{3,4},{4,5},{5,6},{6,7},{7,8},{8,9},{9,10},{10,1... | collective-permute-start | bytes 589832 | tf_op jit(solution)/shard_map/ppermute | solution.py:15
  15.2 5.4 %collective-permute-start.8 = (bf16[1,256,1024]{2,1,0:T(8,128)(2,1)}, bf16[1,256,1024]{2,1,0:T(8,128)(2,1)}, u32[]{:S(2)}, u32[]{:S(2)}) collective-permute-start(bf16[1,256,1024]{2,1,0:T(8,128)(2,1)} %param.21), channel_id=1, source_target_pairs={{32,0},{64,32},{96,64},{128,96},{160,128},{192,160},{224,192},{256... | collective-permute-start | bytes 1572872 | tf_op jit(solution)/shard_map/ppermute | solution.py:15
  23.6 10.8 %collective-permute-start.7 = (bf16[128,256]{1,0:T(8,128)(2,1)S(1)}, bf16[128,256]{1,0:T(8,128)(2,1)S(1)}, u32[]{:S(2)}, u32[]{:S(2)}) collective-permute-start(bf16[128,256]{1,0:T(8,128)(2,1)S(1)} %get-tuple-element.60), channel_id=1, source_target_pairs={{7,27},{8,28},{9,29},{10,30},{11,31},{39,59},{40,60},{41,61},{42,6... | collective-permute-start | bytes 196616 | tf_op jit(solution)/shard_map/ppermute | solution.py:81
  34.4 3.8 %collective-permute-start.6 = (bf16[128,256]{1,0:T(8,128)(2,1)S(1)}, bf16[128,256]{1,0:T(8,128)(2,1)S(1)}, u32[]{:S(2)}, u32[]{:S(2)}) collective-permute-start(bf16[128,256]{1,0:T(8,128)(2,1)S(1)} %get-tuple-element.60), channel_id=1, source_target_pairs={{7,22},{8,23},{9,24},{10,25},{11,26},{15,30},{16,31},{39,54},{40,5... | collective-permute-start | bytes 196616 | tf_op jit(solution)/shard_map/ppermute | solution.py:81
  38.3 1.3 %collective-permute-start.5 = (bf16[128,256]{1,0:T(8,128)(2,1)S(1)}, bf16[128,256]{1,0:T(8,128)(2,1)S(1)}, u32[]{:S(2)}, u32[]{:S(2)}) collective-permute-start(bf16[128,256]{1,0:T(8,128)(2,1)S(1)} %get-tuple-element.60), channel_id=1, source_target_pairs={{7,17},{8,18},{9,19},{10,20},{11,21},{15,25},{16,26},{17,27},{18,2... | collective-permute-start | bytes 196616 | tf_op jit(solution)/shard_map/ppermute | solution.py:81
  39.6 1.3 %collective-permute-start.4 = (bf16[128,256]{1,0:T(8,128)(2,1)S(1)}, bf16[128,256]{1,0:T(8,128)(2,1)S(1)}, u32[]{:S(2)}, u32[]{:S(2)}) collective-permute-start(bf16[128,256]{1,0:T(8,128)(2,1)S(1)} %get-tuple-element.60), channel_id=1, source_target_pairs={{7,12},{8,13},{9,14},{10,15},{11,16},{15,20},{16,21},{17,22},{18,2... | collective-permute-start | bytes 196616 | tf_op jit(solution)/shard_map/ppermute | solution.py:81
  44.4 5.7 %fusion.4 = (bf16[2,8,128,1024]{2,3,1,0:T(8,128)(2,1)}, f32[1024,2,128,8]{2,0,3,1:T(8,128)}) fusion(f32[2,8,128]{2,1,0:T(8,128)S(1)} %bitcast.121, pred[2,128,1024]{1,2,0:T(8,128)(4,1)S(1)} %or_and_fusion, bf16[2,128,8,128]{3,2,1,0:T(8,128)(2,1)S(1)} %bitcast.104, bf16[1024,256]{1,0:T(8,128)(2,1)S(1)} %pad_maximum_fusion), kind=kOutput, calls=%fused_computation.6 | convolution fusion | flops 545259520 | bytes 13639680 | tf_op jit(solution)/shard_map/rtgh,uh->rgtu/dot_general | solution.py:110
  50.1 1.4 %fusion.27 = bf16[32,8,8,128]{3,1,2,0:T(8,128)(2,1)S(1)} fusion(bf16[1,256,1024]{2,1,0:T(8,128)(2,1)} %collective-permute-done.8, bf16[1,256,1024]{2,1,0:T(8,128)(2,1)} %param.20), kind=kLoop, calls=%fused_computation.30 | loop fusion | flops 1048576 | bytes 1572864
  52.0 4.9 %fusion.1 = bf16[2,8,128,1024]{2,3,1,0:T(8,128)(2,1)S(1)} fusion(f32[1024,2,128,8]{2,0,3,1:T(8,128)} %get-tuple-element.62, f32[2,8,128]{2,1,0:T(8,128)S(1)} %copy.46, f32[2,8,128]{2,1,0:T(8,128)S(1)} %bitcast.122, pred[2,128,1024]{1,2,0:T(8,128)(4,1)S(1)} %or_and_fusion, bf16[2,128,8,128]{3,2,1,0:T(8,128)(2,1)S(1)} %bitcast.107, ...), kind=kOutput, calls=%fused_computation.2 | convolution fusion | flops 549453824 | bytes 13647872 | tf_op jit(solution)/shard_map/rtgh,uh->rgtu/dot_general | solution.py:114
  61.7 1.9 %collective-permute-start.9 = (bf16[128,256]{1,0:T(8,128)(2,1)S(1)}, bf16[128,256]{1,0:T(8,128)(2,1)S(1)}, u32[]{:S(2)}, u32[]{:S(2)}) collective-permute-start(bf16[128,256]{1,0:T(8,128)(2,1)S(1)} %fusion.41), channel_id=1, source_target_pairs={{2,0},{3,1},{4,2},{5,3},{6,4},{7,5},{8,6},{9,7},{10,8},{11,9},{12,... | collective-permute-start | bytes 196616 | tf_op jit(solution)/shard_map/ppermute | solution.py:15
  63.7 1.3 %collective-permute-start.11 = (bf16[128,256]{1,0:T(8,128)(2,1)S(1)}, bf16[128,256]{1,0:T(8,128)(2,1)S(1)}, u32[]{:S(2)}, u32[]{:S(2)}) collective-permute-start(bf16[128,256]{1,0:T(8,128)(2,1)S(1)} %get-tuple-element.53), channel_id=1, source_target_pairs={{12,7},{13,8},{14,9},{15,10},{16,11},{20,15},{21,16},{22,17},{23,1... | collective-permute-start | bytes 196616 | tf_op jit(solution)/shard_map/ppermute | solution.py:149
  65.0 1.3 %collective-permute-start.14 = (bf16[128,256]{1,0:T(8,128)(2,1)S(1)}, bf16[128,256]{1,0:T(8,128)(2,1)S(1)}, u32[]{:S(2)}, u32[]{:S(2)}) collective-permute-start(bf16[128,256]{1,0:T(8,128)(2,1)S(1)} %get-tuple-element.54), channel_id=1, source_target_pairs={{27,7},{28,8},{29,9},{30,10},{31,11},{59,39},{60,40},{61,41},{62,4... | collective-permute-start | bytes 196616 | tf_op jit(solution)/shard_map/ppermute | solution.py:149
  66.3 1.3 %collective-permute-start.13 = (bf16[128,256]{1,0:T(8,128)(2,1)S(1)}, bf16[128,256]{1,0:T(8,128)(2,1)S(1)}, u32[]{:S(2)}, u32[]{:S(2)}) collective-permute-start(bf16[128,256]{1,0:T(8,128)(2,1)S(1)} %get-tuple-element.55), channel_id=1, source_target_pairs={{22,7},{23,8},{24,9},{25,10},{26,11},{30,15},{31,16},{54,39},{55,4... | collective-permute-start | bytes 196616 | tf_op jit(solution)/shard_map/ppermute | solution.py:149
  68.9 3.4 %collective-permute-done.11 = bf16[128,256]{1,0:T(8,128)(2,1)S(1)} collective-permute-done((bf16[128,256]{1,0:T(8,128)(2,1)S(1)}, bf16[128,256]{1,0:T(8,128)(2,1)S(1)}, u32[]{:S(2)}, u32[]{:S(2)}) %collective-permute-start.11) | collective-permute-done | bytes 65568 | tf_op jit(solution)/shard_map/ppermute | solution.py:149
  72.2 1.9 %collective-permute-start.10 = (bf16[256,256]{1,0:T(8,128)(2,1)S(1)}, bf16[256,256]{1,0:T(8,128)(2,1)S(1)}, u32[]{:S(2)}, u32[]{:S(2)}) collective-permute-start(bf16[256,256]{1,0:T(8,128)(2,1)S(1)} %get-tuple-element.49), channel_id=1, source_target_pairs={{1,0},{2,1},{3,2},{4,3},{5,4},{6,5},{7,6},{8,7},{9,8},{10,9},{11,1... | collective-permute-start | bytes 393224 | tf_op jit(solution)/shard_map/ppermute | solution.py:15
  74.2 1.5 %collective-permute-done.14 = bf16[128,256]{1,0:T(8,128)(2,1)S(1)} collective-permute-done((bf16[128,256]{1,0:T(8,128)(2,1)S(1)}, bf16[128,256]{1,0:T(8,128)(2,1)S(1)}, u32[]{:S(2)}, u32[]{:S(2)}) %collective-permute-start.14) | collective-permute-done | bytes 65568 | tf_op jit(solution)/shard_map/ppermute | solution.py:149
  75.7 6.2 %collective-permute-done.13 = bf16[128,256]{1,0:T(8,128)(2,1)S(1)} collective-permute-done((bf16[128,256]{1,0:T(8,128)(2,1)S(1)}, bf16[128,256]{1,0:T(8,128)(2,1)S(1)}, u32[]{:S(2)}, u32[]{:S(2)}) %collective-permute-start.13) | collective-permute-done | bytes 65568 | tf_op jit(solution)/shard_map/ppermute | solution.py:149
  85.8 1.3 %collective-permute-start.15 = (f32[128,256]{1,0:T(8,128)S(1)}, f32[128,256]{1,0:T(8,128)S(1)}, u32[]{:S(2)}, u32[]{:S(2)}) collective-permute-start(f32[128,256]{1,0:T(8,128)S(1)} %fusion.40), channel_id=1, source_target_pairs={{8,7},{16,15},{24,23},{40,39},{48,47},{56,55},{72,71},{80,79},{88,... | collective-permute-start | bytes 393224 | tf_op jit(solution)/shard_map/ppermute | solution.py:153
  87.2 6.2 %collective-permute-done.18 = f32[128,256]{1,0:T(8,128)S(1)} collective-permute-done((f32[128,256]{1,0:T(8,128)S(1)}, f32[128,256]{1,0:T(8,128)S(1)}, u32[]{:S(2)}, u32[]{:S(2)}) %collective-permute-start.18) | collective-permute-done | bytes 131104 | tf_op jit(solution)/shard_map/ppermute | solution.py:153
  93.4 1.6 %collective-permute-done.17 = f32[128,256]{1,0:T(8,128)S(1)} collective-permute-done((f32[128,256]{1,0:T(8,128)S(1)}, f32[128,256]{1,0:T(8,128)S(1)}, u32[]{:S(2)}, u32[]{:S(2)}) %collective-permute-start.17) | collective-permute-done | bytes 131104 | tf_op jit(solution)/shard_map/ppermute | solution.py:153
  95.0 1.3 %collective-permute-done.16 = f32[128,256]{1,0:T(8,128)S(1)} collective-permute-done((f32[128,256]{1,0:T(8,128)S(1)}, f32[128,256]{1,0:T(8,128)S(1)}, u32[]{:S(2)}, u32[]{:S(2)}) %collective-permute-start.16) | collective-permute-done | bytes 131104 | tf_op jit(solution)/shard_map/ppermute | solution.py:153
  (70 shorter events, 19.9 us)
Async XLA Ops:
  0.6 43.7 %copy-start.1 = (bf16[1,256,128]{2,1,0:T(8,128)(2,1)S(1)}, bf16[1,256,128]{2,1,0:T(8,128)(2,1)}, u32[]{:S(2)}) copy-start(bf16[1,256,128]{2,1,0:T(8,128)(2,1)} %param.18) | copy-start | bytes 196612
  0.6 43.7 %copy-start.2 = (bf16[1,256,128]{2,1,0:T(8,128)(2,1)S(1)}, bf16[1,256,128]{2,1,0:T(8,128)(2,1)}, u32[]{:S(2)}) copy-start(bf16[1,256,128]{2,1,0:T(8,128)(2,1)} %param.17) | copy-start | bytes 196612
  0.7 43.7 %copy-start.4 = (f32[1,8,256]{2,1,0:T(8,128)S(1)}, f32[1,8,256]{2,1,0:T(8,128)}, u32[]{:S(2)}) copy-start(f32[1,8,256]{2,1,0:T(8,128)} %param.22) | copy-start | bytes 24580
  1.5 21.4 %collective-permute-start.2 = (bf16[128,256]{1,0:T(8,128)(2,1)S(1)}, bf16[128,256]{1,0:T(8,128)(2,1)S(1)}, u32[]{:S(2)}, u32[]{:S(2)}) collective-permute-start(bf16[128,256]{1,0:T(8,128)(2,1)S(1)} %get-tuple-element.47), channel_id=1, source_target_pairs={{7,10},{15,18},{23,26},{39,42},{47,50},{55,58},{71,74},{79,82},{87... | collective-permute-start | bytes 196616 | tf_op jit(solution)/shard_map/ppermute | solution.py:76
  9.1 13.8 %collective-permute-start.3 = (bf16[128,256]{1,0:T(8,128)(2,1)S(1)}, bf16[128,256]{1,0:T(8,128)(2,1)S(1)}, u32[]{:S(2)}, u32[]{:S(2)}) collective-permute-start(bf16[128,256]{1,0:T(8,128)(2,1)S(1)} %get-tuple-element.47), channel_id=1, source_target_pairs={{7,11},{15,19},{23,27},{39,43},{47,51},{55,59},{71,75},{79,83},{87... | collective-permute-start | bytes 196616 | tf_op jit(solution)/shard_map/ppermute | solution.py:76
  10.4 12.5 %collective-permute-start = (bf16[256,256]{1,0:T(8,128)(2,1)S(1)}, bf16[256,256]{1,0:T(8,128)(2,1)S(1)}, u32[]{:S(2)}, u32[]{:S(2)}) collective-permute-start(bf16[256,256]{1,0:T(8,128)(2,1)S(1)} %pad_maximum_fusion.4), channel_id=1, source_target_pairs={{0,2},{1,3},{2,4},{3,5},{4,6},{5,7},{6,8},{7,9},{8,10},{9,11},{10,... | collective-permute-start | bytes 393224 | tf_op jit(solution)/shard_map/ppermute | solution.py:15
  13.2 9.7 %collective-permute-start.1 = (bf16[384,256]{1,0:T(8,128)(2,1)S(1)}, bf16[384,256]{1,0:T(8,128)(2,1)S(1)}, u32[]{:S(2)}, u32[]{:S(2)}) collective-permute-start(bf16[384,256]{1,0:T(8,128)(2,1)S(1)} %pad_maximum_fusion.2), channel_id=1, source_target_pairs={{0,1},{1,2},{2,3},{3,4},{4,5},{5,6},{6,7},{7,8},{8,9},{9,10},{10,1... | collective-permute-start | bytes 589832 | tf_op jit(solution)/shard_map/ppermute | solution.py:15
  15.2 34.9 %collective-permute-start.8 = (bf16[1,256,1024]{2,1,0:T(8,128)(2,1)}, bf16[1,256,1024]{2,1,0:T(8,128)(2,1)}, u32[]{:S(2)}, u32[]{:S(2)}) collective-permute-start(bf16[1,256,1024]{2,1,0:T(8,128)(2,1)} %param.21), channel_id=1, source_target_pairs={{32,0},{64,32},{96,64},{128,96},{160,128},{192,160},{224,192},{256... | collective-permute-start | bytes 1572872 | tf_op jit(solution)/shard_map/ppermute | solution.py:15
  22.9 0.7 copy-start.3
  23.6 20.5 %collective-permute-start.7 = (bf16[128,256]{1,0:T(8,128)(2,1)S(1)}, bf16[128,256]{1,0:T(8,128)(2,1)S(1)}, u32[]{:S(2)}, u32[]{:S(2)}) collective-permute-start(bf16[128,256]{1,0:T(8,128)(2,1)S(1)} %get-tuple-element.60), channel_id=1, source_target_pairs={{7,27},{8,28},{9,29},{10,30},{11,31},{39,59},{40,60},{41,61},{42,6... | collective-permute-start | bytes 196616 | tf_op jit(solution)/shard_map/ppermute | solution.py:81
  34.4 9.7 %collective-permute-start.6 = (bf16[128,256]{1,0:T(8,128)(2,1)S(1)}, bf16[128,256]{1,0:T(8,128)(2,1)S(1)}, u32[]{:S(2)}, u32[]{:S(2)}) collective-permute-start(bf16[128,256]{1,0:T(8,128)(2,1)S(1)} %get-tuple-element.60), channel_id=1, source_target_pairs={{7,22},{8,23},{9,24},{10,25},{11,26},{15,30},{16,31},{39,54},{40,5... | collective-permute-start | bytes 196616 | tf_op jit(solution)/shard_map/ppermute | solution.py:81
  38.3 5.8 %collective-permute-start.5 = (bf16[128,256]{1,0:T(8,128)(2,1)S(1)}, bf16[128,256]{1,0:T(8,128)(2,1)S(1)}, u32[]{:S(2)}, u32[]{:S(2)}) collective-permute-start(bf16[128,256]{1,0:T(8,128)(2,1)S(1)} %get-tuple-element.60), channel_id=1, source_target_pairs={{7,17},{8,18},{9,19},{10,20},{11,21},{15,25},{16,26},{17,27},{18,2... | collective-permute-start | bytes 196616 | tf_op jit(solution)/shard_map/ppermute | solution.py:81
  39.6 4.6 %collective-permute-start.4 = (bf16[128,256]{1,0:T(8,128)(2,1)S(1)}, bf16[128,256]{1,0:T(8,128)(2,1)S(1)}, u32[]{:S(2)}, u32[]{:S(2)}) collective-permute-start(bf16[128,256]{1,0:T(8,128)(2,1)S(1)} %get-tuple-element.60), channel_id=1, source_target_pairs={{7,12},{8,13},{9,14},{10,15},{11,16},{15,20},{16,21},{17,22},{18,2... | collective-permute-start | bytes 196616 | tf_op jit(solution)/shard_map/ppermute | solution.py:81
  56.9 2.2 %copy-start = (bf16[2,8,128,1024]{2,3,1,0:T(8,128)(2,1)S(1)}, bf16[2,8,128,1024]{2,3,1,0:T(8,128)(2,1)}, u32[]{:S(2)}) copy-start(bf16[2,8,128,1024]{2,3,1,0:T(8,128)(2,1)} %get-tuple-element.61) | copy-start | bytes 12582916
  61.7 24.1 %collective-permute-start.9 = (bf16[128,256]{1,0:T(8,128)(2,1)S(1)}, bf16[128,256]{1,0:T(8,128)(2,1)S(1)}, u32[]{:S(2)}, u32[]{:S(2)}) collective-permute-start(bf16[128,256]{1,0:T(8,128)(2,1)S(1)} %fusion.41), channel_id=1, source_target_pairs={{2,0},{3,1},{4,2},{5,3},{6,4},{7,5},{8,6},{9,7},{10,8},{11,9},{12,... | collective-permute-start | bytes 196616 | tf_op jit(solution)/shard_map/ppermute | solution.py:15
  63.7 8.6 %collective-permute-start.11 = (bf16[128,256]{1,0:T(8,128)(2,1)S(1)}, bf16[128,256]{1,0:T(8,128)(2,1)S(1)}, u32[]{:S(2)}, u32[]{:S(2)}) collective-permute-start(bf16[128,256]{1,0:T(8,128)(2,1)S(1)} %get-tuple-element.53), channel_id=1, source_target_pairs={{12,7},{13,8},{14,9},{15,10},{16,11},{20,15},{21,16},{22,17},{23,1... | collective-permute-start | bytes 196616 | tf_op jit(solution)/shard_map/ppermute | solution.py:149
  65.0 10.7 %collective-permute-start.14 = (bf16[128,256]{1,0:T(8,128)(2,1)S(1)}, bf16[128,256]{1,0:T(8,128)(2,1)S(1)}, u32[]{:S(2)}, u32[]{:S(2)}) collective-permute-start(bf16[128,256]{1,0:T(8,128)(2,1)S(1)} %get-tuple-element.54), channel_id=1, source_target_pairs={{27,7},{28,8},{29,9},{30,10},{31,11},{59,39},{60,40},{61,41},{62,4... | collective-permute-start | bytes 196616 | tf_op jit(solution)/shard_map/ppermute | solution.py:149
  66.3 15.6 %collective-permute-start.13 = (bf16[128,256]{1,0:T(8,128)(2,1)S(1)}, bf16[128,256]{1,0:T(8,128)(2,1)S(1)}, u32[]{:S(2)}, u32[]{:S(2)}) collective-permute-start(bf16[128,256]{1,0:T(8,128)(2,1)S(1)} %get-tuple-element.55), channel_id=1, source_target_pairs={{22,7},{23,8},{24,9},{25,10},{26,11},{30,15},{31,16},{54,39},{55,4... | collective-permute-start | bytes 196616 | tf_op jit(solution)/shard_map/ppermute | solution.py:149
  67.6 14.3 %collective-permute-start.12 = (bf16[128,256]{1,0:T(8,128)(2,1)S(1)}, bf16[128,256]{1,0:T(8,128)(2,1)S(1)}, u32[]{:S(2)}, u32[]{:S(2)}) collective-permute-start(bf16[128,256]{1,0:T(8,128)(2,1)S(1)} %get-tuple-element.56), channel_id=1, source_target_pairs={{17,7},{18,8},{19,9},{20,10},{21,11},{25,15},{26,16},{27,17},{28,1... | collective-permute-start | bytes 196616 | tf_op jit(solution)/shard_map/ppermute | solution.py:149
  72.2 14.9 %collective-permute-start.10 = (bf16[256,256]{1,0:T(8,128)(2,1)S(1)}, bf16[256,256]{1,0:T(8,128)(2,1)S(1)}, u32[]{:S(2)}, u32[]{:S(2)}) collective-permute-start(bf16[256,256]{1,0:T(8,128)(2,1)S(1)} %get-tuple-element.49), channel_id=1, source_target_pairs={{1,0},{2,1},{3,2},{4,3},{5,4},{6,5},{7,6},{8,7},{9,8},{10,9},{11,1... | collective-permute-start | bytes 393224 | tf_op jit(solution)/shard_map/ppermute | solution.py:15
  81.9 11.5 %collective-permute-start.18 = (f32[128,256]{1,0:T(8,128)S(1)}, f32[128,256]{1,0:T(8,128)S(1)}, u32[]{:S(2)}, u32[]{:S(2)}) collective-permute-start(f32[128,256]{1,0:T(8,128)S(1)} %fusion.40), channel_id=1, source_target_pairs={{11,7},{19,15},{27,23},{43,39},{51,47},{59,55},{75,71},{83,79},{91... | collective-permute-start | bytes 393224 | tf_op jit(solution)/shard_map/ppermute | solution.py:153
  83.2 11.8 %collective-permute-start.17 = (f32[128,256]{1,0:T(8,128)S(1)}, f32[128,256]{1,0:T(8,128)S(1)}, u32[]{:S(2)}, u32[]{:S(2)}) collective-permute-start(f32[128,256]{1,0:T(8,128)S(1)} %fusion.40), channel_id=1, source_target_pairs={{10,7},{18,15},{26,23},{42,39},{50,47},{58,55},{74,71},{82,79},{90... | collective-permute-start | bytes 393224 | tf_op jit(solution)/shard_map/ppermute | solution.py:153
  84.5 11.9 %collective-permute-start.16 = (f32[128,256]{1,0:T(8,128)S(1)}, f32[128,256]{1,0:T(8,128)S(1)}, u32[]{:S(2)}, u32[]{:S(2)}) collective-permute-start(f32[128,256]{1,0:T(8,128)S(1)} %fusion.40), channel_id=1, source_target_pairs={{9,7},{17,15},{25,23},{41,39},{49,47},{57,55},{73,71},{81,79},{89,... | collective-permute-start | bytes 393224 | tf_op jit(solution)/shard_map/ppermute | solution.py:153
  85.8 11.2 %collective-permute-start.15 = (f32[128,256]{1,0:T(8,128)S(1)}, f32[128,256]{1,0:T(8,128)S(1)}, u32[]{:S(2)}, u32[]{:S(2)}) collective-permute-start(f32[128,256]{1,0:T(8,128)S(1)} %fusion.40), channel_id=1, source_target_pairs={{8,7},{16,15},{24,23},{40,39},{48,47},{56,55},{72,71},{80,79},{88,... | collective-permute-start | bytes 393224 | tf_op jit(solution)/shard_map/ppermute | solution.py:153

commit v4 on v3

--- a/solution.py
+++ b/solution.py
@@ -82,9 +82,8 @@
         for k in range(n_summary):
             summary_parts[k] = summary_parts[k] + jnp.where(member(device - shift, k), arrived, 0)
     summary_kv = jnp.stack(summary_parts).astype(jnp.bfloat16)
-    table = jnp.concatenate(pieces + [summary_kv.reshape(n_summary * block_rows, -1)], axis=0)
-    key_table = table[:, :head_size]
-    value_table = table[:, head_size:]
+    local_table = jnp.concatenate(pieces, axis=0)
+    summary_table = summary_kv.reshape(n_summary * block_rows, -1)
     slots = span + n_summary
 
     targets = block_keys
@@ -102,31 +101,46 @@
     causal = positions[None, :] <= positions[:, None]
     earlier = table_ids[None, :] < query_ids[:, None]
     allowed = chosen[:, None, :, None] & (earlier[:, None, :, None] | causal[None, :, None, :])
-    allowed = allowed.reshape(local_blocks, block_rows, slots * block_rows)
 
     query_heads = queries[0].reshape(local_blocks, block_rows, group_heads, head_size)
     upstream_heads = upstream.reshape(local_blocks, block_rows, group_heads, head_size)
-    scores = (
-        jnp.einsum("rtgh,uh->rgtu", query_heads, key_table, preferred_element_type=jnp.float32)
-        * score_scale
-    )
-    weights = jnp.where(allowed[:, None], jnp.exp(scores - lse_rows[:, :, :, None]), 0.0)
-    dweights = jnp.einsum(
-        "rtgh,uh->rgtu", upstream_heads, value_table, preferred_element_type=jnp.float32
-    )
-    dscores = weights * (dweights - deltas[:, :, :, None])
-    weights_low = weights.astype(jnp.bfloat16)
-    dscores_low = dscores.astype(jnp.bfloat16)
-    grad_q = jnp.einsum("rgtu,uh->rtgh", dscores_low, key_table, preferred_element_type=jnp.float32)
+
+    def attend(table, mask):
+        key_table = table[:, :head_size]
+        value_table = table[:, head_size:]
+        mask = mask.reshape(local_blocks, block_rows, -1)
+        scores = (
+            jnp.einsum(
+                "rtgh,uh->rgtu", query_heads, key_table, preferred_element_type=jnp.float32
+            )
+            * score_scale
+        )
+        weights = jnp.where(mask[:, None], jnp.exp(scores - lse_rows[:, :, :, None]), 0.0)
+        dweights = jnp.einsum(
+            "rtgh,uh->rgtu", upstream_heads, value_table, preferred_element_type=jnp.float32
+        )
+        dscores = weights * (dweights - deltas[:, :, :, None])
+        weights_low = weights.astype(jnp.bfloat16)
+        dscores_low = dscores.astype(jnp.bfloat16)
+        grad_q = jnp.einsum(
+            "rgtu,uh->rtgh", dscores_low, key_table, preferred_element_type=jnp.float32
+        )
+        key_part = (
+            jnp.einsum(
+                "rgtu,rtgh->uh", dscores_low, query_heads, preferred_element_type=jnp.float32
+            )
+            * score_scale
+        )
+        value_part = jnp.einsum(
+            "rgtu,rtgh->uh", weights_low, upstream_heads, preferred_element_type=jnp.float32
+        )
+        return grad_q, jnp.concatenate([key_part, value_part], axis=1).astype(jnp.bfloat16)
+
+    grad_local, partial_local = attend(local_table, allowed[:, :, :span])
+    grad_summary, summary_partial = attend(summary_table, allowed[:, :, span:])
+    grad_q = grad_local + grad_summary
     query_grads = (grad_q * score_scale).reshape(tokens, features).astype(jnp.bfloat16)
-    key_part = (
-        jnp.einsum("rgtu,rtgh->uh", dscores_low, query_heads, preferred_element_type=jnp.float32)
-        * score_scale
-    )
-    value_part = jnp.einsum(
-        "rgtu,rtgh->uh", weights_low, upstream_heads, preferred_element_type=jnp.float32
-    )
-    partial = jnp.concatenate([key_part, value_part], axis=1).astype(jnp.bfloat16)
+    partial = jnp.concatenate([partial_local, summary_partial], axis=0)
 
     totals = partial[(span - local_blocks) * block_rows : span * block_rows].astype(jnp.float32)
     offset = 0

time: 98.5 us -> 96.6 us (0.981)
  waiting for transfers between devices: 20.9 us -> 13.8 us
  matrix products: 13.8 us -> 17 us
  other arithmetic: 6.81 us -> 8.38 us
  starting transfers between devices: 49.5 us -> 50.7 us
    ppermute x4, waiting for transfers between devices: 11.1 us -> 6.71 us  [on_device(): lax.ppermute(outgoing, 'ctx', route).astype(jnp.float32)]
    dot_general x5 -> x10, matrix products: 13.8 us -> 17 us  [the longest x2 7.71 us: attend(): jnp.einsum('rtgh,uh->rgtu', query_heads, key_table, preferred_element_typ...]
    ppermute x4, waiting for transfers between devices: 9.78 us -> 7.04 us  [on_device(): owner_total = owner_total + lax.ppermute(gathered, 'ctx', route)]
    concatenate x2, other arithmetic: 0.91 us -> 2.22 us  [on_device(): arrived = from_behind(jnp.concatenate([piece, owned], axis=0), 'ctx', k)]
    ppermute x2, starting transfers between devices: 8.87 us -> 10.1 us  [on_device(): held = held + lax.ppermute(owned, 'ctx', route)]
    unnamed x15 -> x19, local copies, waits for them, and re-layouts: 2.39 us -> 1.66 us
  transfers between devices with their start and end apart: 19 -> 19, of which waited for: 7 -> 6; matrix products, arithmetic and copies ran while one was open for 13% -> 18% of each run, Pallas kernels for 0% -> 0%
where the time goes in v4:
time: 96.6 us; the launch traced here: 95.9 us
  starting transfers between devices  50.7 us (52%)
  matrix products  17 us (18%)
  waiting for transfers between devices  13.8 us (14%)
  other arithmetic  8.38 us (9%)
  local copies, waits for them, and re-layouts  4.67 us (5%)
  between operations  1.3 us (1%)
    ppermute x4, starting transfers between devices, on_device(): arrived = lax.ppermute(held, 'ctx', route)  17.3 us
    ppermute x5, starting transfers between devices, from_behind(): return lax.ppermute(block, axis, route)  13 us
    ppermute x2, starting transfers between devices, on_device(): held = held + lax.ppermute(owned, 'ctx', route)  10.1 us
    dot_general x2, matrix products, attend(): jnp.einsum('rtgh,uh->rgtu', query_heads, key_table, preferred_element_typ...  7.71 us
    ppermute x4, waiting for transfers between devices, on_device(): owner_total = owner_total + lax.ppermute(gathered, 'ctx', route)  7.04 us
    ppermute x4, waiting for transfers between devices, on_device(): lax.ppermute(outgoing, 'ctx', route).astype(jnp.float32)  6.71 us
    dot_general x2, matrix products, attend(): jnp.einsum('rtgh,uh->rgtu', upstream_heads, value_table, preferred_elemen...  5.35 us
    ppermute x4, starting transfers between devices, on_device(): owner_total = owner_total + lax.ppermute(gathered, 'ctx', route)  5.17 us
  transfers between devices with their start and end apart: 19, of which 6 were waited for; matrix products, arithmetic and copies ran while one was open for 18% of the time, Pallas kernels for 0%

profile of v4, /device:TPU:199, one launch (start us, length us, event | category | flops | bytes accessed | tf_op | source)
XLA Modules:
  0.0 95.9 jit_solution(14750723135847451506)
XLA Ops:
  1.5 8.2 %collective-permute-start.3 = (bf16[128,256]{1,0:T(8,128)(2,1)S(1)}, bf16[128,256]{1,0:T(8,128)(2,1)}, u32[]{:S(2)}, u32[]{:S(2)}) collective-permute-start(bf16[128,256]{1,0:T(8,128)(2,1)S(1)} %get-tuple-element.47), channel_id=1, source_target_pairs={{7,10},{15,18},{23,26},{39,42},{47,50},{55,58},{71,74},{79,82},{87... | collective-permute-start | bytes 196616 | tf_op jit(solution)/shard_map/ppermute | solution.py:76
  9.7 1.9 %collective-permute-start.4 = (bf16[128,256]{1,0:T(8,128)(2,1)S(1)}, bf16[128,256]{1,0:T(8,128)(2,1)}, u32[]{:S(2)}, u32[]{:S(2)}) collective-permute-start(bf16[128,256]{1,0:T(8,128)(2,1)S(1)} %get-tuple-element.47), channel_id=1, source_target_pairs={{7,11},{15,19},{23,27},{39,43},{47,51},{55,59},{71,75},{79,83},{87... | collective-permute-start | bytes 196616 | tf_op jit(solution)/shard_map/ppermute | solution.py:76
  12.3 1.9 %collective-permute-start = (bf16[256,256]{1,0:T(8,128)(2,1)}, bf16[256,256]{1,0:T(8,128)(2,1)S(1)}, u32[]{:S(2)}, u32[]{:S(2)}) collective-permute-start(bf16[256,256]{1,0:T(8,128)(2,1)} %pad_maximum_fusion.3), channel_id=1, source_target_pairs={{0,2},{1,3},{2,4},{3,5},{4,6},{5,7},{6,8},{7,9},{8,10},{9,11},{10,... | collective-permute-start | bytes 393224 | tf_op jit(solution)/shard_map/ppermute | solution.py:15
  14.2 1.6 %pad_maximum_fusion = bf16[384,256]{1,0:T(8,128)(2,1)} fusion(bf16[128,256]{1,0:T(8,128)(2,1)S(1)} %get-tuple-element.47, bf16[256,128]{1,0:T(8,128)(2,1)} %bitcast.171, bf16[256,128]{1,0:T(8,128)(2,1)} %bitcast.174), kind=kLoop, calls=%fused_computation.71 | loop fusion | flops 589824 | bytes 393216 | tf_op jit(solution)/shard_map/concatenate | solution.py:68
  15.7 1.9 %collective-permute-start.1 = (bf16[384,256]{1,0:T(8,128)(2,1)}, bf16[384,256]{1,0:T(8,128)(2,1)}, u32[]{:S(2)}, u32[]{:S(2)}) collective-permute-start(bf16[384,256]{1,0:T(8,128)(2,1)} %pad_maximum_fusion), channel_id=1, source_target_pairs={{0,1},{1,2},{2,3},{3,4},{4,5},{5,6},{6,7},{7,8},{8,9},{9,10},{10,1... | collective-permute-start | bytes 589832 | tf_op jit(solution)/shard_map/ppermute | solution.py:15
  17.7 5.4 %collective-permute-start.2 = (bf16[1,256,1024]{2,1,0:T(8,128)(2,1)}, bf16[1,256,1024]{2,1,0:T(8,128)(2,1)}, u32[]{:S(2)}, u32[]{:S(2)}) collective-permute-start(bf16[1,256,1024]{2,1,0:T(8,128)(2,1)} %param.21), channel_id=1, source_target_pairs={{32,0},{64,32},{96,64},{128,96},{160,128},{192,160},{224,192},{256... | collective-permute-start | bytes 1572872 | tf_op jit(solution)/shard_map/ppermute | solution.py:15
  26.9 10.9 %collective-permute-start.8 = (bf16[128,256]{1,0:T(8,128)(2,1)S(1)}, bf16[128,256]{1,0:T(8,128)(2,1)S(1)}, u32[]{:S(2)}, u32[]{:S(2)}) collective-permute-start(bf16[128,256]{1,0:T(8,128)(2,1)S(1)} %get-tuple-element.59), channel_id=1, source_target_pairs={{7,27},{8,28},{9,29},{10,30},{11,31},{39,59},{40,60},{41,61},{42,6... | collective-permute-start | bytes 196616 | tf_op jit(solution)/shard_map/ppermute | solution.py:81
  37.8 3.9 %collective-permute-start.7 = (bf16[128,256]{1,0:T(8,128)(2,1)S(1)}, bf16[128,256]{1,0:T(8,128)(2,1)S(1)}, u32[]{:S(2)}, u32[]{:S(2)}) collective-permute-start(bf16[128,256]{1,0:T(8,128)(2,1)S(1)} %get-tuple-element.59), channel_id=1, source_target_pairs={{7,22},{8,23},{9,24},{10,25},{11,26},{15,30},{16,31},{39,54},{40,5... | collective-permute-start | bytes 196616 | tf_op jit(solution)/shard_map/ppermute | solution.py:81
  41.6 1.3 %collective-permute-start.6 = (bf16[128,256]{1,0:T(8,128)(2,1)S(1)}, bf16[128,256]{1,0:T(8,128)(2,1)S(1)}, u32[]{:S(2)}, u32[]{:S(2)}) collective-permute-start(bf16[128,256]{1,0:T(8,128)(2,1)S(1)} %get-tuple-element.59), channel_id=1, source_target_pairs={{7,17},{8,18},{9,19},{10,20},{11,21},{15,25},{16,26},{17,27},{18,2... | collective-permute-start | bytes 196616 | tf_op jit(solution)/shard_map/ppermute | solution.py:81
  42.9 1.3 %collective-permute-start.5 = (bf16[128,256]{1,0:T(8,128)(2,1)S(1)}, bf16[128,256]{1,0:T(8,128)(2,1)S(1)}, u32[]{:S(2)}, u32[]{:S(2)}) collective-permute-start(bf16[128,256]{1,0:T(8,128)(2,1)S(1)} %get-tuple-element.59), channel_id=1, source_target_pairs={{7,12},{8,13},{9,14},{10,15},{11,16},{15,20},{16,21},{17,22},{18,2... | collective-permute-start | bytes 196616 | tf_op jit(solution)/shard_map/ppermute | solution.py:81
  45.2 4.7 %fusion.4 = (bf16[2,8,128,640]{2,3,1,0:T(8,128)(2,1)}, f32[640,2,128,8]{2,0,3,1:T(8,128)}) fusion(f32[2,8,128]{2,1,0:T(8,128)S(1)} %bitcast.182, pred[2,128,640]{1,2,0:T(8,128)(4,1)S(1)} %bitcast.168, bf16[2,128,8,128]{3,2,1,0:T(8,128)(2,1)S(1)} %bitcast.159, bf16[640,256]{1,0:T(8,128)(2,1)S(1)} %maximum_maximum_fusion), kind=kOutput, calls=%fused_computation.6 | convolution fusion | flops 340787200 | bytes 8724480 | tf_op jit(solution)/shard_map/rtgh,uh->rgtu/dot_general | solution.py:113
  50.1 3.0 %fusion.7 = (bf16[384,8,2,128]{3,0,1,2:T(8,128)(2,1)}, f32[384,2,128,8]{2,0,3,1:T(8,128)}) fusion(f32[8,2,128]{2,0,1:T(8,128)S(1)} %bitcast.183, pred[384,2,128]{2,0,1:T(8,128)(4,1)S(1)} %bitcast.180, bf16[2,128,8,128]{3,2,1,0:T(8,128)(2,1)S(1)} %bitcast.160, bf16[384,256]{1,0:T(8,128)(2,1)S(1)} %bitcast.165), kind=kOutput, calls=%fused_computation.10 | convolution fusion | flops 204472320 | bytes 5447680 | tf_op jit(solution)/shard_map/rtgh,uh->rgtu/dot_general | solution.py:113
  54.9 4.2 %fusion.1 = bf16[2,8,128,640]{2,3,1,0:T(8,128)(2,1)S(1)} fusion(f32[640,2,128,8]{2,0,3,1:T(8,128)} %get-tuple-element.62, f32[2,8,128]{2,1,0:T(8,128)S(1)} %copy.74, f32[2,8,128]{2,1,0:T(8,128)S(1)} %bitcast.184, pred[2,128,640]{1,2,0:T(8,128)(4,1)S(1)} %bitcast.169, bf16[2,128,8,128]{3,2,1,0:T(8,128)(2,1)S(1)} %bitcast.155, ...), kind=kOutput, calls=%fused_computation.2 | convolution fusion | flops 343408640 | bytes 8732672 | tf_op jit(solution)/shard_map/rtgh,uh->rgtu/dot_general | solution.py:119
  64.2 1.3 %collective-permute-start.11 = (bf16[128,256]{1,0:T(8,128)(2,1)S(1)}, bf16[128,256]{1,0:T(8,128)(2,1)S(1)}, u32[]{:S(2)}, u32[]{:S(2)}) collective-permute-start(bf16[128,256]{1,0:T(8,128)(2,1)S(1)} %get-tuple-element.53), channel_id=1, source_target_pairs={{12,7},{13,8},{14,9},{15,10},{16,11},{20,15},{21,16},{22,17},{23,1... | collective-permute-start | bytes 196616 | tf_op jit(solution)/shard_map/ppermute | solution.py:163
  65.5 1.3 %collective-permute-start.12 = (bf16[128,256]{1,0:T(8,128)(2,1)S(1)}, bf16[128,256]{1,0:T(8,128)(2,1)S(1)}, u32[]{:S(2)}, u32[]{:S(2)}) collective-permute-start(bf16[128,256]{1,0:T(8,128)(2,1)S(1)} %get-tuple-element.54), channel_id=1, source_target_pairs={{17,7},{18,8},{19,9},{20,10},{21,11},{25,15},{26,16},{27,17},{28,1... | collective-permute-start | bytes 196616 | tf_op jit(solution)/shard_map/ppermute | solution.py:163
  66.8 1.3 %collective-permute-start.13 = (bf16[128,256]{1,0:T(8,128)(2,1)S(1)}, bf16[128,256]{1,0:T(8,128)(2,1)S(1)}, u32[]{:S(2)}, u32[]{:S(2)}) collective-permute-start(bf16[128,256]{1,0:T(8,128)(2,1)S(1)} %get-tuple-element.55), channel_id=1, source_target_pairs={{22,7},{23,8},{24,9},{25,10},{26,11},{30,15},{31,16},{54,39},{55,4... | collective-permute-start | bytes 196616 | tf_op jit(solution)/shard_map/ppermute | solution.py:163
  72.1 1.9 %collective-permute-start.9 = (bf16[128,256]{1,0:T(8,128)(2,1)S(1)}, bf16[128,256]{1,0:T(8,128)(2,1)S(1)}, u32[]{:S(2)}, u32[]{:S(2)}) collective-permute-start(bf16[128,256]{1,0:T(8,128)(2,1)S(1)} %fusion.83), channel_id=1, source_target_pairs={{2,0},{3,1},{4,2},{5,3},{6,4},{7,5},{8,6},{9,7},{10,8},{11,9},{12,... | collective-permute-start | bytes 196616 | tf_op jit(solution)/shard_map/ppermute | solution.py:15
  74.1 1.9 %collective-permute-start.10 = (bf16[256,256]{1,0:T(8,128)(2,1)S(1)}, bf16[256,256]{1,0:T(8,128)(2,1)S(1)}, u32[]{:S(2)}, u32[]{:S(2)}) collective-permute-start(bf16[256,256]{1,0:T(8,128)(2,1)S(1)} %get-tuple-element.49), channel_id=1, source_target_pairs={{1,0},{2,1},{3,2},{4,3},{5,4},{6,5},{7,6},{8,7},{9,8},{10,9},{11,1... | collective-permute-start | bytes 393224 | tf_op jit(solution)/shard_map/ppermute | solution.py:15
  76.0 1.3 %collective-permute-done.12 = bf16[128,256]{1,0:T(8,128)(2,1)S(1)} collective-permute-done((bf16[128,256]{1,0:T(8,128)(2,1)S(1)}, bf16[128,256]{1,0:T(8,128)(2,1)S(1)}, u32[]{:S(2)}, u32[]{:S(2)}) %collective-permute-start.12) | collective-permute-done | bytes 65568 | tf_op jit(solution)/shard_map/ppermute | solution.py:163
  77.3 5.4 %collective-permute-done.13 = bf16[128,256]{1,0:T(8,128)(2,1)S(1)} collective-permute-done((bf16[128,256]{1,0:T(8,128)(2,1)S(1)}, bf16[128,256]{1,0:T(8,128)(2,1)S(1)}, u32[]{:S(2)}, u32[]{:S(2)}) %collective-permute-start.13) | collective-permute-done | bytes 65568 | tf_op jit(solution)/shard_map/ppermute | solution.py:163
  86.7 1.3 %collective-permute-start.15 = (f32[128,256]{1,0:T(8,128)S(1)}, f32[128,256]{1,0:T(8,128)S(1)}, u32[]{:S(2)}, u32[]{:S(2)}) collective-permute-start(f32[128,256]{1,0:T(8,128)S(1)} %fusion.71), channel_id=1, source_target_pairs={{8,7},{16,15},{24,23},{40,39},{48,47},{56,55},{72,71},{80,79},{88,... | collective-permute-start | bytes 393224 | tf_op jit(solution)/shard_map/ppermute | solution.py:167
  88.0 2.5 %collective-permute-done.18 = f32[128,256]{1,0:T(8,128)S(1)} collective-permute-done((f32[128,256]{1,0:T(8,128)S(1)}, f32[128,256]{1,0:T(8,128)S(1)}, u32[]{:S(2)}, u32[]{:S(2)}) %collective-permute-start.18) | collective-permute-done | bytes 131104 | tf_op jit(solution)/shard_map/ppermute | solution.py:167
  90.6 2.0 %collective-permute-done.17 = f32[128,256]{1,0:T(8,128)S(1)} collective-permute-done((f32[128,256]{1,0:T(8,128)S(1)}, f32[128,256]{1,0:T(8,128)S(1)}, u32[]{:S(2)}, u32[]{:S(2)}) %collective-permute-start.17) | collective-permute-done | bytes 131104 | tf_op jit(solution)/shard_map/ppermute | solution.py:167
  92.6 2.1 %collective-permute-done.16 = f32[128,256]{1,0:T(8,128)S(1)} collective-permute-done((f32[128,256]{1,0:T(8,128)S(1)}, f32[128,256]{1,0:T(8,128)S(1)}, u32[]{:S(2)}, u32[]{:S(2)}) %collective-permute-start.16) | collective-permute-done | bytes 131104 | tf_op jit(solution)/shard_map/ppermute | solution.py:167
  (79 shorter events, 22.2 us)
Async XLA Ops:
  0.6 25.0 %copy-start.6 = (bf16[1,256,1024]{2,1,0:T(8,128)(2,1)S(1)}, bf16[1,256,1024]{2,1,0:T(8,128)(2,1)}, u32[]{:S(2)}) copy-start(bf16[1,256,1024]{2,1,0:T(8,128)(2,1)} %param.16) | copy-start | bytes 1572868
  1.5 24.4 %collective-permute-start.3 = (bf16[128,256]{1,0:T(8,128)(2,1)S(1)}, bf16[128,256]{1,0:T(8,128)(2,1)}, u32[]{:S(2)}, u32[]{:S(2)}) collective-permute-start(bf16[128,256]{1,0:T(8,128)(2,1)S(1)} %get-tuple-element.47), channel_id=1, source_target_pairs={{7,10},{15,18},{23,26},{39,42},{47,50},{55,58},{71,74},{79,82},{87... | collective-permute-start | bytes 196616 | tf_op jit(solution)/shard_map/ppermute | solution.py:76
  9.7 16.3 %collective-permute-start.4 = (bf16[128,256]{1,0:T(8,128)(2,1)S(1)}, bf16[128,256]{1,0:T(8,128)(2,1)}, u32[]{:S(2)}, u32[]{:S(2)}) collective-permute-start(bf16[128,256]{1,0:T(8,128)(2,1)S(1)} %get-tuple-element.47), channel_id=1, source_target_pairs={{7,11},{15,19},{23,27},{39,43},{47,51},{55,59},{71,75},{79,83},{87... | collective-permute-start | bytes 196616 | tf_op jit(solution)/shard_map/ppermute | solution.py:76
  12.3 13.7 %collective-permute-start = (bf16[256,256]{1,0:T(8,128)(2,1)}, bf16[256,256]{1,0:T(8,128)(2,1)S(1)}, u32[]{:S(2)}, u32[]{:S(2)}) collective-permute-start(bf16[256,256]{1,0:T(8,128)(2,1)} %pad_maximum_fusion.3), channel_id=1, source_target_pairs={{0,2},{1,3},{2,4},{3,5},{4,6},{5,7},{6,8},{7,9},{8,10},{9,11},{10,... | collective-permute-start | bytes 393224 | tf_op jit(solution)/shard_map/ppermute | solution.py:15
  15.7 10.2 %collective-permute-start.1 = (bf16[384,256]{1,0:T(8,128)(2,1)}, bf16[384,256]{1,0:T(8,128)(2,1)}, u32[]{:S(2)}, u32[]{:S(2)}) collective-permute-start(bf16[384,256]{1,0:T(8,128)(2,1)} %pad_maximum_fusion), channel_id=1, source_target_pairs={{0,1},{1,2},{2,3},{3,4},{4,5},{5,6},{6,7},{7,8},{8,9},{9,10},{10,1... | collective-permute-start | bytes 589832 | tf_op jit(solution)/shard_map/ppermute | solution.py:15
  17.7 35.5 %collective-permute-start.2 = (bf16[1,256,1024]{2,1,0:T(8,128)(2,1)}, bf16[1,256,1024]{2,1,0:T(8,128)(2,1)}, u32[]{:S(2)}, u32[]{:S(2)}) collective-permute-start(bf16[1,256,1024]{2,1,0:T(8,128)(2,1)} %param.21), channel_id=1, source_target_pairs={{32,0},{64,32},{96,64},{128,96},{160,128},{192,160},{224,192},{256... | collective-permute-start | bytes 1572872 | tf_op jit(solution)/shard_map/ppermute | solution.py:15
  23.9 21.3 %copy-start.3 = (bf16[1,256,128]{2,1,0:T(8,128)(2,1)S(1)}, bf16[1,256,128]{2,1,0:T(8,128)(2,1)}, u32[]{:S(2)}) copy-start(bf16[1,256,128]{2,1,0:T(8,128)(2,1)} %param.18) | copy-start | bytes 196612
  23.9 21.3 %copy-start.4 = (bf16[1,256,128]{2,1,0:T(8,128)(2,1)S(1)}, bf16[1,256,128]{2,1,0:T(8,128)(2,1)}, u32[]{:S(2)}) copy-start(bf16[1,256,128]{2,1,0:T(8,128)(2,1)} %param.17) | copy-start | bytes 196612
  25.1 20.1 %copy-start.7 = (f32[1,8,256]{2,1,0:T(8,128)S(1)}, f32[1,8,256]{2,1,0:T(8,128)}, u32[]{:S(2)}) copy-start(f32[1,8,256]{2,1,0:T(8,128)} %param.22) | copy-start | bytes 24580
  26.9 23.0 %collective-permute-start.8 = (bf16[128,256]{1,0:T(8,128)(2,1)S(1)}, bf16[128,256]{1,0:T(8,128)(2,1)S(1)}, u32[]{:S(2)}, u32[]{:S(2)}) collective-permute-start(bf16[128,256]{1,0:T(8,128)(2,1)S(1)} %get-tuple-element.59), channel_id=1, source_target_pairs={{7,27},{8,28},{9,29},{10,30},{11,31},{39,59},{40,60},{41,61},{42,6... | collective-permute-start | bytes 196616 | tf_op jit(solution)/shard_map/ppermute | solution.py:81
  37.8 12.1 %collective-permute-start.7 = (bf16[128,256]{1,0:T(8,128)(2,1)S(1)}, bf16[128,256]{1,0:T(8,128)(2,1)S(1)}, u32[]{:S(2)}, u32[]{:S(2)}) collective-permute-start(bf16[128,256]{1,0:T(8,128)(2,1)S(1)} %get-tuple-element.59), channel_id=1, source_target_pairs={{7,22},{8,23},{9,24},{10,25},{11,26},{15,30},{16,31},{39,54},{40,5... | collective-permute-start | bytes 196616 | tf_op jit(solution)/shard_map/ppermute | solution.py:81
  41.6 8.3 %collective-permute-start.6 = (bf16[128,256]{1,0:T(8,128)(2,1)S(1)}, bf16[128,256]{1,0:T(8,128)(2,1)S(1)}, u32[]{:S(2)}, u32[]{:S(2)}) collective-permute-start(bf16[128,256]{1,0:T(8,128)(2,1)S(1)} %get-tuple-element.59), channel_id=1, source_target_pairs={{7,17},{8,18},{9,19},{10,20},{11,21},{15,25},{16,26},{17,27},{18,2... | collective-permute-start | bytes 196616 | tf_op jit(solution)/shard_map/ppermute | solution.py:81
  42.9 7.0 %collective-permute-start.5 = (bf16[128,256]{1,0:T(8,128)(2,1)S(1)}, bf16[128,256]{1,0:T(8,128)(2,1)S(1)}, u32[]{:S(2)}, u32[]{:S(2)}) collective-permute-start(bf16[128,256]{1,0:T(8,128)(2,1)S(1)} %get-tuple-element.59), channel_id=1, source_target_pairs={{7,12},{8,13},{9,14},{10,15},{11,16},{15,20},{16,21},{17,22},{18,2... | collective-permute-start | bytes 196616 | tf_op jit(solution)/shard_map/ppermute | solution.py:81
  63.0 6.4 %copy-start.1 = (bf16[2,8,128,640]{2,3,1,0:T(8,128)(2,1)S(1)}, bf16[2,8,128,640]{2,3,1,0:T(8,128)(2,1)}, u32[]{:S(2)}) copy-start(bf16[2,8,128,640]{2,3,1,0:T(8,128)(2,1)} %get-tuple-element.61) | copy-start | bytes 7864324
  64.2 9.9 %collective-permute-start.11 = (bf16[128,256]{1,0:T(8,128)(2,1)S(1)}, bf16[128,256]{1,0:T(8,128)(2,1)S(1)}, u32[]{:S(2)}, u32[]{:S(2)}) collective-permute-start(bf16[128,256]{1,0:T(8,128)(2,1)S(1)} %get-tuple-element.53), channel_id=1, source_target_pairs={{12,7},{13,8},{14,9},{15,10},{16,11},{20,15},{21,16},{22,17},{23,1... | collective-permute-start | bytes 196616 | tf_op jit(solution)/shard_map/ppermute | solution.py:163
  65.5 11.8 %collective-permute-start.12 = (bf16[128,256]{1,0:T(8,128)(2,1)S(1)}, bf16[128,256]{1,0:T(8,128)(2,1)S(1)}, u32[]{:S(2)}, u32[]{:S(2)}) collective-permute-start(bf16[128,256]{1,0:T(8,128)(2,1)S(1)} %get-tuple-element.54), channel_id=1, source_target_pairs={{17,7},{18,8},{19,9},{20,10},{21,11},{25,15},{26,16},{27,17},{28,1... | collective-permute-start | bytes 196616 | tf_op jit(solution)/shard_map/ppermute | solution.py:163
  66.8 15.9 %collective-permute-start.13 = (bf16[128,256]{1,0:T(8,128)(2,1)S(1)}, bf16[128,256]{1,0:T(8,128)(2,1)S(1)}, u32[]{:S(2)}, u32[]{:S(2)}) collective-permute-start(bf16[128,256]{1,0:T(8,128)(2,1)S(1)} %get-tuple-element.55), channel_id=1, source_target_pairs={{22,7},{23,8},{24,9},{25,10},{26,11},{30,15},{31,16},{54,39},{55,4... | collective-permute-start | bytes 196616 | tf_op jit(solution)/shard_map/ppermute | solution.py:163
  68.1 14.6 %collective-permute-start.14 = (bf16[128,256]{1,0:T(8,128)(2,1)S(1)}, bf16[128,256]{1,0:T(8,128)(2,1)S(1)}, u32[]{:S(2)}, u32[]{:S(2)}) collective-permute-start(bf16[128,256]{1,0:T(8,128)(2,1)S(1)} %get-tuple-element.56), channel_id=1, source_target_pairs={{27,7},{28,8},{29,9},{30,10},{31,11},{59,39},{60,40},{61,41},{62,4... | collective-permute-start | bytes 196616 | tf_op jit(solution)/shard_map/ppermute | solution.py:163
  72.1 14.6 %collective-permute-start.9 = (bf16[128,256]{1,0:T(8,128)(2,1)S(1)}, bf16[128,256]{1,0:T(8,128)(2,1)S(1)}, u32[]{:S(2)}, u32[]{:S(2)}) collective-permute-start(bf16[128,256]{1,0:T(8,128)(2,1)S(1)} %fusion.83), channel_id=1, source_target_pairs={{2,0},{3,1},{4,2},{5,3},{6,4},{7,5},{8,6},{9,7},{10,8},{11,9},{12,... | collective-permute-start | bytes 196616 | tf_op jit(solution)/shard_map/ppermute | solution.py:15
  74.1 13.9 %collective-permute-start.10 = (bf16[256,256]{1,0:T(8,128)(2,1)S(1)}, bf16[256,256]{1,0:T(8,128)(2,1)S(1)}, u32[]{:S(2)}, u32[]{:S(2)}) collective-permute-start(bf16[256,256]{1,0:T(8,128)(2,1)S(1)} %get-tuple-element.49), channel_id=1, source_target_pairs={{1,0},{2,1},{3,2},{4,3},{5,4},{6,5},{7,6},{8,7},{9,8},{10,9},{11,1... | collective-permute-start | bytes 393224 | tf_op jit(solution)/shard_map/ppermute | solution.py:15
  82.8 7.8 %collective-permute-start.18 = (f32[128,256]{1,0:T(8,128)S(1)}, f32[128,256]{1,0:T(8,128)S(1)}, u32[]{:S(2)}, u32[]{:S(2)}) collective-permute-start(f32[128,256]{1,0:T(8,128)S(1)} %fusion.71), channel_id=1, source_target_pairs={{11,7},{19,15},{27,23},{43,39},{51,47},{59,55},{75,71},{83,79},{91... | collective-permute-start | bytes 393224 | tf_op jit(solution)/shard_map/ppermute | solution.py:167
  84.1 8.5 %collective-permute-start.17 = (f32[128,256]{1,0:T(8,128)S(1)}, f32[128,256]{1,0:T(8,128)S(1)}, u32[]{:S(2)}, u32[]{:S(2)}) collective-permute-start(f32[128,256]{1,0:T(8,128)S(1)} %fusion.71), channel_id=1, source_target_pairs={{10,7},{18,15},{26,23},{42,39},{50,47},{58,55},{74,71},{82,79},{90... | collective-permute-start | bytes 393224 | tf_op jit(solution)/shard_map/ppermute | solution.py:167
  85.4 9.2 %collective-permute-start.16 = (f32[128,256]{1,0:T(8,128)S(1)}, f32[128,256]{1,0:T(8,128)S(1)}, u32[]{:S(2)}, u32[]{:S(2)}) collective-permute-start(f32[128,256]{1,0:T(8,128)S(1)} %fusion.71), channel_id=1, source_target_pairs={{9,7},{17,15},{25,23},{41,39},{49,47},{57,55},{73,71},{81,79},{89,... | collective-permute-start | bytes 393224 | tf_op jit(solution)/shard_map/ppermute | solution.py:167
  86.7 8.4 %collective-permute-start.15 = (f32[128,256]{1,0:T(8,128)S(1)}, f32[128,256]{1,0:T(8,128)S(1)}, u32[]{:S(2)}, u32[]{:S(2)}) collective-permute-start(f32[128,256]{1,0:T(8,128)S(1)} %fusion.71), channel_id=1, source_target_pairs={{8,7},{16,15},{24,23},{40,39},{48,47},{56,55},{72,71},{80,79},{88,... | collective-permute-start | bytes 393224 | tf_op jit(solution)/shard_map/ppermute | solution.py:167
  (3 other events, 6.7 us)

commit v5 on v4

--- a/solution.py
+++ b/solution.py
@@ -143,12 +143,6 @@
     partial = jnp.concatenate([partial_local, summary_partial], axis=0)
 
     totals = partial[(span - local_blocks) * block_rows : span * block_rows].astype(jnp.float32)
-    offset = 0
-    for k in range(behind, 0, -1):
-        size = counts[k - 1] * block_rows
-        returned = from_behind(partial[offset : offset + size], "ctx", -k).astype(jnp.float32)
-        totals = totals.at[tokens - size :].add(returned)
-        offset += size
     summary_low = partial[span * block_rows :].reshape(n_summary, block_rows, -1)
 
     def slot_at(position):
@@ -162,7 +156,19 @@
         outgoing = lax.dynamic_index_in_dim(summary_low, slot_at(device - shift), 0, keepdims=False)
         gathered = gathered + lax.ppermute(outgoing, "ctx", route).astype(jnp.float32)
     owner_total = gathered
-    for shift in range(1, radix):
+    offset = 0
+    for k in range(behind, 0, -1):
+        size = counts[k - 1] * block_rows
+        piece = partial[offset : offset + size].astype(jnp.float32)
+        if k < radix:
+            returned = from_behind(jnp.concatenate([piece, gathered], axis=0), "ctx", -k)
+            owner_total = owner_total + returned[size:]
+            returned = returned[:size]
+        else:
+            returned = from_behind(piece, "ctx", -k)
+        totals = totals.at[tokens - size :].add(returned)
+        offset += size
+    for shift in range(behind + 1, radix):
         route = [(o + shift, o) for o in owners if o + shift < ctx_count]
         owner_total = owner_total + lax.ppermute(gathered, "ctx", route)
     start = ((stride - 1) % local_blocks) * block_rows

time: 96.6 us -> 102 us (1.056)
  waiting for transfers between devices: 13.8 us -> 21.9 us
  starting transfers between devices: 50.7 us -> 48.1 us
    ppermute x4, waiting for transfers between devices: 6.71 us -> 12.4 us  [on_device(): lax.ppermute(outgoing, 'ctx', route).astype(jnp.float32)]
    ppermute x5, waiting for transfers between devices: 0.01 us -> 4.71 us  [from_behind(): return lax.ppermute(block, axis, route)]
    ppermute x4 -> x2, starting transfers between devices: 5.17 us -> 2.57 us  [on_device(): owner_total = owner_total + lax.ppermute(gathered, 'ctx', route)]
    ppermute x4 -> x2, waiting for transfers between devices: 7.04 us -> 4.85 us  [on_device(): owner_total = owner_total + lax.ppermute(gathered, 'ctx', route)]
  transfers between devices with their start and end apart: 19 -> 17, of which waited for: 6 -> 7; matrix products, arithmetic and copies ran while one was open for 18% -> 17% of each run, Pallas kernels for 0% -> 0%
where the time goes in v5:
time: 102 us; the launch traced here: 101 us
  starting transfers between devices  48.1 us (47%)
  waiting for transfers between devices  21.9 us (21%)
  matrix products  17 us (17%)
  other arithmetic  8.44 us (8%)
  local copies, waits for them, and re-layouts  4.67 us (5%)
  between operations  1.28 us (1%)
    ppermute x4, starting transfers between devices, on_device(): arrived = lax.ppermute(held, 'ctx', route)  17.3 us
    ppermute x5, starting transfers between devices, from_behind(): return lax.ppermute(block, axis, route)  13 us
    ppermute x4, waiting for transfers between devices, on_device(): lax.ppermute(outgoing, 'ctx', route).astype(jnp.float32)  12.4 us
    ppermute x2, starting transfers between devices, on_device(): held = held + lax.ppermute(owned, 'ctx', route)  10.1 us
    dot_general x2, matrix products, attend(): jnp.einsum('rtgh,uh->rgtu', query_heads, key_table, preferred_element_typ...  7.75 us
    dot_general x2, matrix products, attend(): jnp.einsum('rtgh,uh->rgtu', upstream_heads, value_table, preferred_elemen...  5.34 us
    ppermute x4, starting transfers between devices, on_device(): lax.ppermute(outgoing, 'ctx', route).astype(jnp.float32)  5.17 us
    ppermute x2, waiting for transfers between devices, on_device(): owner_total = owner_total + lax.ppermute(gathered, 'ctx', route)  4.85 us
  transfers between devices with their start and end apart: 17, of which 7 were waited for; matrix products, arithmetic and copies ran while one was open for 17% of the time, Pallas kernels for 0%

profile of v5, /device:TPU:199, one launch (start us, length us, event | category | flops | bytes accessed | tf_op | source)
XLA Modules:
  0.0 101.5 jit_solution(8290880764271917939)
XLA Ops:
  1.5 8.2 %collective-permute-start.3 = (bf16[128,256]{1,0:T(8,128)(2,1)S(1)}, bf16[128,256]{1,0:T(8,128)(2,1)}, u32[]{:S(2)}, u32[]{:S(2)}) collective-permute-start(bf16[128,256]{1,0:T(8,128)(2,1)S(1)} %get-tuple-element.47), channel_id=1, source_target_pairs={{7,10},{15,18},{23,26},{39,42},{47,50},{55,58},{71,74},{79,82},{87... | collective-permute-start | bytes 196616 | tf_op jit(solution)/shard_map/ppermute | solution.py:76
  9.7 1.9 %collective-permute-start.4 = (bf16[128,256]{1,0:T(8,128)(2,1)S(1)}, bf16[128,256]{1,0:T(8,128)(2,1)}, u32[]{:S(2)}, u32[]{:S(2)}) collective-permute-start(bf16[128,256]{1,0:T(8,128)(2,1)S(1)} %get-tuple-element.47), channel_id=1, source_target_pairs={{7,11},{15,19},{23,27},{39,43},{47,51},{55,59},{71,75},{79,83},{87... | collective-permute-start | bytes 196616 | tf_op jit(solution)/shard_map/ppermute | solution.py:76
  12.2 1.9 %collective-permute-start = (bf16[256,256]{1,0:T(8,128)(2,1)}, bf16[256,256]{1,0:T(8,128)(2,1)S(1)}, u32[]{:S(2)}, u32[]{:S(2)}) collective-permute-start(bf16[256,256]{1,0:T(8,128)(2,1)} %pad_maximum_fusion.5), channel_id=1, source_target_pairs={{0,2},{1,3},{2,4},{3,5},{4,6},{5,7},{6,8},{7,9},{8,10},{9,11},{10,... | collective-permute-start | bytes 393224 | tf_op jit(solution)/shard_map/ppermute | solution.py:15
  14.2 1.6 %pad_maximum_fusion.2 = bf16[384,256]{1,0:T(8,128)(2,1)} fusion(bf16[128,256]{1,0:T(8,128)(2,1)S(1)} %get-tuple-element.47, bf16[256,128]{1,0:T(8,128)(2,1)} %bitcast.171, bf16[256,128]{1,0:T(8,128)(2,1)} %bitcast.174), kind=kLoop, calls=%fused_computation.73 | loop fusion | flops 589824 | bytes 393216 | tf_op jit(solution)/shard_map/concatenate | solution.py:68
  15.7 1.9 %collective-permute-start.1 = (bf16[384,256]{1,0:T(8,128)(2,1)}, bf16[384,256]{1,0:T(8,128)(2,1)}, u32[]{:S(2)}, u32[]{:S(2)}) collective-permute-start(bf16[384,256]{1,0:T(8,128)(2,1)} %pad_maximum_fusion.2), channel_id=1, source_target_pairs={{0,1},{1,2},{2,3},{3,4},{4,5},{5,6},{6,7},{7,8},{8,9},{9,10},{10,1... | collective-permute-start | bytes 589832 | tf_op jit(solution)/shard_map/ppermute | solution.py:15
  17.7 5.4 %collective-permute-start.2 = (bf16[1,256,1024]{2,1,0:T(8,128)(2,1)}, bf16[1,256,1024]{2,1,0:T(8,128)(2,1)}, u32[]{:S(2)}, u32[]{:S(2)}) collective-permute-start(bf16[1,256,1024]{2,1,0:T(8,128)(2,1)} %param.21), channel_id=1, source_target_pairs={{32,0},{64,32},{96,64},{128,96},{160,128},{192,160},{224,192},{256... | collective-permute-start | bytes 1572872 | tf_op jit(solution)/shard_map/ppermute | solution.py:15
  26.9 10.9 %collective-permute-start.8 = (bf16[128,256]{1,0:T(8,128)(2,1)S(1)}, bf16[128,256]{1,0:T(8,128)(2,1)S(1)}, u32[]{:S(2)}, u32[]{:S(2)}) collective-permute-start(bf16[128,256]{1,0:T(8,128)(2,1)S(1)} %get-tuple-element.59), channel_id=1, source_target_pairs={{7,27},{8,28},{9,29},{10,30},{11,31},{39,59},{40,60},{41,61},{42,6... | collective-permute-start | bytes 196616 | tf_op jit(solution)/shard_map/ppermute | solution.py:81
  37.8 3.9 %collective-permute-start.7 = (bf16[128,256]{1,0:T(8,128)(2,1)S(1)}, bf16[128,256]{1,0:T(8,128)(2,1)S(1)}, u32[]{:S(2)}, u32[]{:S(2)}) collective-permute-start(bf16[128,256]{1,0:T(8,128)(2,1)S(1)} %get-tuple-element.59), channel_id=1, source_target_pairs={{7,22},{8,23},{9,24},{10,25},{11,26},{15,30},{16,31},{39,54},{40,5... | collective-permute-start | bytes 196616 | tf_op jit(solution)/shard_map/ppermute | solution.py:81
  41.6 1.3 %collective-permute-start.6 = (bf16[128,256]{1,0:T(8,128)(2,1)S(1)}, bf16[128,256]{1,0:T(8,128)(2,1)S(1)}, u32[]{:S(2)}, u32[]{:S(2)}) collective-permute-start(bf16[128,256]{1,0:T(8,128)(2,1)S(1)} %get-tuple-element.59), channel_id=1, source_target_pairs={{7,17},{8,18},{9,19},{10,20},{11,21},{15,25},{16,26},{17,27},{18,2... | collective-permute-start | bytes 196616 | tf_op jit(solution)/shard_map/ppermute | solution.py:81
  42.9 1.3 %collective-permute-start.5 = (bf16[128,256]{1,0:T(8,128)(2,1)S(1)}, bf16[128,256]{1,0:T(8,128)(2,1)S(1)}, u32[]{:S(2)}, u32[]{:S(2)}) collective-permute-start(bf16[128,256]{1,0:T(8,128)(2,1)S(1)} %get-tuple-element.59), channel_id=1, source_target_pairs={{7,12},{8,13},{9,14},{10,15},{11,16},{15,20},{16,21},{17,22},{18,2... | collective-permute-start | bytes 196616 | tf_op jit(solution)/shard_map/ppermute | solution.py:81
  45.2 4.7 %fusion.4 = (bf16[2,8,128,640]{2,3,1,0:T(8,128)(2,1)}, f32[640,2,128,8]{2,0,3,1:T(8,128)}) fusion(f32[2,8,128]{2,1,0:T(8,128)S(1)} %bitcast.182, pred[2,128,640]{1,2,0:T(8,128)(4,1)S(1)} %bitcast.168, bf16[2,128,8,128]{3,2,1,0:T(8,128)(2,1)S(1)} %bitcast.159, bf16[640,256]{1,0:T(8,128)(2,1)S(1)} %maximum_maximum_fusion), kind=kOutput, calls=%fused_computation.6 | convolution fusion | flops 340787200 | bytes 8724480 | tf_op jit(solution)/shard_map/rtgh,uh->rgtu/dot_general | solution.py:113
  50.1 3.0 %fusion.7 = (bf16[384,8,2,128]{3,0,1,2:T(8,128)(2,1)}, f32[384,2,128,8]{2,0,3,1:T(8,128)}) fusion(f32[8,2,128]{2,0,1:T(8,128)S(1)} %bitcast.183, pred[384,2,128]{2,0,1:T(8,128)(4,1)S(1)} %bitcast.180, bf16[2,128,8,128]{3,2,1,0:T(8,128)(2,1)S(1)} %bitcast.160, bf16[384,256]{1,0:T(8,128)(2,1)S(1)} %bitcast.165), kind=kOutput, calls=%fused_computation.10 | convolution fusion | flops 204472320 | bytes 5447680 | tf_op jit(solution)/shard_map/rtgh,uh->rgtu/dot_general | solution.py:113
  54.9 4.2 %fusion.1 = bf16[2,8,128,640]{2,3,1,0:T(8,128)(2,1)S(1)} fusion(f32[640,2,128,8]{2,0,3,1:T(8,128)} %get-tuple-element.62, f32[2,8,128]{2,1,0:T(8,128)S(1)} %copy.74, f32[2,8,128]{2,1,0:T(8,128)S(1)} %bitcast.184, pred[2,128,640]{1,2,0:T(8,128)(4,1)S(1)} %bitcast.169, bf16[2,128,8,128]{3,2,1,0:T(8,128)(2,1)S(1)} %bitcast.155, ...), kind=kOutput, calls=%fused_computation.2 | convolution fusion | flops 343408640 | bytes 8732672 | tf_op jit(solution)/shard_map/rtgh,uh->rgtu/dot_general | solution.py:119
  64.2 1.3 %collective-permute-start.9 = (bf16[128,256]{1,0:T(8,128)(2,1)S(1)}, bf16[128,256]{1,0:T(8,128)(2,1)S(1)}, u32[]{:S(2)}, u32[]{:S(2)}) collective-permute-start(bf16[128,256]{1,0:T(8,128)(2,1)S(1)} %get-tuple-element.53), channel_id=1, source_target_pairs={{12,7},{13,8},{14,9},{15,10},{16,11},{20,15},{21,16},{22,17},{23,1... | collective-permute-start | bytes 196616 | tf_op jit(solution)/shard_map/ppermute | solution.py:157
  65.5 1.3 %collective-permute-start.10 = (bf16[128,256]{1,0:T(8,128)(2,1)S(1)}, bf16[128,256]{1,0:T(8,128)(2,1)S(1)}, u32[]{:S(2)}, u32[]{:S(2)}) collective-permute-start(bf16[128,256]{1,0:T(8,128)(2,1)S(1)} %get-tuple-element.54), channel_id=1, source_target_pairs={{17,7},{18,8},{19,9},{20,10},{21,11},{25,15},{26,16},{27,17},{28,1... | collective-permute-start | bytes 196616 | tf_op jit(solution)/shard_map/ppermute | solution.py:157
  66.8 1.3 %collective-permute-start.11 = (bf16[128,256]{1,0:T(8,128)(2,1)S(1)}, bf16[128,256]{1,0:T(8,128)(2,1)S(1)}, u32[]{:S(2)}, u32[]{:S(2)}) collective-permute-start(bf16[128,256]{1,0:T(8,128)(2,1)S(1)} %get-tuple-element.55), channel_id=1, source_target_pairs={{22,7},{23,8},{24,9},{25,10},{26,11},{30,15},{31,16},{54,39},{55,4... | collective-permute-start | bytes 196616 | tf_op jit(solution)/shard_map/ppermute | solution.py:157
  70.3 2.6 %collective-permute-done.9 = bf16[128,256]{1,0:T(8,128)(2,1)S(1)} collective-permute-done((bf16[128,256]{1,0:T(8,128)(2,1)S(1)}, bf16[128,256]{1,0:T(8,128)(2,1)S(1)}, u32[]{:S(2)}, u32[]{:S(2)}) %collective-permute-start.9) | collective-permute-done | bytes 65568 | tf_op jit(solution)/shard_map/ppermute | solution.py:157
  72.9 4.3 %collective-permute-done.10 = bf16[128,256]{1,0:T(8,128)(2,1)S(1)} collective-permute-done((bf16[128,256]{1,0:T(8,128)(2,1)S(1)}, bf16[128,256]{1,0:T(8,128)(2,1)S(1)}, u32[]{:S(2)}, u32[]{:S(2)}) %collective-permute-start.10) | collective-permute-done | bytes 65568 | tf_op jit(solution)/shard_map/ppermute | solution.py:157
  77.3 5.5 %collective-permute-done.11 = bf16[128,256]{1,0:T(8,128)(2,1)S(1)} collective-permute-done((bf16[128,256]{1,0:T(8,128)(2,1)S(1)}, bf16[128,256]{1,0:T(8,128)(2,1)S(1)}, u32[]{:S(2)}, u32[]{:S(2)}) %collective-permute-start.11) | collective-permute-done | bytes 65568 | tf_op jit(solution)/shard_map/ppermute | solution.py:157
  82.8 1.9 %collective-permute-start.13 = (f32[256,256]{1,0:T(8,128)S(1)}, f32[256,256]{1,0:T(8,128)S(1)}, u32[]{:S(2)}, u32[]{:S(2)}) collective-permute-start(f32[256,256]{1,0:T(8,128)S(1)} %pad_maximum_fusion.1), channel_id=1, source_target_pairs={{2,0},{3,1},{4,2},{5,3},{6,4},{7,5},{8,6},{9,7},{10,8},{11,9},{12,... | collective-permute-start | bytes 786440 | tf_op jit(solution)/shard_map/ppermute | solution.py:15
  84.8 1.9 %collective-permute-start.14 = (f32[384,256]{1,0:T(8,128)S(1)}, f32[384,256]{1,0:T(8,128)S(1)}, u32[]{:S(2)}, u32[]{:S(2)}) collective-permute-start(f32[384,256]{1,0:T(8,128)S(1)} %pad_maximum_fusion), channel_id=1, source_target_pairs={{1,0},{2,1},{3,2},{4,3},{5,4},{6,5},{7,6},{8,7},{9,8},{10,9},{11,1... | collective-permute-start | bytes 1179656 | tf_op jit(solution)/shard_map/ppermute | solution.py:15
  91.5 4.3 %collective-permute-done.14 = f32[384,256]{1,0:T(8,128)S(1)} collective-permute-done((f32[384,256]{1,0:T(8,128)S(1)}, f32[384,256]{1,0:T(8,128)S(1)}, u32[]{:S(2)}, u32[]{:S(2)}) %collective-permute-start.14) | collective-permute-done | bytes 393248 | tf_op jit(solution)/shard_map/ppermute | solution.py:15
  95.9 1.9 %collective-permute-done.16 = f32[128,256]{1,0:T(8,128)S(1)} collective-permute-done((f32[128,256]{1,0:T(8,128)S(1)}, f32[128,256]{1,0:T(8,128)S(1)}, u32[]{:S(2)}, u32[]{:S(2)}) %collective-permute-start.16) | collective-permute-done | bytes 131104 | tf_op jit(solution)/shard_map/ppermute | solution.py:173
  97.7 3.0 %collective-permute-done.15 = f32[128,256]{1,0:T(8,128)S(1)} collective-permute-done((f32[128,256]{1,0:T(8,128)S(1)}, f32[128,256]{1,0:T(8,128)S(1)}, u32[]{:S(2)}, u32[]{:S(2)}) %collective-permute-start.15) | collective-permute-done | bytes 131104 | tf_op jit(solution)/shard_map/ppermute | solution.py:173
  (77 shorter events, 20.9 us)
Async XLA Ops:
  0.6 25.0 %copy-start.6 = (bf16[1,256,1024]{2,1,0:T(8,128)(2,1)S(1)}, bf16[1,256,1024]{2,1,0:T(8,128)(2,1)}, u32[]{:S(2)}) copy-start(bf16[1,256,1024]{2,1,0:T(8,128)(2,1)} %param.16) | copy-start | bytes 1572868
  1.5 24.4 %collective-permute-start.3 = (bf16[128,256]{1,0:T(8,128)(2,1)S(1)}, bf16[128,256]{1,0:T(8,128)(2,1)}, u32[]{:S(2)}, u32[]{:S(2)}) collective-permute-start(bf16[128,256]{1,0:T(8,128)(2,1)S(1)} %get-tuple-element.47), channel_id=1, source_target_pairs={{7,10},{15,18},{23,26},{39,42},{47,50},{55,58},{71,74},{79,82},{87... | collective-permute-start | bytes 196616 | tf_op jit(solution)/shard_map/ppermute | solution.py:76
  9.7 16.2 %collective-permute-start.4 = (bf16[128,256]{1,0:T(8,128)(2,1)S(1)}, bf16[128,256]{1,0:T(8,128)(2,1)}, u32[]{:S(2)}, u32[]{:S(2)}) collective-permute-start(bf16[128,256]{1,0:T(8,128)(2,1)S(1)} %get-tuple-element.47), channel_id=1, source_target_pairs={{7,11},{15,19},{23,27},{39,43},{47,51},{55,59},{71,75},{79,83},{87... | collective-permute-start | bytes 196616 | tf_op jit(solution)/shard_map/ppermute | solution.py:76
  12.2 13.7 %collective-permute-start = (bf16[256,256]{1,0:T(8,128)(2,1)}, bf16[256,256]{1,0:T(8,128)(2,1)S(1)}, u32[]{:S(2)}, u32[]{:S(2)}) collective-permute-start(bf16[256,256]{1,0:T(8,128)(2,1)} %pad_maximum_fusion.5), channel_id=1, source_target_pairs={{0,2},{1,3},{2,4},{3,5},{4,6},{5,7},{6,8},{7,9},{8,10},{9,11},{10,... | collective-permute-start | bytes 393224 | tf_op jit(solution)/shard_map/ppermute | solution.py:15
  15.7 10.2 %collective-permute-start.1 = (bf16[384,256]{1,0:T(8,128)(2,1)}, bf16[384,256]{1,0:T(8,128)(2,1)}, u32[]{:S(2)}, u32[]{:S(2)}) collective-permute-start(bf16[384,256]{1,0:T(8,128)(2,1)} %pad_maximum_fusion.2), channel_id=1, source_target_pairs={{0,1},{1,2},{2,3},{3,4},{4,5},{5,6},{6,7},{7,8},{8,9},{9,10},{10,1... | collective-permute-start | bytes 589832 | tf_op jit(solution)/shard_map/ppermute | solution.py:15
  17.7 35.5 %collective-permute-start.2 = (bf16[1,256,1024]{2,1,0:T(8,128)(2,1)}, bf16[1,256,1024]{2,1,0:T(8,128)(2,1)}, u32[]{:S(2)}, u32[]{:S(2)}) collective-permute-start(bf16[1,256,1024]{2,1,0:T(8,128)(2,1)} %param.21), channel_id=1, source_target_pairs={{32,0},{64,32},{96,64},{128,96},{160,128},{192,160},{224,192},{256... | collective-permute-start | bytes 1572872 | tf_op jit(solution)/shard_map/ppermute | solution.py:15
  23.9 21.3 %copy-start.3 = (bf16[1,256,128]{2,1,0:T(8,128)(2,1)S(1)}, bf16[1,256,128]{2,1,0:T(8,128)(2,1)}, u32[]{:S(2)}) copy-start(bf16[1,256,128]{2,1,0:T(8,128)(2,1)} %param.18) | copy-start | bytes 196612
  23.9 21.3 %copy-start.4 = (bf16[1,256,128]{2,1,0:T(8,128)(2,1)S(1)}, bf16[1,256,128]{2,1,0:T(8,128)(2,1)}, u32[]{:S(2)}) copy-start(bf16[1,256,128]{2,1,0:T(8,128)(2,1)} %param.17) | copy-start | bytes 196612
  25.1 20.1 %copy-start.7 = (f32[1,8,256]{2,1,0:T(8,128)S(1)}, f32[1,8,256]{2,1,0:T(8,128)}, u32[]{:S(2)}) copy-start(f32[1,8,256]{2,1,0:T(8,128)} %param.22) | copy-start | bytes 24580
  26.9 23.0 %collective-permute-start.8 = (bf16[128,256]{1,0:T(8,128)(2,1)S(1)}, bf16[128,256]{1,0:T(8,128)(2,1)S(1)}, u32[]{:S(2)}, u32[]{:S(2)}) collective-permute-start(bf16[128,256]{1,0:T(8,128)(2,1)S(1)} %get-tuple-element.59), channel_id=1, source_target_pairs={{7,27},{8,28},{9,29},{10,30},{11,31},{39,59},{40,60},{41,61},{42,6... | collective-permute-start | bytes 196616 | tf_op jit(solution)/shard_map/ppermute | solution.py:81
  37.8 12.2 %collective-permute-start.7 = (bf16[128,256]{1,0:T(8,128)(2,1)S(1)}, bf16[128,256]{1,0:T(8,128)(2,1)S(1)}, u32[]{:S(2)}, u32[]{:S(2)}) collective-permute-start(bf16[128,256]{1,0:T(8,128)(2,1)S(1)} %get-tuple-element.59), channel_id=1, source_target_pairs={{7,22},{8,23},{9,24},{10,25},{11,26},{15,30},{16,31},{39,54},{40,5... | collective-permute-start | bytes 196616 | tf_op jit(solution)/shard_map/ppermute | solution.py:81
  41.6 8.3 %collective-permute-start.6 = (bf16[128,256]{1,0:T(8,128)(2,1)S(1)}, bf16[128,256]{1,0:T(8,128)(2,1)S(1)}, u32[]{:S(2)}, u32[]{:S(2)}) collective-permute-start(bf16[128,256]{1,0:T(8,128)(2,1)S(1)} %get-tuple-element.59), channel_id=1, source_target_pairs={{7,17},{8,18},{9,19},{10,20},{11,21},{15,25},{16,26},{17,27},{18,2... | collective-permute-start | bytes 196616 | tf_op jit(solution)/shard_map/ppermute | solution.py:81
  42.9 7.0 %collective-permute-start.5 = (bf16[128,256]{1,0:T(8,128)(2,1)S(1)}, bf16[128,256]{1,0:T(8,128)(2,1)S(1)}, u32[]{:S(2)}, u32[]{:S(2)}) collective-permute-start(bf16[128,256]{1,0:T(8,128)(2,1)S(1)} %get-tuple-element.59), channel_id=1, source_target_pairs={{7,12},{8,13},{9,14},{10,15},{11,16},{15,20},{16,21},{17,22},{18,2... | collective-permute-start | bytes 196616 | tf_op jit(solution)/shard_map/ppermute | solution.py:81
  50.0 3.1 %copy-start.5 = (bf16[1,256,1024]{2,1,0:T(8,128)(2,1)S(1)}, bf16[1,256,1024]{2,1,0:T(8,128)(2,1)}, u32[]{:S(2)}) copy-start(bf16[1,256,1024]{2,1,0:T(8,128)(2,1)} %param.20) | copy-start | bytes 1572868
  60.0 1.9 %copy-start = (f32[384,2,128,8]{2,0,3,1:T(8,128)S(1)}, f32[384,2,128,8]{2,0,3,1:T(8,128)}, u32[]{:S(2)}) copy-start(f32[384,2,128,8]{2,0,3,1:T(8,128)} %get-tuple-element.64) | copy-start | bytes 9437188
  63.0 6.4 %copy-start.1 = (bf16[2,8,128,640]{2,3,1,0:T(8,128)(2,1)S(1)}, bf16[2,8,128,640]{2,3,1,0:T(8,128)(2,1)}, u32[]{:S(2)}) copy-start(bf16[2,8,128,640]{2,3,1,0:T(8,128)(2,1)} %get-tuple-element.61) | copy-start | bytes 7864324
  64.2 8.7 %collective-permute-start.9 = (bf16[128,256]{1,0:T(8,128)(2,1)S(1)}, bf16[128,256]{1,0:T(8,128)(2,1)S(1)}, u32[]{:S(2)}, u32[]{:S(2)}) collective-permute-start(bf16[128,256]{1,0:T(8,128)(2,1)S(1)} %get-tuple-element.53), channel_id=1, source_target_pairs={{12,7},{13,8},{14,9},{15,10},{16,11},{20,15},{21,16},{22,17},{23,1... | collective-permute-start | bytes 196616 | tf_op jit(solution)/shard_map/ppermute | solution.py:157
  65.5 11.7 %collective-permute-start.10 = (bf16[128,256]{1,0:T(8,128)(2,1)S(1)}, bf16[128,256]{1,0:T(8,128)(2,1)S(1)}, u32[]{:S(2)}, u32[]{:S(2)}) collective-permute-start(bf16[128,256]{1,0:T(8,128)(2,1)S(1)} %get-tuple-element.54), channel_id=1, source_target_pairs={{17,7},{18,8},{19,9},{20,10},{21,11},{25,15},{26,16},{27,17},{28,1... | collective-permute-start | bytes 196616 | tf_op jit(solution)/shard_map/ppermute | solution.py:157
  66.8 15.9 %collective-permute-start.11 = (bf16[128,256]{1,0:T(8,128)(2,1)S(1)}, bf16[128,256]{1,0:T(8,128)(2,1)S(1)}, u32[]{:S(2)}, u32[]{:S(2)}) collective-permute-start(bf16[128,256]{1,0:T(8,128)(2,1)S(1)} %get-tuple-element.55), channel_id=1, source_target_pairs={{22,7},{23,8},{24,9},{25,10},{26,11},{30,15},{31,16},{54,39},{55,4... | collective-permute-start | bytes 196616 | tf_op jit(solution)/shard_map/ppermute | solution.py:157
  68.1 14.6 %collective-permute-start.12 = (bf16[128,256]{1,0:T(8,128)(2,1)S(1)}, bf16[128,256]{1,0:T(8,128)(2,1)S(1)}, u32[]{:S(2)}, u32[]{:S(2)}) collective-permute-start(bf16[128,256]{1,0:T(8,128)(2,1)S(1)} %get-tuple-element.56), channel_id=1, source_target_pairs={{27,7},{28,8},{29,9},{30,10},{31,11},{59,39},{60,40},{61,41},{62,4... | collective-permute-start | bytes 196616 | tf_op jit(solution)/shard_map/ppermute | solution.py:157
  82.8 8.6 %collective-permute-start.13 = (f32[256,256]{1,0:T(8,128)S(1)}, f32[256,256]{1,0:T(8,128)S(1)}, u32[]{:S(2)}, u32[]{:S(2)}) collective-permute-start(f32[256,256]{1,0:T(8,128)S(1)} %pad_maximum_fusion.1), channel_id=1, source_target_pairs={{2,0},{3,1},{4,2},{5,3},{6,4},{7,5},{8,6},{9,7},{10,8},{11,9},{12,... | collective-permute-start | bytes 786440 | tf_op jit(solution)/shard_map/ppermute | solution.py:15
  84.8 11.1 %collective-permute-start.14 = (f32[384,256]{1,0:T(8,128)S(1)}, f32[384,256]{1,0:T(8,128)S(1)}, u32[]{:S(2)}, u32[]{:S(2)}) collective-permute-start(f32[384,256]{1,0:T(8,128)S(1)} %pad_maximum_fusion), channel_id=1, source_target_pairs={{1,0},{2,1},{3,2},{4,3},{5,4},{6,5},{7,6},{8,7},{9,8},{10,9},{11,1... | collective-permute-start | bytes 1179656 | tf_op jit(solution)/shard_map/ppermute | solution.py:15
  88.5 9.2 %collective-permute-start.16 = (f32[128,256]{1,0:T(8,128)S(1)}, f32[128,256]{1,0:T(8,128)S(1)}, u32[]{:S(2)}, u32[]{:S(2)}) collective-permute-start(f32[128,256]{1,0:T(8,128)S(1)} %fusion.76), channel_id=1, source_target_pairs={{11,7},{19,15},{27,23},{43,39},{51,47},{59,55},{75,71},{83,79},{91... | collective-permute-start | bytes 393224 | tf_op jit(solution)/shard_map/ppermute | solution.py:173
  89.8 10.9 %collective-permute-start.15 = (f32[128,256]{1,0:T(8,128)S(1)}, f32[128,256]{1,0:T(8,128)S(1)}, u32[]{:S(2)}, u32[]{:S(2)}) collective-permute-start(f32[128,256]{1,0:T(8,128)S(1)} %fusion.76), channel_id=1, source_target_pairs={{10,7},{18,15},{26,23},{42,39},{50,47},{58,55},{74,71},{82,79},{90... | collective-permute-start | bytes 393224 | tf_op jit(solution)/shard_map/ppermute | solution.py:173
  (1 other events, 1.7 us)

commit v6 on v4

--- a/solution.py
+++ b/solution.py
@@ -152,14 +152,14 @@
     summary_low = partial[span * block_rows :].reshape(n_summary, block_rows, -1)
 
     def slot_at(position):
-        return sum(jnp.where(member(position, k), k, 0) for k in range(n_summary))
+        picked = [jnp.where(member(position, k), summary_low[k], 0) for k in range(n_summary)]
+        return functools.reduce(jnp.add, picked).astype(jnp.bfloat16)
 
-    gathered = lax.dynamic_index_in_dim(summary_low, slot_at(device), 0, keepdims=False)
-    gathered = gathered.astype(jnp.float32)
+    gathered = slot_at(device).astype(jnp.float32)
     for hop in range(1, radix):
         shift = hop * radix
         route = [(x + shift, x) for x in relays if x + shift < ctx_count]
-        outgoing = lax.dynamic_index_in_dim(summary_low, slot_at(device - shift), 0, keepdims=False)
+        outgoing = slot_at(device - shift)
         gathered = gathered + lax.ppermute(outgoing, "ctx", route).astype(jnp.float32)
     owner_total = gathered
     for shift in range(1, radix):

time: 96.6 us -> 98.9 us (1.024)
  local copies, waits for them, and re-layouts: 4.67 us -> 6.72 us
  matrix products: 17 us -> 18.4 us
    dot_general x2, matrix products: 5.35 us -> 7.24 us  [attend(): jnp.einsum('rtgh,uh->rgtu', upstream_heads, value_table, preferred_elemen...]
    another operation x0 -> x1, local copies, waits for them, and re-layouts: none -> 1.12 us  [on_device(): queries[0].reshape(local_blocks, block_rows, group_heads, head_size)]
    convert_element_type x1, local copies, waits for them, and re-layouts: 0.04 us -> 1.13 us  [on_device(): (head_grad[0].astype(jnp.float32) + incoming[0].astype(jnp.float32)).asty...]
where the time goes in v6:
time: 98.9 us; the launch traced here: 98.1 us
  starting transfers between devices  50.2 us (51%)
  matrix products  18.4 us (19%)
  waiting for transfers between devices  13 us (13%)
  other arithmetic  8.42 us (9%)
  local copies, waits for them, and re-layouts  6.72 us (7%)
  between operations  1.37 us (1%)
    ppermute x4, starting transfers between devices, on_device(): arrived = lax.ppermute(held, 'ctx', route)  17.3 us
    ppermute x5, starting transfers between devices, from_behind(): return lax.ppermute(block, axis, route)  13 us
    ppermute x2, starting transfers between devices, on_device(): held = held + lax.ppermute(owned, 'ctx', route)  9.49 us
    dot_general x2, matrix products, attend(): jnp.einsum('rtgh,uh->rgtu', query_heads, key_table, preferred_element_typ...  7.28 us
    dot_general x2, matrix products, attend(): jnp.einsum('rtgh,uh->rgtu', upstream_heads, value_table, preferred_elemen...  7.24 us
    ppermute x4, waiting for transfers between devices, on_device(): owner_total = owner_total + lax.ppermute(gathered, 'ctx', route)  7.04 us
    ppermute x4, waiting for transfers between devices, on_device(): lax.ppermute(outgoing, 'ctx', route).astype(jnp.float32)  5.92 us
    ppermute x4, starting transfers between devices, on_device(): lax.ppermute(outgoing, 'ctx', route).astype(jnp.float32)  5.17 us
  transfers between devices with their start and end apart: 19, of which 6 were waited for; matrix products, arithmetic and copies ran while one was open for 18% of the time, Pallas kernels for 0%

profile of v6, /device:TPU:199, one launch (start us, length us, event | category | flops | bytes accessed | tf_op | source)
XLA Modules:
  0.0 98.1 jit_solution(8668147646454225660)
XLA Ops:
  1.5 7.6 %collective-permute-start.3 = (bf16[128,256]{1,0:T(8,128)(2,1)S(1)}, bf16[128,256]{1,0:T(8,128)(2,1)S(1)}, u32[]{:S(2)}, u32[]{:S(2)}) collective-permute-start(bf16[128,256]{1,0:T(8,128)(2,1)S(1)} %get-tuple-element.51), channel_id=1, source_target_pairs={{7,10},{15,18},{23,26},{39,42},{47,50},{55,58},{71,74},{79,82},{87... | collective-permute-start | bytes 196616 | tf_op jit(solution)/shard_map/ppermute | solution.py:76
  9.1 1.9 %collective-permute-start.4 = (bf16[128,256]{1,0:T(8,128)(2,1)S(1)}, bf16[128,256]{1,0:T(8,128)(2,1)}, u32[]{:S(2)}, u32[]{:S(2)}) collective-permute-start(bf16[128,256]{1,0:T(8,128)(2,1)S(1)} %get-tuple-element.51), channel_id=1, source_target_pairs={{7,11},{15,19},{23,27},{39,43},{47,51},{55,59},{71,75},{79,83},{87... | collective-permute-start | bytes 196616 | tf_op jit(solution)/shard_map/ppermute | solution.py:76
  11.7 1.9 %collective-permute-start = (bf16[256,256]{1,0:T(8,128)(2,1)}, bf16[256,256]{1,0:T(8,128)(2,1)}, u32[]{:S(2)}, u32[]{:S(2)}) collective-permute-start(bf16[256,256]{1,0:T(8,128)(2,1)} %pad_maximum_fusion.3), channel_id=1, source_target_pairs={{0,2},{1,3},{2,4},{3,5},{4,6},{5,7},{6,8},{7,9},{8,10},{9,11},{10,... | collective-permute-start | bytes 393224 | tf_op jit(solution)/shard_map/ppermute | solution.py:15
  14.5 1.9 %collective-permute-start.1 = (bf16[384,256]{1,0:T(8,128)(2,1)S(1)}, bf16[384,256]{1,0:T(8,128)(2,1)S(1)}, u32[]{:S(2)}, u32[]{:S(2)}) collective-permute-start(bf16[384,256]{1,0:T(8,128)(2,1)S(1)} %pad_maximum_fusion), channel_id=1, source_target_pairs={{0,1},{1,2},{2,3},{3,4},{4,5},{5,6},{6,7},{7,8},{8,9},{9,10},{10,1... | collective-permute-start | bytes 589832 | tf_op jit(solution)/shard_map/ppermute | solution.py:15
  16.4 5.4 %collective-permute-start.2 = (bf16[1,256,1024]{2,1,0:T(8,128)(2,1)}, bf16[1,256,1024]{2,1,0:T(8,128)(2,1)}, u32[]{:S(2)}, u32[]{:S(2)}) collective-permute-start(bf16[1,256,1024]{2,1,0:T(8,128)(2,1)} %param.21), channel_id=1, source_target_pairs={{32,0},{64,32},{96,64},{128,96},{160,128},{192,160},{224,192},{256... | collective-permute-start | bytes 1572872 | tf_op jit(solution)/shard_map/ppermute | solution.py:15
  27.4 10.9 %collective-permute-start.8 = (bf16[128,256]{1,0:T(8,128)(2,1)S(1)}, bf16[128,256]{1,0:T(8,128)(2,1)S(1)}, u32[]{:S(2)}, u32[]{:S(2)}) collective-permute-start(bf16[128,256]{1,0:T(8,128)(2,1)S(1)} %get-tuple-element.62), channel_id=1, source_target_pairs={{7,27},{8,28},{9,29},{10,30},{11,31},{39,59},{40,60},{41,61},{42,6... | collective-permute-start | bytes 196616 | tf_op jit(solution)/shard_map/ppermute | solution.py:81
  38.3 3.9 %collective-permute-start.7 = (bf16[128,256]{1,0:T(8,128)(2,1)S(1)}, bf16[128,256]{1,0:T(8,128)(2,1)S(1)}, u32[]{:S(2)}, u32[]{:S(2)}) collective-permute-start(bf16[128,256]{1,0:T(8,128)(2,1)S(1)} %get-tuple-element.62), channel_id=1, source_target_pairs={{7,22},{8,23},{9,24},{10,25},{11,26},{15,30},{16,31},{39,54},{40,5... | collective-permute-start | bytes 196616 | tf_op jit(solution)/shard_map/ppermute | solution.py:81
  42.1 1.3 %collective-permute-start.6 = (bf16[128,256]{1,0:T(8,128)(2,1)S(1)}, bf16[128,256]{1,0:T(8,128)(2,1)S(1)}, u32[]{:S(2)}, u32[]{:S(2)}) collective-permute-start(bf16[128,256]{1,0:T(8,128)(2,1)S(1)} %get-tuple-element.62), channel_id=1, source_target_pairs={{7,17},{8,18},{9,19},{10,20},{11,21},{15,25},{16,26},{17,27},{18,2... | collective-permute-start | bytes 196616 | tf_op jit(solution)/shard_map/ppermute | solution.py:81
  43.4 1.3 %collective-permute-start.5 = (bf16[128,256]{1,0:T(8,128)(2,1)S(1)}, bf16[128,256]{1,0:T(8,128)(2,1)S(1)}, u32[]{:S(2)}, u32[]{:S(2)}) collective-permute-start(bf16[128,256]{1,0:T(8,128)(2,1)S(1)} %get-tuple-element.62), channel_id=1, source_target_pairs={{7,12},{8,13},{9,14},{10,15},{11,16},{15,20},{16,21},{17,22},{18,2... | collective-permute-start | bytes 196616 | tf_op jit(solution)/shard_map/ppermute | solution.py:81
  44.8 4.7 %fusion.4 = (bf16[2,8,128,640]{2,3,1,0:T(8,128)(2,1)}, f32[640,2,128,8]{2,0,3,1:T(8,128)}) fusion(f32[2,8,128]{2,1,0:T(8,128)S(1)} %bitcast.152, pred[2,128,640]{1,2,0:T(8,128)(4,1)S(1)} %bitcast.140, bf16[2,128,8,128]{3,2,1,0:T(8,128)(2,1)S(1)} %bitcast.130, bf16[640,256]{1,0:T(8,128)(2,1)S(1)} %maximum_maximum_fusion), kind=kOutput, calls=%fused_computation.6 | convolution fusion | flops 340787200 | bytes 8724480 | tf_op jit(solution)/shard_map/rtgh,uh->rgtu/dot_general | solution.py:113
  49.7 2.6 %fusion.13 = (bf16[2,8,128,384]{2,3,1,0:T(8,128)(2,1)S(1)}, f32[384,2,128,8]{2,0,3,1:T(8,128)}) fusion(f32[2,8,128]{2,1,0:T(8,128)S(1)} %bitcast.153, pred[2,128,384]{1,2,0:T(8,128)(4,1)S(1)} %bitcast.151, bf16[2,128,8,128]{3,2,1,0:T(8,128)(2,1)S(1)} %bitcast.131, bf16[384,256]{1,0:T(8,128)(2,1)S(1)} %bitcast.137), kind=kOutput, calls=%fused_computation.17 | convolution fusion | flops 204472320 | bytes 5447680 | tf_op jit(solution)/shard_map/rtgh,uh->rgtu/dot_general | solution.py:113
  56.7 3.0 %fusion.6 = bf16[2,8,128,384]{2,3,1,0:T(8,128)(2,1)S(1)} fusion(f32[384,2,128,8]{2,0,3,1:T(8,128)} %get-tuple-element.67, f32[2,8,128]{2,1,0:T(8,128)S(1)} %copy.77, f32[2,8,128]{2,1,0:T(8,128)S(1)} %bitcast.154, pred[2,128,384]{1,2,0:T(8,128)(4,1)} %bitcast.150, bf16[2,128,8,128]{3,2,1,0:T(8,128)(2,1)S(1)} %bitcast.134, bf16[384,256]{1,0:T(8,128)(2,1)} %bitcast.138), kind=kOutput, calls=%fused_computation.9 | convolution fusion | flops 206045184 | bytes 5455872 | tf_op jit(solution)/shard_map/rtgh,uh->rgtu/dot_general | solution.py:119
  59.8 4.2 %fusion.1 = bf16[2,8,128,640]{2,3,1,0:T(8,128)(2,1)S(1)} fusion(f32[640,2,128,8]{2,0,3,1:T(8,128)} %get-tuple-element.65, f32[2,8,128]{2,1,0:T(8,128)S(1)} %copy.77, f32[2,8,128]{2,1,0:T(8,128)S(1)} %bitcast.155, pred[2,128,640]{1,2,0:T(8,128)(4,1)S(1)} %bitcast.141, bf16[2,128,8,128]{3,2,1,0:T(8,128)(2,1)S(1)} %bitcast.135, ...), kind=kOutput, calls=%fused_computation.2 | convolution fusion | flops 343408640 | bytes 8732672 | tf_op jit(solution)/shard_map/rtgh,uh->rgtu/dot_general | solution.py:119
  67.1 1.3 %collective-permute-start.11 = (bf16[128,256]{1,0:T(8,128)(2,1)S(1)}, bf16[128,256]{1,0:T(8,128)(2,1)S(1)}, u32[]{:S(2)}, u32[]{:S(2)}) collective-permute-start(bf16[128,256]{1,0:T(8,128)(2,1)S(1)} %get-tuple-element.47), channel_id=1, source_target_pairs={{12,7},{13,8},{14,9},{15,10},{16,11},{20,15},{21,16},{22,17},{23,1... | collective-permute-start | bytes 196616 | tf_op jit(solution)/shard_map/ppermute | solution.py:163
  68.5 1.3 %collective-permute-start.12 = (bf16[128,256]{1,0:T(8,128)(2,1)S(1)}, bf16[128,256]{1,0:T(8,128)(2,1)S(1)}, u32[]{:S(2)}, u32[]{:S(2)}) collective-permute-start(bf16[128,256]{1,0:T(8,128)(2,1)S(1)} %get-tuple-element.57), channel_id=1, source_target_pairs={{17,7},{18,8},{19,9},{20,10},{21,11},{25,15},{26,16},{27,17},{28,1... | collective-permute-start | bytes 196616 | tf_op jit(solution)/shard_map/ppermute | solution.py:163
  69.8 1.3 %collective-permute-start.13 = (bf16[128,256]{1,0:T(8,128)(2,1)S(1)}, bf16[128,256]{1,0:T(8,128)(2,1)S(1)}, u32[]{:S(2)}, u32[]{:S(2)}) collective-permute-start(bf16[128,256]{1,0:T(8,128)(2,1)S(1)} %get-tuple-element.58), channel_id=1, source_target_pairs={{22,7},{23,8},{24,9},{25,10},{26,11},{30,15},{31,16},{54,39},{55,4... | collective-permute-start | bytes 196616 | tf_op jit(solution)/shard_map/ppermute | solution.py:163
  71.1 1.3 %collective-permute-start.14 = (bf16[128,256]{1,0:T(8,128)(2,1)S(1)}, bf16[128,256]{1,0:T(8,128)(2,1)S(1)}, u32[]{:S(2)}, u32[]{:S(2)}) collective-permute-start(bf16[128,256]{1,0:T(8,128)(2,1)S(1)} %get-tuple-element.59), channel_id=1, source_target_pairs={{27,7},{28,8},{29,9},{30,10},{31,11},{59,39},{60,40},{61,41},{62,4... | collective-permute-start | bytes 196616 | tf_op jit(solution)/shard_map/ppermute | solution.py:163
  75.1 1.9 %collective-permute-start.9 = (bf16[128,256]{1,0:T(8,128)(2,1)S(1)}, bf16[128,256]{1,0:T(8,128)(2,1)S(1)}, u32[]{:S(2)}, u32[]{:S(2)}) collective-permute-start(bf16[128,256]{1,0:T(8,128)(2,1)S(1)} %fusion.66), channel_id=1, source_target_pairs={{2,0},{3,1},{4,2},{5,3},{6,4},{7,5},{8,6},{9,7},{10,8},{11,9},{12,... | collective-permute-start | bytes 196616 | tf_op jit(solution)/shard_map/ppermute | solution.py:15
  77.0 1.9 %collective-permute-start.10 = (bf16[256,256]{1,0:T(8,128)(2,1)S(1)}, bf16[256,256]{1,0:T(8,128)(2,1)S(1)}, u32[]{:S(2)}, u32[]{:S(2)}) collective-permute-start(bf16[256,256]{1,0:T(8,128)(2,1)S(1)} %get-tuple-element.53), channel_id=1, source_target_pairs={{1,0},{2,1},{3,2},{4,3},{5,4},{6,5},{7,6},{8,7},{9,8},{10,9},{11,1... | collective-permute-start | bytes 393224 | tf_op jit(solution)/shard_map/ppermute | solution.py:15
  79.5 5.4 %collective-permute-done.13 = bf16[128,256]{1,0:T(8,128)(2,1)S(1)} collective-permute-done((bf16[128,256]{1,0:T(8,128)(2,1)S(1)}, bf16[128,256]{1,0:T(8,128)(2,1)S(1)}, u32[]{:S(2)}, u32[]{:S(2)}) %collective-permute-start.13) | collective-permute-done | bytes 65568 | tf_op jit(solution)/shard_map/ppermute | solution.py:163
  85.0 1.3 %collective-permute-start.18 = (f32[128,256]{1,0:T(8,128)S(1)}, f32[128,256]{1,0:T(8,128)S(1)}, u32[]{:S(2)}, u32[]{:S(2)}) collective-permute-start(f32[128,256]{1,0:T(8,128)S(1)} %convert_add_fusion.1), channel_id=1, source_target_pairs={{11,7},{19,15},{27,23},{43,39},{51,47},{59,55},{75,71},{83,79},{91... | collective-permute-start | bytes 393224 | tf_op jit(solution)/shard_map/ppermute | solution.py:167
  90.3 2.5 %collective-permute-done.18 = f32[128,256]{1,0:T(8,128)S(1)} collective-permute-done((f32[128,256]{1,0:T(8,128)S(1)}, f32[128,256]{1,0:T(8,128)S(1)}, u32[]{:S(2)}, u32[]{:S(2)}) %collective-permute-start.18) | collective-permute-done | bytes 131104 | tf_op jit(solution)/shard_map/ppermute | solution.py:167
  92.8 2.3 %collective-permute-done.17 = f32[128,256]{1,0:T(8,128)S(1)} collective-permute-done((f32[128,256]{1,0:T(8,128)S(1)}, f32[128,256]{1,0:T(8,128)S(1)}, u32[]{:S(2)}, u32[]{:S(2)}) %collective-permute-start.17) | collective-permute-done | bytes 131104 | tf_op jit(solution)/shard_map/ppermute | solution.py:167
  95.1 1.7 %collective-permute-done.16 = f32[128,256]{1,0:T(8,128)S(1)} collective-permute-done((f32[128,256]{1,0:T(8,128)S(1)}, f32[128,256]{1,0:T(8,128)S(1)}, u32[]{:S(2)}, u32[]{:S(2)}) %collective-permute-start.16) | collective-permute-done | bytes 131104 | tf_op jit(solution)/shard_map/ppermute | solution.py:167
  (91 shorter events, 24.1 us)
Async XLA Ops:
  0.6 24.3 %copy-start.8 = (bf16[1,256,1024]{2,1,0:T(8,128)(2,1)S(1)}, bf16[1,256,1024]{2,1,0:T(8,128)(2,1)}, u32[]{:S(2)}) copy-start(bf16[1,256,1024]{2,1,0:T(8,128)(2,1)} %param.16) | copy-start | bytes 1572868
  1.5 24.9 %collective-permute-start.3 = (bf16[128,256]{1,0:T(8,128)(2,1)S(1)}, bf16[128,256]{1,0:T(8,128)(2,1)S(1)}, u32[]{:S(2)}, u32[]{:S(2)}) collective-permute-start(bf16[128,256]{1,0:T(8,128)(2,1)S(1)} %get-tuple-element.51), channel_id=1, source_target_pairs={{7,10},{15,18},{23,26},{39,42},{47,50},{55,58},{71,74},{79,82},{87... | collective-permute-start | bytes 196616 | tf_op jit(solution)/shard_map/ppermute | solution.py:76
  9.1 17.3 %collective-permute-start.4 = (bf16[128,256]{1,0:T(8,128)(2,1)S(1)}, bf16[128,256]{1,0:T(8,128)(2,1)}, u32[]{:S(2)}, u32[]{:S(2)}) collective-permute-start(bf16[128,256]{1,0:T(8,128)(2,1)S(1)} %get-tuple-element.51), channel_id=1, source_target_pairs={{7,11},{15,19},{23,27},{39,43},{47,51},{55,59},{71,75},{79,83},{87... | collective-permute-start | bytes 196616 | tf_op jit(solution)/shard_map/ppermute | solution.py:76
  11.7 14.8 %collective-permute-start = (bf16[256,256]{1,0:T(8,128)(2,1)}, bf16[256,256]{1,0:T(8,128)(2,1)}, u32[]{:S(2)}, u32[]{:S(2)}) collective-permute-start(bf16[256,256]{1,0:T(8,128)(2,1)} %pad_maximum_fusion.3), channel_id=1, source_target_pairs={{0,2},{1,3},{2,4},{3,5},{4,6},{5,7},{6,8},{7,9},{8,10},{9,11},{10,... | collective-permute-start | bytes 393224 | tf_op jit(solution)/shard_map/ppermute | solution.py:15
  14.5 12.0 %collective-permute-start.1 = (bf16[384,256]{1,0:T(8,128)(2,1)S(1)}, bf16[384,256]{1,0:T(8,128)(2,1)S(1)}, u32[]{:S(2)}, u32[]{:S(2)}) collective-permute-start(bf16[384,256]{1,0:T(8,128)(2,1)S(1)} %pad_maximum_fusion), channel_id=1, source_target_pairs={{0,1},{1,2},{2,3},{3,4},{4,5},{5,6},{6,7},{7,8},{8,9},{9,10},{10,1... | collective-permute-start | bytes 589832 | tf_op jit(solution)/shard_map/ppermute | solution.py:15
  16.4 35.9 %collective-permute-start.2 = (bf16[1,256,1024]{2,1,0:T(8,128)(2,1)}, bf16[1,256,1024]{2,1,0:T(8,128)(2,1)}, u32[]{:S(2)}, u32[]{:S(2)}) collective-permute-start(bf16[1,256,1024]{2,1,0:T(8,128)(2,1)} %param.21), channel_id=1, source_target_pairs={{32,0},{64,32},{96,64},{128,96},{160,128},{192,160},{224,192},{256... | collective-permute-start | bytes 1572872 | tf_op jit(solution)/shard_map/ppermute | solution.py:15
  23.8 21.0 %copy-start.5 = (bf16[1,256,128]{2,1,0:T(8,128)(2,1)S(1)}, bf16[1,256,128]{2,1,0:T(8,128)(2,1)}, u32[]{:S(2)}) copy-start(bf16[1,256,128]{2,1,0:T(8,128)(2,1)} %param.18) | copy-start | bytes 196612
  23.8 20.9 %copy-start.6 = (bf16[1,256,128]{2,1,0:T(8,128)(2,1)S(1)}, bf16[1,256,128]{2,1,0:T(8,128)(2,1)}, u32[]{:S(2)}) copy-start(bf16[1,256,128]{2,1,0:T(8,128)(2,1)} %param.17) | copy-start | bytes 196612
  24.2 20.6 %copy-start.12 = (f32[1,8,256]{2,1,0:T(8,128)S(1)}, f32[1,8,256]{2,1,0:T(8,128)}, u32[]{:S(2)}) copy-start(f32[1,8,256]{2,1,0:T(8,128)} %param.22) | copy-start | bytes 24580
  24.9 24.6 %copy-start.3 = (pred[2,128,5,128]{1,3,2,0:T(8,128)(4,1)}, pred[2,128,5,128]{1,3,2,0:T(8,128)(4,1)S(1)}, u32[]{:S(2)}) copy-start(pred[2,128,5,128]{1,3,2,0:T(8,128)(4,1)S(1)} %slice.152) | copy-start | bytes 491524
  27.4 22.1 %collective-permute-start.8 = (bf16[128,256]{1,0:T(8,128)(2,1)S(1)}, bf16[128,256]{1,0:T(8,128)(2,1)S(1)}, u32[]{:S(2)}, u32[]{:S(2)}) collective-permute-start(bf16[128,256]{1,0:T(8,128)(2,1)S(1)} %get-tuple-element.62), channel_id=1, source_target_pairs={{7,27},{8,28},{9,29},{10,30},{11,31},{39,59},{40,60},{41,61},{42,6... | collective-permute-start | bytes 196616 | tf_op jit(solution)/shard_map/ppermute | solution.py:81
  38.3 11.2 %collective-permute-start.7 = (bf16[128,256]{1,0:T(8,128)(2,1)S(1)}, bf16[128,256]{1,0:T(8,128)(2,1)S(1)}, u32[]{:S(2)}, u32[]{:S(2)}) collective-permute-start(bf16[128,256]{1,0:T(8,128)(2,1)S(1)} %get-tuple-element.62), channel_id=1, source_target_pairs={{7,22},{8,23},{9,24},{10,25},{11,26},{15,30},{16,31},{39,54},{40,5... | collective-permute-start | bytes 196616 | tf_op jit(solution)/shard_map/ppermute | solution.py:81
  42.1 7.4 %collective-permute-start.6 = (bf16[128,256]{1,0:T(8,128)(2,1)S(1)}, bf16[128,256]{1,0:T(8,128)(2,1)S(1)}, u32[]{:S(2)}, u32[]{:S(2)}) collective-permute-start(bf16[128,256]{1,0:T(8,128)(2,1)S(1)} %get-tuple-element.62), channel_id=1, source_target_pairs={{7,17},{8,18},{9,19},{10,20},{11,21},{15,25},{16,26},{17,27},{18,2... | collective-permute-start | bytes 196616 | tf_op jit(solution)/shard_map/ppermute | solution.py:81
  43.4 6.1 %collective-permute-start.5 = (bf16[128,256]{1,0:T(8,128)(2,1)S(1)}, bf16[128,256]{1,0:T(8,128)(2,1)S(1)}, u32[]{:S(2)}, u32[]{:S(2)}) collective-permute-start(bf16[128,256]{1,0:T(8,128)(2,1)S(1)} %get-tuple-element.62), channel_id=1, source_target_pairs={{7,12},{8,13},{9,14},{10,15},{11,16},{15,20},{16,21},{17,22},{18,2... | collective-permute-start | bytes 196616 | tf_op jit(solution)/shard_map/ppermute | solution.py:81
  67.1 9.9 %collective-permute-start.11 = (bf16[128,256]{1,0:T(8,128)(2,1)S(1)}, bf16[128,256]{1,0:T(8,128)(2,1)S(1)}, u32[]{:S(2)}, u32[]{:S(2)}) collective-permute-start(bf16[128,256]{1,0:T(8,128)(2,1)S(1)} %get-tuple-element.47), channel_id=1, source_target_pairs={{12,7},{13,8},{14,9},{15,10},{16,11},{20,15},{21,16},{22,17},{23,1... | collective-permute-start | bytes 196616 | tf_op jit(solution)/shard_map/ppermute | solution.py:163
  68.5 11.0 %collective-permute-start.12 = (bf16[128,256]{1,0:T(8,128)(2,1)S(1)}, bf16[128,256]{1,0:T(8,128)(2,1)S(1)}, u32[]{:S(2)}, u32[]{:S(2)}) collective-permute-start(bf16[128,256]{1,0:T(8,128)(2,1)S(1)} %get-tuple-element.57), channel_id=1, source_target_pairs={{17,7},{18,8},{19,9},{20,10},{21,11},{25,15},{26,16},{27,17},{28,1... | collective-permute-start | bytes 196616 | tf_op jit(solution)/shard_map/ppermute | solution.py:163
  69.8 15.1 %collective-permute-start.13 = (bf16[128,256]{1,0:T(8,128)(2,1)S(1)}, bf16[128,256]{1,0:T(8,128)(2,1)S(1)}, u32[]{:S(2)}, u32[]{:S(2)}) collective-permute-start(bf16[128,256]{1,0:T(8,128)(2,1)S(1)} %get-tuple-element.58), channel_id=1, source_target_pairs={{22,7},{23,8},{24,9},{25,10},{26,11},{30,15},{31,16},{54,39},{55,4... | collective-permute-start | bytes 196616 | tf_op jit(solution)/shard_map/ppermute | solution.py:163
  71.1 13.8 %collective-permute-start.14 = (bf16[128,256]{1,0:T(8,128)(2,1)S(1)}, bf16[128,256]{1,0:T(8,128)(2,1)S(1)}, u32[]{:S(2)}, u32[]{:S(2)}) collective-permute-start(bf16[128,256]{1,0:T(8,128)(2,1)S(1)} %get-tuple-element.59), channel_id=1, source_target_pairs={{27,7},{28,8},{29,9},{30,10},{31,11},{59,39},{60,40},{61,41},{62,4... | collective-permute-start | bytes 196616 | tf_op jit(solution)/shard_map/ppermute | solution.py:163
  75.1 13.8 %collective-permute-start.9 = (bf16[128,256]{1,0:T(8,128)(2,1)S(1)}, bf16[128,256]{1,0:T(8,128)(2,1)S(1)}, u32[]{:S(2)}, u32[]{:S(2)}) collective-permute-start(bf16[128,256]{1,0:T(8,128)(2,1)S(1)} %fusion.66), channel_id=1, source_target_pairs={{2,0},{3,1},{4,2},{5,3},{6,4},{7,5},{8,6},{9,7},{10,8},{11,9},{12,... | collective-permute-start | bytes 196616 | tf_op jit(solution)/shard_map/ppermute | solution.py:15
  77.0 13.2 %collective-permute-start.10 = (bf16[256,256]{1,0:T(8,128)(2,1)S(1)}, bf16[256,256]{1,0:T(8,128)(2,1)S(1)}, u32[]{:S(2)}, u32[]{:S(2)}) collective-permute-start(bf16[256,256]{1,0:T(8,128)(2,1)S(1)} %get-tuple-element.53), channel_id=1, source_target_pairs={{1,0},{2,1},{3,2},{4,3},{5,4},{6,5},{7,6},{8,7},{9,8},{10,9},{11,1... | collective-permute-start | bytes 393224 | tf_op jit(solution)/shard_map/ppermute | solution.py:15
  85.0 7.8 %collective-permute-start.18 = (f32[128,256]{1,0:T(8,128)S(1)}, f32[128,256]{1,0:T(8,128)S(1)}, u32[]{:S(2)}, u32[]{:S(2)}) collective-permute-start(f32[128,256]{1,0:T(8,128)S(1)} %convert_add_fusion.1), channel_id=1, source_target_pairs={{11,7},{19,15},{27,23},{43,39},{51,47},{59,55},{75,71},{83,79},{91... | collective-permute-start | bytes 393224 | tf_op jit(solution)/shard_map/ppermute | solution.py:167
  86.3 8.8 %collective-permute-start.17 = (f32[128,256]{1,0:T(8,128)S(1)}, f32[128,256]{1,0:T(8,128)S(1)}, u32[]{:S(2)}, u32[]{:S(2)}) collective-permute-start(f32[128,256]{1,0:T(8,128)S(1)} %convert_add_fusion.1), channel_id=1, source_target_pairs={{10,7},{18,15},{26,23},{42,39},{50,47},{58,55},{74,71},{82,79},{90... | collective-permute-start | bytes 393224 | tf_op jit(solution)/shard_map/ppermute | solution.py:167
  87.6 9.2 %collective-permute-start.16 = (f32[128,256]{1,0:T(8,128)S(1)}, f32[128,256]{1,0:T(8,128)S(1)}, u32[]{:S(2)}, u32[]{:S(2)}) collective-permute-start(f32[128,256]{1,0:T(8,128)S(1)} %convert_add_fusion.1), channel_id=1, source_target_pairs={{9,7},{17,15},{25,23},{41,39},{49,47},{57,55},{73,71},{81,79},{89,... | collective-permute-start | bytes 393224 | tf_op jit(solution)/shard_map/ppermute | solution.py:167
  88.9 8.4 %collective-permute-start.15 = (f32[128,256]{1,0:T(8,128)S(1)}, f32[128,256]{1,0:T(8,128)S(1)}, u32[]{:S(2)}, u32[]{:S(2)}) collective-permute-start(f32[128,256]{1,0:T(8,128)S(1)} %convert_add_fusion.1), channel_id=1, source_target_pairs={{8,7},{16,15},{24,23},{40,39},{48,47},{56,55},{72,71},{80,79},{88,... | collective-permute-start | bytes 393224 | tf_op jit(solution)/shard_map/ppermute | solution.py:167
  (8 other events, 29.6 us)
